TPU v7x, 32 devices: a whole 2x2x4 slice. The times are simulated.
32 devices in a mesh: gx: 8 (over y, x, core), gy: 4 (over z).
Axes of the slice: x: 2, y: 2, z: 4, core: 2. Of those that a mesh axis runs over, the one named last changes fastest.
Arguments:
- positions: float32 [3, 65536], P(None, ('gx', 'gy')), may hold values from 0 to 8, as said below
- density: float32 [65536], P(('gx', 'gy')), may hold values from 0.5 to 4
- momentum: float32 [3, 65536], P(None, ('gx', 'gy')), may hold values from -3 to 3
- field: float32 [3, 65536], P(None, ('gx', 'gy')), may hold values from -3 to 3
- psi: float32 [65536], P(('gx', 'gy')), may hold values from -3 to 3
- ohmic: float32 [65536], P(('gx', 'gy')), may hold values from 0.05 to 20
- ambipolar: float32 [65536], P(('gx', 'gy')), may hold values from 0.02 to 0.3
- ghost_index: int32 [34816], P(('gx', 'gy')), may hold values from 0 to 2047, as said below
- tile_i: int32 [2048], P(('gx', 'gy')), may hold values from 0 to 15, as said below
- tile_j: int32 [2048], P(('gx', 'gy')), may hold values from 0 to 24, as said below
- tile_count: int32 [32], P(('gx', 'gy')), may hold values from 16 to 64, as said below
Outputs:
- density_new: float32 [65536], P(('gx', 'gy'))
- momentum_new: float32 [3, 65536], P(None, ('gx', 'gy'))
- field_new: float32 [3, 65536], P(None, ('gx', 'gy'))
- psi_new: float32 [65536], P(('gx', 'gy'))
Inputs may be any that keep to these rules, and one draw needn't show every extreme that they name: `positions`: x lies in [ix, ix+1) and y in [iy, iy+1) for the owner (ix, iy); z lies in [0, 0.5). `ghost_index`: within one device the 1088 numbers are distinct. `tile_i`: a block of 128 local particles. `tile_j`: a block of 128 in the extended set; the pairs (tile_i, tile_j) of one device are distinct. `tile_count`: the devices of a dense region of three by three slabs use all 64 entries.
All inputs are finite; a program needn't handle non-finite values.
Results may differ from a plain program's by a relative error of at most 0.0003.
Values sent between devices are 32-bit elements; how exact they have to be, the bound alone decides.
No kernel may reach another device: no remote copies, remote signals or barrier semaphores. Data moves between devices by JAX's collectives and lax.ppermute only.
A program may use at most 64 MiB of HBM per device.

v0:
```python
import math

import jax
import jax.numpy as jnp
from jax import lax
from jax.sharding import PartitionSpec as P

TILE = 128
SECTIONS = 4
GHOST_X = 320
GHOST_Y = 160
GHOST_C = 32
EXT_BLOCKS = 25


DIRECTIONS = [(-1, -1), (-1, 0), (-1, 1), (0, -1), (0, 1), (1, -1), (1, 0), (1, 1)]
courant = 0.3
damping = 0.5


def extended(array, sides, width):
    for axis, dim in sides:
        size, length = (lax.axis_size(axis), array.shape[dim])
        up = [(i, (i + 1) % size) for i in range(size - 1)]
        down = [(j, i) for i, j in up]
        last = lax.slice_in_dim(array, length - width, length, axis=dim)
        leading = lax.slice_in_dim(array, 0, width, axis=dim)
        before = lax.ppermute(last, axis, up)
        after = lax.ppermute(leading, axis, down)
        array = jnp.concatenate([before, array, after], axis=dim)
    return array


def ghost_sizes():
    return [GHOST_C, GHOST_X, GHOST_C, GHOST_Y, GHOST_Y, GHOST_C, GHOST_X, GHOST_C]


def ghost_offsets():
    sizes = ghost_sizes()
    starts = [0]
    for value in sizes[:-1]:
        starts.append(starts[-1] + value)
    return starts


def rkl_table(sections):
    wfirst = 4.0 / (sections * sections + sections - 2)
    bvals = [1.0 / 3.0, 1.0 / 3.0, 1.0 / 3.0] + [
        (j * j + j - 2) / (2.0 * j * (j + 1)) for j in range(3, sections + 1)
    ]
    first = bvals[1] * wfirst
    rows = []
    for j in range(2, sections + 1):
        mu_j = (2.0 * j - 1.0) / j * bvals[j] / bvals[j - 1]
        nu_j = -(j - 1.0) / j * bvals[j] / bvals[j - 2]
        mut_j = mu_j * wfirst
        rows.append((mu_j, nu_j, mut_j, -(1.0 - bvals[j - 1]) * mut_j))
    return (first, rows)


def kernel_tile(near, far):
    dist = (near[0][..., :, None] - far[0][..., None, :]) ** 2
    dist = dist + (near[1][..., :, None] - far[1][..., None, :]) ** 2
    dist = dist + (near[2][..., :, None] - far[2][..., None, :]) ** 2
    base = jnp.maximum(1.0 - 4.0 * dist, 0.0)
    return base * base


def flux_rows(ext):
    posit = ext[0:3]
    live = ext[3]
    rho = ext[4]
    vel = ext[5:8]
    bfl = ext[8:11]
    cpsi = ext[11]
    speed = ext[12]
    mom = rho * vel
    ptot = rho + 0.5 * jnp.sum(bfl * bfl, axis=0)
    fluxes = []
    for d in range(3):
        rows_d = [mom[d]]
        for k in range(3):
            term = mom[k] * vel[d] - bfl[k] * bfl[d]
            rows_d.append(term + ptot if k == d else term)
        for k in range(3):
            term = vel[d] * bfl[k] - bfl[d] * vel[k]
            rows_d.append(term + cpsi if k == d else term)
        rows_d.append(bfl[d])
        fluxes.append(jnp.stack(rows_d))
    flux = jnp.stack(fluxes)
    state = jnp.concatenate([rho[None], mom, bfl, cpsi[None]], axis=0)
    gsum = posit[0] * flux[0] + posit[1] * flux[1] + posit[2] * flux[2]
    return jnp.concatenate(
        [live[None], posit, flux.reshape(24, -1), gsum, speed * state, speed[None], state], axis=0
    )


def hydro_rate(acc, local, ch):
    count_n = acc[0]
    num = acc.shape[1]
    wflux = acc[4:28].reshape(3, 8, num)
    flux = local[4:28].reshape(3, 8, num)
    posit = local[1:4]
    speed = local[44]
    state = local[45:53]
    central = acc[28:36]
    for d in range(3):
        central = central + flux[d] * (acc[1 + d] - posit[d] * count_n) - posit[d] * wflux[d]
    central = jnp.concatenate([central[:7], (ch * ch) * central[7:8]], axis=0)
    dissip = speed * (acc[45:53] - state * count_n) + acc[36:44] - state * acc[44]
    return ((0.5 * dissip - 0.5 * central) / (1.0 + count_n), count_n)


def diffusion_rate(acc, bloc, etaloc, count_n):
    return 0.5 * (etaloc * (acc[0:3] - bloc * count_n) + acc[3:6] - bloc * acc[6]) / (1.0 + count_n)


def spread_ghosts(rows, ghost_index, extra=None):
    sizes = ghost_sizes()
    starts = ghost_offsets()
    width = max(sizes)
    nx, ny = (lax.axis_size("gx"), lax.axis_size("gy"))
    ix, iy = (lax.axis_index("gx"), lax.axis_index("gy"))
    sent = jnp.take(rows, ghost_index, axis=1)
    segments = []
    for d in range(8):
        part = sent[:, starts[d] : starts[d] + sizes[d]]
        segments.append(jnp.pad(part, ((0, 0), (0, width - sizes[d]))))
    segments.append(jnp.zeros_like(segments[0]))
    segments = jnp.stack(segments)
    table = [8] * 9
    for d, (p, q) in enumerate(DIRECTIONS):
        table[(p + 1) * 3 + q + 1] = d
    peer = jnp.arange(nx * ny, dtype=jnp.int32)
    du = peer // ny - ix
    dv = peer % ny - iy
    near = (jnp.abs(du) <= 1) & (jnp.abs(dv) <= 1)
    code = jnp.clip((du + 1) * 3 + dv + 1, 0, 8)
    pick = jnp.where(near, jnp.array(table, jnp.int32)[code], 8)
    outgoing = jnp.take(segments, pick, axis=0)
    nrows = rows.shape[0]
    if extra is not None:
        tag = jnp.full((nx * ny, 1, width), extra, jnp.float32)
        outgoing = jnp.concatenate([outgoing, tag], axis=1)
    incoming = lax.all_to_all(outgoing, ("gx", "gy"), 0, 0, tiled=True)
    pieces = []
    for d, (p, q) in enumerate(DIRECTIONS):
        sx, sy = (ix + p, iy + q)
        inside = (sx >= 0) & (sx < nx) & (sy >= 0) & (sy < ny)
        source = jnp.clip(sx, 0, nx - 1) * ny + jnp.clip(sy, 0, ny - 1)
        block = lax.dynamic_index_in_dim(incoming, source, 0, keepdims=False)
        pieces.append(jnp.where(inside, block[:nrows, : sizes[d]], 0.0))
    ghosts = jnp.concatenate(pieces, axis=1)
    if extra is None:
        return ghosts
    return (ghosts, jnp.max(incoming[:, nrows, 0]))


def extend(rows, extra):
    filler = jnp.zeros(
        (rows.shape[0], EXT_BLOCKS * TILE - rows.shape[1] - extra.shape[1]), jnp.float32
    )
    return jnp.concatenate([rows, extra, filler], axis=1)


def shards(
    positions,
    density,
    momentum,
    field,
    psi,
    ohmic,
    ambipolar,
    ghost_index,
    tile_i,
    tile_j,
    tile_count,
):
    nlocal = density.shape[0]
    nblocks = nlocal // TILE
    velocity = momentum / density
    speed = jnp.sqrt(1.0 + jnp.sum(field * field, axis=0) / density)
    fac = ambipolar / (density * jnp.sqrt(density))
    live = jnp.ones_like(density)
    core_rows = [positions, live[None], density[None], velocity, field, psi[None], speed[None]]
    payload = jnp.concatenate(core_rows + [ohmic[None], fac[None]], axis=0)
    qlocal = flux_rows(payload)
    ghosts, ch = spread_ghosts(payload, ghost_index, jnp.max(speed))
    dt = courant / ch
    ext = extend(payload, ghosts)
    pos_blocks = ext[0:3].reshape(3, EXT_BLOCKS, TILE)
    pos_local = positions.reshape(3, nblocks, TILE)
    qext = jnp.concatenate([qlocal, flux_rows(ext[:, nlocal:])], axis=1)
    nrow = qext.shape[0]
    q_blocks = qext.reshape(nrow, EXT_BLOCKS, TILE)
    q_local_blocks = qlocal.reshape(nrow, nblocks, TILE)
    count = tile_count[0]
    tiles_total = tile_i.shape[0]
    batch = math.gcd(32, tiles_total)
    block_ids = jnp.arange(nblocks, dtype=jnp.int32)
    slots = jnp.arange(tiles_total, dtype=jnp.int32)
    key = jnp.where(slots < count, (tile_j >= nblocks).astype(jnp.int32), 2)
    first_n = jnp.sum((key == 0).astype(jnp.int32))
    second_n = jnp.sum((key == 1).astype(jnp.int32))
    rank = [jnp.cumsum((key == c).astype(jnp.int32)) - 1 for c in range(3)]
    dest = jnp.where(
        key == 0, rank[0], jnp.where(key == 1, first_n + rank[1], first_n + second_n + rank[2])
    )
    place = dest[None, :] == slots[:, None]
    pad = jnp.zeros((batch,), jnp.int32)
    list_i = jnp.concatenate([jnp.sum(jnp.where(place, tile_i[None, :], 0), axis=1), pad])
    list_j = jnp.concatenate([jnp.sum(jnp.where(place, tile_j[None, :], 0), axis=1), pad])

    def batch_lists(offset, stop, clip):
        near_ids = lax.dynamic_slice_in_dim(list_i, offset, batch, 0)
        far_ids = lax.dynamic_slice_in_dim(list_j, offset, batch, 0)
        if clip:
            far_ids = jnp.minimum(far_ids, nblocks - 1)
        usable = offset + jnp.arange(batch, dtype=jnp.int32) < stop
        onehot = ((near_ids[None, :] == block_ids[:, None]) & usable[None, :]).astype(jnp.float32)
        return (near_ids, far_ids, onehot)

    def fold_batch(acc, blocks, weight, far_ids, onehot):
        qsel = jnp.take(blocks, far_ids, axis=1)
        part = jnp.einsum(
            "rtb,tab->rta",
            qsel,
            weight,
            precision=lax.Precision.HIGH,
            preferred_element_type=jnp.float32,
        )
        return acc + jnp.einsum(
            "pt,rta->rpa",
            onehot,
            part,
            precision=lax.Precision.HIGHEST,
            preferred_element_type=jnp.float32,
        )

    def hydro_pass(start, stop, pos_far, blocks, carry, clip):
        def step(turn, carry):
            acc, stored = carry
            offset = start + turn * batch
            near_ids, far_ids, onehot = batch_lists(offset, stop, clip)
            near = jnp.take(pos_local, near_ids, axis=1)
            far = jnp.take(pos_far, far_ids, axis=1)
            weight = kernel_tile(near, far)
            stored = lax.dynamic_update_slice_in_dim(stored, weight, offset, 0)
            return (fold_batch(acc, blocks, weight, far_ids, onehot), stored)

        return lax.fori_loop(0, (stop - start + batch - 1) // batch, step, carry)

    acc_start = jnp.zeros((nrow, nblocks, TILE), jnp.float32)
    stored_start = jnp.zeros((tiles_total + batch, TILE, TILE), jnp.float32)
    carry = hydro_pass(0, first_n, pos_local, q_local_blocks, (acc_start, stored_start), True)
    acc, stored = hydro_pass(first_n, count, pos_blocks, q_blocks, carry, False)
    acc = acc.reshape(nrow, nlocal)
    rate, count_n = hydro_rate(acc, qlocal, ch)
    density_new = density + dt * rate[0]
    momentum_new = momentum + dt * rate[1:4]
    yzero = field + dt * rate[4:7]
    psi_new = (psi + dt * rate[7]) * jnp.exp(-damping * dt * ch)

    def diff_pass(start, stop, blocks, acc, clip):
        def step(turn, acc_diff):
            offset = start + turn * batch
            near_ids, far_ids, onehot = batch_lists(offset, stop, clip)
            weight = lax.dynamic_slice_in_dim(stored, offset, batch, 0)
            return fold_batch(acc_diff, blocks, weight, far_ids, onehot)

        return lax.fori_loop(0, (stop - start + batch - 1) // batch, step, acc)

    def operator(bfl):
        eta = ohmic + fac * jnp.sum(bfl * bfl, axis=0)
        q_near = jnp.concatenate([bfl, eta[None] * bfl, eta[None]], axis=0)
        acc_diff = diff_pass(
            0, first_n, q_near.reshape(7, nblocks, TILE), jnp.zeros((7, nblocks, TILE), jnp.float32), True
        )
        ghost_b = spread_ghosts(bfl, ghost_index)
        ghost_eta = ghosts[13] + ghosts[14] * jnp.sum(ghost_b * ghost_b, axis=0)
        b_ext = extend(bfl, ghost_b)
        eta_ext = extend(eta[None], ghost_eta[None])[0]
        qdiff = jnp.concatenate([b_ext, eta_ext[None] * b_ext, eta_ext[None]], axis=0)
        diff_blocks = qdiff.reshape(7, EXT_BLOCKS, TILE)
        acc_diff = diff_pass(first_n, count, diff_blocks, acc_diff, False)
        return diffusion_rate(acc_diff.reshape(7, nlocal), bfl, eta, count_n)

    first, rows = rkl_table(SECTIONS)
    lzero = operator(yzero)
    older = yzero
    prev = yzero + first * dt * lzero
    for mu_j, nu_j, mut_j, gam_j in rows:
        nxt = (
            mu_j * prev
            + nu_j * older
            + (1.0 - mu_j - nu_j) * yzero
            + mut_j * dt * operator(prev)
            + gam_j * dt * lzero
        )
        older = prev
        prev = nxt
    return (density_new, momentum_new, prev, psi_new)


def solution(mesh):
    placed = (
        P(None, ("gx", "gy")),
        P(("gx", "gy")),
        P(None, ("gx", "gy")),
        P(None, ("gx", "gy")),
        P(("gx", "gy")),
        P(("gx", "gy")),
        P(("gx", "gy")),
        P(("gx", "gy")),
        P(("gx", "gy")),
        P(("gx", "gy")),
        P(("gx", "gy")),
    )
    return jax.shard_map(
        shards,
        mesh=mesh,
        in_specs=placed,
        out_specs=(P(("gx", "gy")), P(None, ("gx", "gy")), P(None, ("gx", "gy")), P(("gx", "gy"))),
        check_vma=False,
    )
```

profile of v0, /device:TPU:0, one launch (start us, length us, event | category | flops | bytes accessed | tf_op | source)
XLA Modules:
  0.0 189.3 jit_solution(10829627870983480777)
XLA Ops:
  14.7 7.3 %all-to-all-start = ((f32[32,16,320]{2,1,0:T(8,128)}), f32[32,16,320]{2,1,0:T(8,128)S(1)}, u32[]{:S(2)}, u32[]{:S(2)}) async-start(f32[32,16,320]{2,1,0:T(8,128)} %concatenate.178), calls=%async_computation | async-start | bytes 1572864 | tf_op jit(solution)/shard_map/all_to_all | solution.py:145
  29.0 3.4 %broadcast_in_dim.295 = f32[96,128,128]{2,1,0:T(8,128)} broadcast(f32[]{:T(128)} %constant.480.clone.1), dimensions={} | broadcast | bytes 6291460 | tf_op jit(solution)/shard_map/broadcast_in_dim | solution.py:254
  32.5 11.5 %while.114 = (s32[]{:T(128)}, f32[53,16,128]{2,1,0:T(8,128)S(1)}, f32[96,128,128]{2,1,0:T(8,128)}, s32[]{:T(128)}, s32[96]{0:T(128)S(1)}, /*index=5*/f32[3,16,12...) while((s32[]{:T(128)}, f32[53,16,128]{2,1,0:T(8,128)S(1)}, ...), condition=%wide.region_11.13_spmd.clone, body=%wide.region_10.12_spmd.clone.sunk | while | flops 221341248 | bytes 8103835 | solution.py:251
  34.1 3.1 %fusion.407 = f32[96,128,128]{2,1,0:T(8,128)} fusion(f32[96,128,128]{2,1,0:T(8,128)} %get-tuple-element.1955, s32[]{:T(128)S(6)} %select_n.1019, f32[32,128]{1,0:T(8,128)S(1)} %bitcast.739, f32[32,128]{1,0:T(8,128)S(1)} %bitcast.751, f32[32,128]{1,0:T(8,128)S(1)} %bitcast.741, f32[32,128]{1,0:T(8,128)S(1)} %bitcast.753, f32[32,128]{1,0:T(8,128)S(1)} %bitcast.737, ...), kind=kLoop, calls=%fused_computation.36.clone.1 | loop fusion | flops 6291456 | bytes 2195460 | tf_op jit(solution)/shard_map/while/body/dynamic_update_slice | solution.py:248
  37.8 4.9 %fusion.405 = f32[53,32,128]{2,0,1:T(8,128)S(1)} fusion(f32[32,128]{1,0:T(8,128)S(1)} %bitcast.740, f32[32,128]{1,0:T(8,128)S(1)} %bitcast.752, f32[32,128]{1,0:T(8,128)S(1)} %bitcast.742, f32[32,128]{1,0:T(8,128)S(1)} %bitcast.754, f32[32,128]{1,0:T(8,128)S(1)} %bitcast.738, f32[32,128]{1,0:T(8,128)S(1)} %bitcast.750, ...), kind=kOutput, calls=%fused_computation.38.clone.1 | convolution fusion | flops 173232128 | bytes 1835040 | tf_op jit(solution)/shard_map/while/body/rtb,tab->rta/dot_general | solution.py:225
  50.9 12.3 %while.115 = (s32[]{:T(128)}, f32[53,16,128]{2,1,0:T(8,128)S(1)}, f32[96,128,128]{2,1,0:T(8,128)}, s32[]{:T(128)}, s32[]{:T(128)}, /*index=5*/s32[96]{0:T(128)S(...) while((s32[]{:T(128)}, f32[53,16,128]{2,1,0:T(8,128)S(1)}, ...), condition=%wide.region_14.16_spmd.clone, body=%wide.region_13.15_spmd.clone.sunk | while | flops 221341216 | bytes 8103863 | solution.py:251
  53.2 3.1 %fusion.415 = f32[96,128,128]{2,1,0:T(8,128)} fusion(f32[96,128,128]{2,1,0:T(8,128)} %get-tuple-element.1996, s32[]{:T(128)S(6)} %select_n.1025, f32[32,128]{1,0:T(8,128)S(1)} %bitcast.745, f32[32,128]{1,0:T(8,128)S(1)} %bitcast.757, f32[32,128]{1,0:T(8,128)S(1)} %bitcast.747, f32[32,128]{1,0:T(8,128)S(1)} %bitcast.759, f32[32,128]{1,0:T(8,128)S(1)} %bitcast.743, ...), kind=kLoop, calls=%fused_computation.74.clone.1 | loop fusion | flops 6291456 | bytes 2195460 | tf_op jit(solution)/shard_map/while/body/dynamic_update_slice | solution.py:248
  56.8 4.9 %fusion.413 = f32[53,32,128]{2,0,1:T(8,128)S(1)} fusion(f32[32,128]{1,0:T(8,128)S(1)} %bitcast.746, f32[32,128]{1,0:T(8,128)S(1)} %bitcast.758, f32[32,128]{1,0:T(8,128)S(1)} %bitcast.748, f32[32,128]{1,0:T(8,128)S(1)} %bitcast.760, f32[32,128]{1,0:T(8,128)S(1)} %bitcast.744, f32[32,128]{1,0:T(8,128)S(1)} %bitcast.756, ...), kind=kOutput, calls=%fused_computation.76.clone.1 | convolution fusion | flops 173232128 | bytes 1835040 | tf_op jit(solution)/shard_map/while/body/rtb,tab->rta/dot_general | solution.py:225
  73.4 16.4 %all-to-all-start.1 = ((f32[32,3,320]{2,1,0:T(4,128)}), f32[32,3,320]{2,1,0:T(4,128)S(1)}, u32[]{:S(2)}, u32[]{:S(2)}) async-start(f32[32,3,320]{2,1,0:T(4,128)} %broadcast_select_fusion.4), calls=%async_computation.1 | async-start | bytes 393216 | tf_op jit(solution)/shard_map/all_to_all | solution.py:145
  89.9 5.0 %while.116 = (s32[]{:T(128)}, f32[7,16,128]{2,1,0:T(8,128)S(1)}, s32[]{:T(128)}, f32[96,128,128]{2,1,0:T(8,128)}, s32[96]{0:T(128)S(1)}, /*index=5*/f32[7,16,128...) while((s32[]{:T(128)}, f32[7,16,128]{2,1,0:T(8,128)S(1)}, ...), condition=%wide.region_17.20_spmd.clone, body=%wide.region_16.19_spmd.clone.sunk | while | flops 27570468 | bytes 2790583 | solution.py:271
  91.3 3.4 %fusion.420 = f32[7,32,128]{2,0,1:T(8,128)S(1)} fusion(f32[96,128,128]{2,1,0:T(8,128)} %get-tuple-element.2051, s32[]{:T(128)S(6)} %select_n.1027, f32[32,7,128]{2,1,0:T(8,128)S(1)} %gather_fusion.6, pred[32]{0:T(512)(128)(4,1)S(1)} %get-tuple-element.1857), kind=kOutput, calls=%fused_computation.113.clone.1 | convolution fusion | flops 22048768 | bytes 2326564 | tf_op jit(solution)/shard_map/while/body/rtb,tab->rta/dot_general | solution.py:225
  99.7 5.6 %while.117 = (s32[]{:T(128)}, f32[7,16,128]{2,1,0:T(8,128)S(1)}, s32[]{:T(128)}, s32[]{:T(128)}, f32[96,128,128]{2,1,0:T(8,128)}, /*index=5*/s32[96]{0:T(128)S(1...) while((s32[]{:T(128)}, f32[7,16,128]{2,1,0:T(8,128)S(1)}, ...), condition=%wide.region_20.26_spmd.clone, body=%wide.region_19.25_spmd.clone.sunk | while | flops 27570440 | bytes 2790603 | solution.py:271
  101.7 3.4 %fusion.426 = f32[7,32,128]{2,0,1:T(8,128)S(1)} fusion(f32[96,128,128]{2,1,0:T(8,128)} %get-tuple-element.2090, s32[]{:T(128)S(6)} %select_n.1029, f32[32,7,128]{2,1,0:T(8,128)S(1)} %gather_fusion.7, pred[32]{0:T(512)(128)(4,1)S(1)} %get-tuple-element.1869), kind=kOutput, calls=%fused_computation.134.clone.1 | convolution fusion | flops 22048768 | bytes 2326564 | tf_op jit(solution)/shard_map/while/body/rtb,tab->rta/dot_general | solution.py:225
  111.1 7.7 %all-to-all-start.2 = ((f32[32,3,320]{2,1,0:T(4,128)}), f32[32,3,320]{2,1,0:T(4,128)S(1)}, u32[]{:S(2)}, u32[]{:S(2)}) async-start(f32[32,3,320]{2,1,0:T(4,128)} %broadcast_select_fusion.3), calls=%async_computation.2 | async-start | bytes 393216 | tf_op jit(solution)/shard_map/all_to_all | solution.py:145
  118.9 5.0 %while.118 = (s32[]{:T(128)}, f32[7,16,128]{2,1,0:T(8,128)S(1)}, s32[]{:T(128)}, f32[96,128,128]{2,1,0:T(8,128)}, s32[96]{0:T(128)S(1)}, /*index=5*/f32[7,16,128...) while((s32[]{:T(128)}, f32[7,16,128]{2,1,0:T(8,128)S(1)}, ...), condition=%wide.region_23.29_spmd.clone, body=%wide.region_22.28_spmd.clone.sunk | while | flops 27570468 | bytes 2790583 | solution.py:271
  120.3 3.4 %fusion.432 = f32[7,32,128]{2,0,1:T(8,128)S(1)} fusion(f32[96,128,128]{2,1,0:T(8,128)} %get-tuple-element.2126, s32[]{:T(128)S(6)} %select_n.1031, f32[32,7,128]{2,1,0:T(8,128)S(1)} %gather_fusion.8, pred[32]{0:T(512)(128)(4,1)S(1)} %get-tuple-element.1880), kind=kOutput, calls=%fused_computation.155.clone.1 | convolution fusion | flops 22048768 | bytes 2326564 | tf_op jit(solution)/shard_map/while/body/rtb,tab->rta/dot_general | solution.py:225
  123.9 4.2 %all-to-all-done.2 = f32[32,3,320]{2,1,0:T(4,128)S(1)} async-done(((f32[32,3,320]{2,1,0:T(4,128)}), f32[32,3,320]{2,1,0:T(4,128)S(1)}, u32[]{:S(2)}, u32[]{:S(2)}) %all-to-all-start.2) | async-done | bytes 122912 | tf_op jit(solution)/shard_map/all_to_all | solution.py:145
  128.7 5.8 %while.119 = (s32[]{:T(128)}, f32[7,16,128]{2,1,0:T(8,128)S(1)}, s32[]{:T(128)}, s32[]{:T(128)}, f32[96,128,128]{2,1,0:T(8,128)}, /*index=5*/s32[96]{0:T(128)S(1...) while((s32[]{:T(128)}, f32[7,16,128]{2,1,0:T(8,128)S(1)}, ...), condition=%wide.region_26.32_spmd.clone, body=%wide.region_25.31_spmd.clone.sunk | while | flops 27570440 | bytes 2790603 | solution.py:271
  130.7 3.4 %fusion.438 = f32[7,32,128]{2,0,1:T(8,128)S(1)} fusion(f32[96,128,128]{2,1,0:T(8,128)} %get-tuple-element.2165, s32[]{:T(128)S(6)} %select_n.1033, f32[32,7,128]{2,1,0:T(8,128)S(1)} %gather_fusion.9, pred[32]{0:T(512)(128)(4,1)S(1)} %get-tuple-element.1892), kind=kOutput, calls=%fused_computation.176.clone.1 | convolution fusion | flops 22048768 | bytes 2326564 | tf_op jit(solution)/shard_map/while/body/rtb,tab->rta/dot_general | solution.py:225
  135.1 2.4 %gather_fusion.21 = f32[1088,3]{1,0:T(8,128)S(1)} fusion(f32[3,2048]{0,1:T(8,128)S(1)} %copy.453, s32[2048]{0:T(1024)S(1)} %pad_clamp_fusion.12), kind=kCustom, calls=%fused_computation.14.clone | custom fusion | bytes 30464 | tf_op jit(solution)/shard_map/jit(_take)/gather | solution.py:124
  140.4 5.6 %all-to-all-start.3 = ((f32[32,3,320]{2,1,0:T(4,128)}), f32[32,3,320]{2,1,0:T(4,128)S(1)}, u32[]{:S(2)}, u32[]{:S(2)}) async-start(f32[32,3,320]{2,1,0:T(4,128)} %broadcast_select_fusion.2), calls=%async_computation.3 | async-start | bytes 393216 | tf_op jit(solution)/shard_map/all_to_all | solution.py:145
  146.1 5.0 %while.120 = (s32[]{:T(128)}, f32[7,16,128]{2,1,0:T(8,128)S(1)}, s32[]{:T(128)}, f32[96,128,128]{2,1,0:T(8,128)}, s32[96]{0:T(128)S(1)}, /*index=5*/f32[7,16,128...) while((s32[]{:T(128)}, f32[7,16,128]{2,1,0:T(8,128)S(1)}, ...), condition=%wide.region_29.35_spmd.clone, body=%wide.region_28.34_spmd.clone.sunk | while | flops 27570468 | bytes 2790583 | solution.py:271
  147.5 3.4 %fusion.444 = f32[7,32,128]{2,0,1:T(8,128)S(1)} fusion(f32[96,128,128]{2,1,0:T(8,128)} %get-tuple-element.2201, s32[]{:T(128)S(6)} %select_n.1035, f32[32,7,128]{2,1,0:T(8,128)S(1)} %gather_fusion.10, pred[32]{0:T(512)(128)(4,1)S(1)} %get-tuple-element.1903), kind=kOutput, calls=%fused_computation.197.clone.1 | convolution fusion | flops 22048768 | bytes 2326564 | tf_op jit(solution)/shard_map/while/body/rtb,tab->rta/dot_general | solution.py:225
  151.1 4.2 %all-to-all-done.3 = f32[32,3,320]{2,1,0:T(4,128)S(1)} async-done(((f32[32,3,320]{2,1,0:T(4,128)}), f32[32,3,320]{2,1,0:T(4,128)S(1)}, u32[]{:S(2)}, u32[]{:S(2)}) %all-to-all-start.3) | async-done | bytes 122912 | tf_op jit(solution)/shard_map/all_to_all | solution.py:145
  155.9 5.6 %while.121 = (s32[]{:T(128)}, f32[7,16,128]{2,1,0:T(8,128)S(1)}, s32[]{:T(128)}, s32[]{:T(128)}, f32[96,128,128]{2,1,0:T(8,128)}, /*index=5*/s32[96]{0:T(128)S(1...) while((s32[]{:T(128)}, f32[7,16,128]{2,1,0:T(8,128)S(1)}, ...), condition=%wide.region_32.38_spmd.clone, body=%wide.region_31.37_spmd.clone.sunk | while | flops 27570440 | bytes 2790603 | solution.py:271
  157.9 3.4 %fusion.450 = f32[7,32,128]{2,0,1:T(8,128)S(1)} fusion(f32[96,128,128]{2,1,0:T(8,128)} %get-tuple-element.2240, s32[]{:T(128)S(6)} %select_n.1037, f32[32,7,128]{2,1,0:T(8,128)S(1)} %gather_fusion.11, pred[32]{0:T(512)(128)(4,1)S(1)} %get-tuple-element.1915), kind=kOutput, calls=%fused_computation.218.clone.1 | convolution fusion | flops 22048768 | bytes 2326564 | tf_op jit(solution)/shard_map/while/body/rtb,tab->rta/dot_general | solution.py:225
  167.4 5.6 %all-to-all-start.4 = ((f32[32,3,320]{2,1,0:T(4,128)}), f32[32,3,320]{2,1,0:T(4,128)S(1)}, u32[]{:S(2)}, u32[]{:S(2)}) async-start(f32[32,3,320]{2,1,0:T(4,128)} %broadcast_select_fusion.1), calls=%async_computation.4 | async-start | bytes 393216 | tf_op jit(solution)/shard_map/all_to_all | solution.py:145
  173.1 5.0 %while.122 = (s32[]{:T(128)}, f32[7,16,128]{2,1,0:T(8,128)S(1)}, s32[]{:T(128)}, f32[96,128,128]{2,1,0:T(8,128)}, s32[96]{0:T(128)S(1)}, /*index=5*/f32[7,16,128...) while((s32[]{:T(128)}, f32[7,16,128]{2,1,0:T(8,128)S(1)}, ...), condition=%wide.region_35.41_spmd.clone, body=%wide.region_34.40_spmd.clone.sunk | while | flops 27570468 | bytes 2790583 | solution.py:271
  174.5 3.4 %fusion.456 = f32[7,32,128]{2,0,1:T(8,128)S(1)} fusion(f32[96,128,128]{2,1,0:T(8,128)} %get-tuple-element.2276, s32[]{:T(128)S(6)} %select_n.1039, f32[32,7,128]{2,1,0:T(8,128)S(1)} %gather_fusion.12, pred[32]{0:T(512)(128)(4,1)S(1)} %get-tuple-element.1926), kind=kOutput, calls=%fused_computation.239.clone.1 | convolution fusion | flops 22048768 | bytes 2326564 | tf_op jit(solution)/shard_map/while/body/rtb,tab->rta/dot_general | solution.py:225
  178.1 4.2 %all-to-all-done.4 = f32[32,3,320]{2,1,0:T(4,128)S(1)} async-done(((f32[32,3,320]{2,1,0:T(4,128)}), f32[32,3,320]{2,1,0:T(4,128)S(1)}, u32[]{:S(2)}, u32[]{:S(2)}) %all-to-all-start.4) | async-done | bytes 122912 | tf_op jit(solution)/shard_map/all_to_all | solution.py:145
  182.9 5.6 %while.123 = (s32[]{:T(128)}, f32[7,16,128]{2,1,0:T(8,128)S(1)}, s32[]{:T(128)}, s32[]{:T(128)}, f32[96,128,128]{2,1,0:T(8,128)}, /*index=5*/s32[96]{0:T(128)S(1...) while((s32[]{:T(128)}, f32[7,16,128]{2,1,0:T(8,128)S(1)}, ...), condition=%wide.region_38.44_spmd.clone, body=%wide.region_37.43_spmd.clone.sunk | while | flops 27570440 | bytes 2790603 | solution.py:271
  184.9 3.4 %fusion.462 = f32[7,32,128]{2,0,1:T(8,128)S(1)} fusion(f32[96,128,128]{2,1,0:T(8,128)} %get-tuple-element.2315, s32[]{:T(128)S(6)} %select_n.1041, f32[32,7,128]{2,1,0:T(8,128)S(1)} %gather_fusion.13, pred[32]{0:T(512)(128)(4,1)S(1)} %get-tuple-element.1938), kind=kOutput, calls=%fused_computation.260.clone.1 | convolution fusion | flops 22048768 | bytes 2326564 | tf_op jit(solution)/shard_map/while/body/rtb,tab->rta/dot_general | solution.py:225
  (486 shorter events, 72.0 us)
Async XLA Ops:
  0.6 9.1 %copy-start = (s32[9]{0:T(128)S(1)}, s32[9]{0:T(128)}, u32[]{:S(2)}) copy-start(s32[9]{0:T(128)} %constant.504.clone) | copy-start | bytes 112
  5.0 6.1 %copy-start.24 = (pred[320]{0:T(512)(128)(4,1)S(1)}, pred[320]{0:T(512)(128)(4,1)}, u32[]{:S(2)}) copy-start(pred[320]{0:T(512)(128)(4,1)} %constant.476.clone.1) | copy-start | bytes 964
  11.1 1.8 copy-start.22
  12.9 9.1 %copy-start.2 = (f32[3,2048]{1,0:T(4,128)S(1)}, f32[3,2048]{1,0:T(4,128)}, u32[]{:S(2)}) copy-start(f32[3,2048]{1,0:T(4,128)} %param.49) | copy-start | bytes 73732
  13.0 9.3 %copy-start.1 = (f32[3,2048]{1,0:T(4,128)S(1)}, f32[3,2048]{1,0:T(4,128)}, u32[]{:S(2)}) copy-start(f32[3,2048]{1,0:T(4,128)} %param.46) | copy-start | bytes 73732
  13.1 10.0 %copy-start.28 = (s32[64]{0:T(128)S(1)}, s32[64]{0:T(128)}, u32[]{:S(2)}) copy-start(s32[64]{0:T(128)} %param.55) | copy-start | bytes 772
  13.1 11.4 %copy-start.3 = (f32[2048]{0:T(1024)S(1)}, f32[2048]{0:T(1024)}, u32[]{:S(2)}) copy-start(f32[2048]{0:T(1024)} %param.47) | copy-start | bytes 24580
  13.1 11.5 %copy-start.4 = (f32[2048]{0:T(1024)S(1)}, f32[2048]{0:T(1024)}, u32[]{:S(2)}) copy-start(f32[2048]{0:T(1024)} %param.50) | copy-start | bytes 24580
  14.7 32.3 %all-to-all-start = ((f32[32,16,320]{2,1,0:T(8,128)}), f32[32,16,320]{2,1,0:T(8,128)S(1)}, u32[]{:S(2)}, u32[]{:S(2)}) async-start(f32[32,16,320]{2,1,0:T(8,128)} %concatenate.178), calls=%async_computation | async-start | bytes 1572864 | tf_op jit(solution)/shard_map/all_to_all | solution.py:145
  22.3 22.4 %copy-start.14 = (f32[1,2048]{1,0:T(1,128)}, f32[1,2048]{1,0:T(1,128)S(1)}, u32[]{:S(2)}) copy-start(f32[1,2048]{1,0:T(1,128)S(1)} %get-tuple-element.1273) | copy-start | bytes 24580
  22.3 22.4 %copy-start.16 = (f32[1,2048]{1,0:T(1,128)}, f32[1,2048]{1,0:T(1,128)S(1)}, u32[]{:S(2)}) copy-start(f32[1,2048]{1,0:T(1,128)S(1)} %get-tuple-element.1274) | copy-start | bytes 24580
  22.4 22.4 %copy-start.18 = (f32[1,2048]{1,0:T(1,128)}, f32[1,2048]{1,0:T(1,128)S(1)}, u32[]{:S(2)}) copy-start(f32[1,2048]{1,0:T(1,128)S(1)} %get-tuple-element.1275) | copy-start | bytes 24580
  24.5 4.3 %copy-start.29 = (s32[64]{0:T(128)S(1)}, s32[64]{0:T(128)}, u32[]{:S(2)}) copy-start(s32[64]{0:T(128)} %param.54) | copy-start | bytes 772
  32.5 13.9 %copy-start.27 = (s32[32]{0:T(128)S(1)}, s32[32]{0:T(128)}, u32[]{:S(2)}) copy-start(s32[32]{0:T(128)} %get-tuple-element.1079) | copy-start | bytes 388
  44.0 3.0 %copy-start.20 = (s32[96]{0:T(128)}, s32[96]{0:T(128)S(1)}, u32[]{:S(2)}) copy-start(s32[96]{0:T(128)S(1)} %get-tuple-element.2347) | copy-start | bytes 1156
  47.0 1.5 copy-start.5
  47.1 2.4 %copy-start.12 = (f32[15,32]{1,0:T(8,128)}, f32[15,32]{1,0:T(8,128)S(1)}, u32[]{:S(2)}) copy-start(f32[15,32]{1,0:T(8,128)S(1)} %slice_select_fusion.10) | copy-start | bytes 5764
  49.3 1.5 copy-start.21
  50.8 15.1 %copy-start.15 = (f32[1,2048]{1,0:T(1,128)S(1)}, f32[1,2048]{1,0:T(1,128)}, u32[]{:S(2)}) copy-start(f32[1,2048]{1,0:T(1,128)} %copy-done.14) | copy-start | bytes 24580
  50.9 15.1 %copy-start.17 = (f32[1,2048]{1,0:T(1,128)S(1)}, f32[1,2048]{1,0:T(1,128)}, u32[]{:S(2)}) copy-start(f32[1,2048]{1,0:T(1,128)} %copy-done.16) | copy-start | bytes 24580
  50.9 15.1 %copy-start.19 = (f32[1,2048]{1,0:T(1,128)S(1)}, f32[1,2048]{1,0:T(1,128)}, u32[]{:S(2)}) copy-start(f32[1,2048]{1,0:T(1,128)} %copy-done.18) | copy-start | bytes 24580
  63.2 7.4 %copy-start.25 = (pred[320]{0:T(512)(128)(4,1)S(1)}, pred[320]{0:T(512)(128)(4,1)}, u32[]{:S(2)}) copy-start(pred[320]{0:T(512)(128)(4,1)} %constant.476.clone.1) | copy-start | bytes 964
  70.6 2.0 %copy-start.23 = (pred[32]{0:T(512)(128)(4,1)S(1)}, pred[32]{0:T(512)(128)(4,1)}, u32[]{:S(2)}) copy-start(pred[32]{0:T(512)(128)(4,1)} %copy-done.22) | copy-start | bytes 100
  70.8 19.0 %copy-start.7 = (f32[2048]{0:T(1024)S(1)}, f32[2048]{0:T(1024)}, u32[]{:S(2)}) copy-start(f32[2048]{0:T(1024)} %param.51) | copy-start | bytes 24580
  73.4 25.7 %all-to-all-start.1 = ((f32[32,3,320]{2,1,0:T(4,128)}), f32[32,3,320]{2,1,0:T(4,128)S(1)}, u32[]{:S(2)}, u32[]{:S(2)}) async-start(f32[32,3,320]{2,1,0:T(4,128)} %broadcast_select_fusion.4), calls=%async_computation.1 | async-start | bytes 393216 | tf_op jit(solution)/shard_map/all_to_all | solution.py:145
  89.9 5.1 %copy-start.6 = (f32[15,160]{1,0:T(8,128)S(1)}, f32[15,160]{1,0:T(8,128)}, u32[]{:S(2)}) copy-start(f32[15,160]{1,0:T(8,128)} %copy-done.5) | copy-start | bytes 28804
  89.9 5.0 %copy-start.9 = (f32[15,32]{1,0:T(8,128)S(1)}, f32[15,32]{1,0:T(8,128)}, u32[]{:S(2)}) copy-start(f32[15,32]{1,0:T(8,128)} %copy-done.8) | copy-start | bytes 5764
  89.9 5.0 %copy-start.11 = (f32[15,32]{1,0:T(8,128)S(1)}, f32[15,32]{1,0:T(8,128)}, u32[]{:S(2)}) copy-start(f32[15,32]{1,0:T(8,128)} %copy-done.10) | copy-start | bytes 5764
  89.9 5.0 %copy-start.13 = (f32[15,32]{1,0:T(8,128)S(1)}, f32[15,32]{1,0:T(8,128)}, u32[]{:S(2)}) copy-start(f32[15,32]{1,0:T(8,128)} %copy-done.12) | copy-start | bytes 5764
  111.1 17.0 %all-to-all-start.2 = ((f32[32,3,320]{2,1,0:T(4,128)}), f32[32,3,320]{2,1,0:T(4,128)S(1)}, u32[]{:S(2)}, u32[]{:S(2)}) async-start(f32[32,3,320]{2,1,0:T(4,128)} %broadcast_select_fusion.3), calls=%async_computation.2 | async-start | bytes 393216 | tf_op jit(solution)/shard_map/all_to_all | solution.py:145
  140.4 14.9 %all-to-all-start.3 = ((f32[32,3,320]{2,1,0:T(4,128)}), f32[32,3,320]{2,1,0:T(4,128)S(1)}, u32[]{:S(2)}, u32[]{:S(2)}) async-start(f32[32,3,320]{2,1,0:T(4,128)} %broadcast_select_fusion.2), calls=%async_computation.3 | async-start | bytes 393216 | tf_op jit(solution)/shard_map/all_to_all | solution.py:145
  167.4 14.9 %all-to-all-start.4 = ((f32[32,3,320]{2,1,0:T(4,128)}), f32[32,3,320]{2,1,0:T(4,128)S(1)}, u32[]{:S(2)}, u32[]{:S(2)}) async-start(f32[32,3,320]{2,1,0:T(4,128)} %broadcast_select_fusion.1), calls=%async_computation.4 | async-start | bytes 393216 | tf_op jit(solution)/shard_map/all_to_all | solution.py:145
  (3 other events, 4.3 us)
where the time goes:
time: 191 us; the launch traced here: 189 us
  local copies, waits for them, and re-layouts  46.1 us (24%)
  starting transfers between devices  42.7 us (22%)
  matrix products  39.3 us (21%)
  other arithmetic  33 us (17%)
  waiting for transfers between devices  14.8 us (8%)
  between operations  9.05 us (5%)
  loops' own time  4.18 us (2%)
    all_to_all x5, starting transfers between devices, spread_ghosts(): incoming = lax.all_to_all(outgoing, ('gx', 'gy'), 0, 0, tiled=True)  42.7 us
    dot_general x10, matrix products, fold_batch(): jnp.einsum('rtb,tab->rta', qsel, weight, precision=lax.Precision.HIGH, pr...  36.7 us
    all_to_all x5, waiting for transfers between devices, spread_ghosts(): incoming = lax.all_to_all(outgoing, ('gx', 'gy'), 0, 0, tiled=True)  14.8 us
    gather x5, local copies, waits for them, and re-layouts, spread_ghosts(): sent = jnp.take(rows, ghost_index, axis=1)  12 us
    dynamic_update_slice x2, other arithmetic, step(): stored = lax.dynamic_update_slice_in_dim(stored, weight, offset, 0)  6.13 us
    gather x10, local copies, waits for them, and re-layouts, fold_batch(): qsel = jnp.take(blocks, far_ids, axis=1)  5.9 us
    and x8, other arithmetic, fold_batch(): qsel = jnp.take(blocks, far_ids, axis=1)  5.77 us
    another operation x68, local copies, waits for them, and re-layouts, spread_ghosts(): segments = jnp.stack(segments)  4.7 us
  transfers between devices with their start and end apart: 5, of which 4 were waited for; matrix products, arithmetic and copies ran while one was open for 22% of the time, Pallas kernels for 0%

commit v1 on v0

--- a/solution.py
+++ b/solution.py
@@ -196,7 +196,7 @@
     q_local_blocks = qlocal.reshape(nrow, nblocks, TILE)
     count = tile_count[0]
     tiles_total = tile_i.shape[0]
-    batch = math.gcd(32, tiles_total)
+    batch = math.gcd(16, tiles_total)
     block_ids = jnp.arange(nblocks, dtype=jnp.int32)
     slots = jnp.arange(tiles_total, dtype=jnp.int32)
     key = jnp.where(slots < count, (tile_j >= nblocks).astype(jnp.int32), 2)

time: 191 us -> 215 us (1.13)
  the two profiles are of different devices: /device:TPU:0 before, /device:TPU:21 now
where the time goes in v1:
time: 215 us; the launch traced here: 217 us
  matrix products  61.7 us (29%)
  local copies, waits for them, and re-layouts  58.4 us (27%)
  other arithmetic  48.8 us (23%)
  starting transfers between devices  29.5 us (14%)
  between operations  9.53 us (4%)
  loops' own time  8.81 us (4%)
    dot_general x25, matrix products, fold_batch(): jnp.einsum('rtb,tab->rta', qsel, weight, precision=lax.Precision.HIGH, pr...  56 us
    all_to_all x5, starting transfers between devices, spread_ghosts(): incoming = lax.all_to_all(outgoing, ('gx', 'gy'), 0, 0, tiled=True)  29.5 us
    and x20, other arithmetic, fold_batch(): qsel = jnp.take(blocks, far_ids, axis=1)  15.1 us
    gather x25, local copies, waits for them, and re-layouts, fold_batch(): qsel = jnp.take(blocks, far_ids, axis=1)  14.2 us
    gather x5, local copies, waits for them, and re-layouts, spread_ghosts(): sent = jnp.take(rows, ghost_index, axis=1)  12 us
    dynamic_update_slice x5, other arithmetic, step(): stored = lax.dynamic_update_slice_in_dim(stored, weight, offset, 0)  9.01 us
    another operation x8, loops' own time, diff_pass(): return lax.fori_loop(0, (stop - start + batch - 1) // batch, step, acc)  6.64 us
    dot_general x25, matrix products, fold_batch(): jnp.einsum('pt,rta->rpa', onehot, part, precision=lax.Precision.HIGHEST,...  5.69 us
  transfers between devices with their start and end apart: 5, of which 0 were waited for; matrix products, arithmetic and copies ran while one was open for 36% of the time, Pallas kernels for 0%

profile of v1, /device:TPU:21, one launch (start us, length us, event | category | flops | bytes accessed | tf_op | source)
XLA Modules:
  0.0 216.6 jit_solution(15732515313329426881)
XLA Ops:
  7.0 2.4 %gather_fusion.15 = f32[1088,15]{1,0:T(8,128)S(1)} fusion(f32[15,2048]{0,1:T(8,128)S(1)} %copy.406, s32[2048]{0:T(1024)S(1)} %pad_clamp_fusion.12), kind=kCustom, calls=%fused_computation.23 | custom fusion | bytes 134912 | tf_op jit(solution)/shard_map/jit(_take)/gather | solution.py:124
  16.0 6.2 %all-to-all-start = ((f32[32,16,320]{2,1,0:T(8,128)}), f32[32,16,320]{2,1,0:T(8,128)S(1)}, u32[]{:S(2)}, u32[]{:S(2)}) async-start(f32[32,16,320]{2,1,0:T(8,128)} %concatenate.178), calls=%async_computation | async-start | bytes 1572864 | tf_op jit(solution)/shard_map/all_to_all | solution.py:145
  28.7 3.0 %broadcast_in_dim.295 = f32[80,128,128]{2,1,0:T(8,128)} broadcast(f32[]{:T(128)} %constant.480.clone.1), dimensions={} | broadcast | bytes 5242884 | tf_op jit(solution)/shard_map/broadcast_in_dim | solution.py:254
  31.8 22.8 %while.114 = (s32[]{:T(128)}, f32[53,16,128]{2,1,0:T(8,128)S(1)}, f32[80,128,128]{2,1,0:T(8,128)}, s32[]{:T(128)}, s32[80]{0:T(128)S(1)}, /*index=5*/f32[3,16,12...) while((s32[]{:T(128)}, f32[53,16,128]{2,1,0:T(8,128)S(1)}, ...), condition=%wide.region_11.13_spmd.clone, body=%wide.region_10.12_spmd.clone.sunk | while | flops 110725928 | bytes 4490283 | solution.py:251
  35.7 2.5 %convolution_bitcast_fusion.30 = f32[53,16,128]{2,0,1:T(8,128)S(1)} fusion(f32[16,128]{1,0:T(8,128)S(1)} %bitcast.747, f32[16,128]{1,0:T(8,128)S(1)} %bitcast.759, f32[16,128]{1,0:T(8,128)S(1)} %bitcast.749, f32[16,128]{1,0:T(8,128)S(1)} %bitcast.761, f32[16,128]{1,0:T(8,128)S(1)} %bitcast.745, f32[16,128]{1,0:T(8,128)S(1)} %bitcast.757, ...), kind=kOutput, calls=%fused_computation.35.clone.1 | convolution fusion | flops 86616064 | bytes 917520 | tf_op jit(solution)/shard_map/while/body/rtb,tab->rta/dot_general | solution.py:225
  43.3 2.5 %convolution_bitcast_fusion.30 = f32[53,16,128]{2,0,1:T(8,128)S(1)} fusion(f32[16,128]{1,0:T(8,128)S(1)} %bitcast.747, f32[16,128]{1,0:T(8,128)S(1)} %bitcast.759, f32[16,128]{1,0:T(8,128)S(1)} %bitcast.749, f32[16,128]{1,0:T(8,128)S(1)} %bitcast.761, f32[16,128]{1,0:T(8,128)S(1)} %bitcast.745, f32[16,128]{1,0:T(8,128)S(1)} %bitcast.757, ...), kind=kOutput, calls=%fused_computation.35.clone.1 | convolution fusion | flops 86616064 | bytes 917520 | tf_op jit(solution)/shard_map/while/body/rtb,tab->rta/dot_general | solution.py:225
  50.9 2.5 %convolution_bitcast_fusion.30 = f32[53,16,128]{2,0,1:T(8,128)S(1)} fusion(f32[16,128]{1,0:T(8,128)S(1)} %bitcast.747, f32[16,128]{1,0:T(8,128)S(1)} %bitcast.759, f32[16,128]{1,0:T(8,128)S(1)} %bitcast.749, f32[16,128]{1,0:T(8,128)S(1)} %bitcast.761, f32[16,128]{1,0:T(8,128)S(1)} %bitcast.745, f32[16,128]{1,0:T(8,128)S(1)} %bitcast.757, ...), kind=kOutput, calls=%fused_computation.35.clone.1 | convolution fusion | flops 86616064 | bytes 917520 | tf_op jit(solution)/shard_map/while/body/rtb,tab->rta/dot_general | solution.py:225
  60.8 17.9 %while.115 = (s32[]{:T(128)}, f32[53,16,128]{2,1,0:T(8,128)S(1)}, f32[80,128,128]{2,1,0:T(8,128)}, s32[]{:T(128)}, s32[]{:T(128)}, /*index=5*/s32[80]{0:T(128)},...) while((s32[]{:T(128)}, f32[53,16,128]{2,1,0:T(8,128)S(1)}, ...), condition=%wide.region_14.16_spmd.clone, body=%wide.region_13.15_spmd.clone.sunk | while | flops 110725912 | bytes 4490311 | solution.py:251
  66.1 2.5 %convolution_bitcast_fusion.31 = f32[53,16,128]{2,0,1:T(8,128)S(1)} fusion(f32[16,128]{1,0:T(8,128)S(1)} %bitcast.753, f32[16,128]{1,0:T(8,128)S(1)} %bitcast.765, f32[16,128]{1,0:T(8,128)S(1)} %bitcast.755, f32[16,128]{1,0:T(8,128)S(1)} %bitcast.767, f32[16,128]{1,0:T(8,128)S(1)} %bitcast.751, f32[16,128]{1,0:T(8,128)S(1)} %bitcast.763, ...), kind=kOutput, calls=%fused_computation.72.clone.1 | convolution fusion | flops 86616064 | bytes 917520 | tf_op jit(solution)/shard_map/while/body/rtb,tab->rta/dot_general | solution.py:225
  74.9 2.5 %convolution_bitcast_fusion.31 = f32[53,16,128]{2,0,1:T(8,128)S(1)} fusion(f32[16,128]{1,0:T(8,128)S(1)} %bitcast.753, f32[16,128]{1,0:T(8,128)S(1)} %bitcast.765, f32[16,128]{1,0:T(8,128)S(1)} %bitcast.755, f32[16,128]{1,0:T(8,128)S(1)} %bitcast.767, f32[16,128]{1,0:T(8,128)S(1)} %bitcast.751, f32[16,128]{1,0:T(8,128)S(1)} %bitcast.763, ...), kind=kOutput, calls=%fused_computation.72.clone.1 | convolution fusion | flops 86616064 | bytes 917520 | tf_op jit(solution)/shard_map/while/body/rtb,tab->rta/dot_general | solution.py:225
  82.8 2.4 %gather_fusion.17 = f32[1088,3]{1,0:T(8,128)S(1)} fusion(f32[3,2048]{0,1:T(8,128)S(1)} %copy.425, s32[2048]{0:T(1024)S(1)} %pad_clamp_fusion.12), kind=kCustom, calls=%fused_computation.2.clone | custom fusion | bytes 30464 | tf_op jit(solution)/shard_map/jit(_take)/gather | solution.py:124
  88.3 5.8 %all-to-all-start.1 = ((f32[32,3,320]{2,1,0:T(4,128)}), f32[32,3,320]{2,1,0:T(4,128)S(1)}, u32[]{:S(2)}, u32[]{:S(2)}) async-start(f32[32,3,320]{2,1,0:T(4,128)} %broadcast_select_fusion.4), calls=%async_computation.1 | async-start | bytes 393216 | tf_op jit(solution)/shard_map/all_to_all | solution.py:145
  94.2 11.5 %while.116 = (s32[]{:T(128)}, f32[7,16,128]{2,1,0:T(8,128)S(1)}, s32[]{:T(128)}, f32[80,128,128]{2,1,0:T(8,128)}, s32[80]{0:T(128)S(1)}, /*index=5*/f32[7,16,128...) while((s32[]{:T(128)}, f32[7,16,128]{2,1,0:T(8,128)S(1)}, ...), condition=%wide.region_17.20_spmd.clone, body=%wide.region_16.19_spmd.clone.sunk | while | flops 13792918 | bytes 1454775 | solution.py:271
  108.3 8.9 %while.117 = (s32[]{:T(128)}, f32[7,16,128]{2,1,0:T(8,128)S(1)}, s32[]{:T(128)}, s32[]{:T(128)}, f32[80,128,128]{2,1,0:T(8,128)}, /*index=5*/s32[80]{0:T(128)S(1...) while((s32[]{:T(128)}, f32[7,16,128]{2,1,0:T(8,128)S(1)}, ...), condition=%wide.region_20.26_spmd.clone, body=%wide.region_19.25_spmd.clone.sunk | while | flops 13792903 | bytes 1454795 | solution.py:271
  110.4 2.2 %convolution_bitcast_fusion.33 = f32[7,16,128]{2,0,1:T(8,128)S(1)} fusion(f32[80,128,128]{2,1,0:T(8,128)} %get-tuple-element.2090, s32[]{:T(128)S(6)} %select_n.1029, f32[16,7,128]{2,1,0:T(8,128)S(1)} %gather_fusion.7, pred[16]{0:T(512)(128)(4,1)S(1)} %get-tuple-element.1869), kind=kOutput, calls=%fused_computation.129.clone.1 | convolution fusion | flops 11024384 | bytes 1163284 | tf_op jit(solution)/shard_map/while/body/rtb,tab->rta/dot_general | solution.py:225
  114.8 2.2 %convolution_bitcast_fusion.33 = f32[7,16,128]{2,0,1:T(8,128)S(1)} fusion(f32[80,128,128]{2,1,0:T(8,128)} %get-tuple-element.2090, s32[]{:T(128)S(6)} %select_n.1029, f32[16,7,128]{2,1,0:T(8,128)S(1)} %gather_fusion.7, pred[16]{0:T(512)(128)(4,1)S(1)} %get-tuple-element.1869), kind=kOutput, calls=%fused_computation.129.clone.1 | convolution fusion | flops 11024384 | bytes 1163284 | tf_op jit(solution)/shard_map/while/body/rtb,tab->rta/dot_general | solution.py:225
  117.7 2.4 %gather_fusion.19 = f32[1088,3]{1,0:T(8,128)S(1)} fusion(f32[3,2048]{0,1:T(8,128)S(1)} %copy.439, s32[2048]{0:T(1024)S(1)} %pad_clamp_fusion.12), kind=kCustom, calls=%fused_computation.13.clone | custom fusion | bytes 30464 | tf_op jit(solution)/shard_map/jit(_take)/gather | solution.py:124
  123.1 5.8 %all-to-all-start.2 = ((f32[32,3,320]{2,1,0:T(4,128)}), f32[32,3,320]{2,1,0:T(4,128)S(1)}, u32[]{:S(2)}, u32[]{:S(2)}) async-start(f32[32,3,320]{2,1,0:T(4,128)} %broadcast_select_fusion.3), calls=%async_computation.2 | async-start | bytes 393216 | tf_op jit(solution)/shard_map/all_to_all | solution.py:145
  129.0 11.5 %while.118 = (s32[]{:T(128)}, f32[7,16,128]{2,1,0:T(8,128)S(1)}, s32[]{:T(128)}, f32[80,128,128]{2,1,0:T(8,128)}, s32[80]{0:T(128)S(1)}, /*index=5*/f32[7,16,128...) while((s32[]{:T(128)}, f32[7,16,128]{2,1,0:T(8,128)S(1)}, ...), condition=%wide.region_23.29_spmd.clone, body=%wide.region_22.28_spmd.clone.sunk | while | flops 13792918 | bytes 1454775 | solution.py:271
  141.1 8.9 %while.119 = (s32[]{:T(128)}, f32[7,16,128]{2,1,0:T(8,128)S(1)}, s32[]{:T(128)}, s32[]{:T(128)}, f32[80,128,128]{2,1,0:T(8,128)}, /*index=5*/s32[80]{0:T(128)S(1...) while((s32[]{:T(128)}, f32[7,16,128]{2,1,0:T(8,128)S(1)}, ...), condition=%wide.region_26.32_spmd.clone, body=%wide.region_25.31_spmd.clone.sunk | while | flops 13792903 | bytes 1454795 | solution.py:271
  143.1 2.2 %convolution_bitcast_fusion.35 = f32[7,16,128]{2,0,1:T(8,128)S(1)} fusion(f32[80,128,128]{2,1,0:T(8,128)} %get-tuple-element.2165, s32[]{:T(128)S(6)} %select_n.1033, f32[16,7,128]{2,1,0:T(8,128)S(1)} %gather_fusion.9, pred[16]{0:T(512)(128)(4,1)S(1)} %get-tuple-element.1892), kind=kOutput, calls=%fused_computation.169.clone.1 | convolution fusion | flops 11024384 | bytes 1163284 | tf_op jit(solution)/shard_map/while/body/rtb,tab->rta/dot_general | solution.py:225
  147.6 2.2 %convolution_bitcast_fusion.35 = f32[7,16,128]{2,0,1:T(8,128)S(1)} fusion(f32[80,128,128]{2,1,0:T(8,128)} %get-tuple-element.2165, s32[]{:T(128)S(6)} %select_n.1033, f32[16,7,128]{2,1,0:T(8,128)S(1)} %gather_fusion.9, pred[16]{0:T(512)(128)(4,1)S(1)} %get-tuple-element.1892), kind=kOutput, calls=%fused_computation.169.clone.1 | convolution fusion | flops 11024384 | bytes 1163284 | tf_op jit(solution)/shard_map/while/body/rtb,tab->rta/dot_general | solution.py:225
  150.5 2.4 %gather_fusion.21 = f32[1088,3]{1,0:T(8,128)S(1)} fusion(f32[3,2048]{0,1:T(8,128)S(1)} %copy.453, s32[2048]{0:T(1024)S(1)} %pad_clamp_fusion.12), kind=kCustom, calls=%fused_computation.14.clone | custom fusion | bytes 30464 | tf_op jit(solution)/shard_map/jit(_take)/gather | solution.py:124
  155.9 5.8 %all-to-all-start.3 = ((f32[32,3,320]{2,1,0:T(4,128)}), f32[32,3,320]{2,1,0:T(4,128)S(1)}, u32[]{:S(2)}, u32[]{:S(2)}) async-start(f32[32,3,320]{2,1,0:T(4,128)} %broadcast_select_fusion.2), calls=%async_computation.3 | async-start | bytes 393216 | tf_op jit(solution)/shard_map/all_to_all | solution.py:145
  161.8 11.5 %while.120 = (s32[]{:T(128)}, f32[7,16,128]{2,1,0:T(8,128)S(1)}, s32[]{:T(128)}, f32[80,128,128]{2,1,0:T(8,128)}, s32[80]{0:T(128)S(1)}, /*index=5*/f32[7,16,128...) while((s32[]{:T(128)}, f32[7,16,128]{2,1,0:T(8,128)S(1)}, ...), condition=%wide.region_29.35_spmd.clone, body=%wide.region_28.34_spmd.clone.sunk | while | flops 13792918 | bytes 1454775 | solution.py:271
  163.2 2.2 %convolution_bitcast_fusion.36 = f32[7,16,128]{2,0,1:T(8,128)S(1)} fusion(f32[80,128,128]{2,1,0:T(8,128)} %get-tuple-element.2201, s32[]{:T(128)S(6)} %select_n.1035, f32[16,7,128]{2,1,0:T(8,128)S(1)} %gather_fusion.10, pred[16]{0:T(512)(128)(4,1)S(1)} %get-tuple-element.1903), kind=kOutput, calls=%fused_computation.189.clone.1 | convolution fusion | flops 11024384 | bytes 1163284 | tf_op jit(solution)/shard_map/while/body/rtb,tab->rta/dot_general | solution.py:225
  170.8 2.2 %convolution_bitcast_fusion.36 = f32[7,16,128]{2,0,1:T(8,128)S(1)} fusion(f32[80,128,128]{2,1,0:T(8,128)} %get-tuple-element.2201, s32[]{:T(128)S(6)} %select_n.1035, f32[16,7,128]{2,1,0:T(8,128)S(1)} %gather_fusion.10, pred[16]{0:T(512)(128)(4,1)S(1)} %get-tuple-element.1903), kind=kOutput, calls=%fused_computation.189.clone.1 | convolution fusion | flops 11024384 | bytes 1163284 | tf_op jit(solution)/shard_map/while/body/rtb,tab->rta/dot_general | solution.py:225
  173.9 9.2 %while.121 = (s32[]{:T(128)}, f32[7,16,128]{2,1,0:T(8,128)S(1)}, s32[]{:T(128)}, s32[]{:T(128)}, f32[80,128,128]{2,1,0:T(8,128)}, /*index=5*/s32[80]{0:T(128)S(1...) while((s32[]{:T(128)}, f32[7,16,128]{2,1,0:T(8,128)S(1)}, ...), condition=%wide.region_32.38_spmd.clone, body=%wide.region_31.37_spmd.clone.sunk | while | flops 13792903 | bytes 1454795 | solution.py:271
  183.6 2.4 %gather_fusion.23 = f32[1088,3]{1,0:T(8,128)S(1)} fusion(f32[3,2048]{0,1:T(8,128)S(1)} %copy.467, s32[2048]{0:T(1024)S(1)} %pad_clamp_fusion.12), kind=kCustom, calls=%fused_computation.15.clone | custom fusion | bytes 30464 | tf_op jit(solution)/shard_map/jit(_take)/gather | solution.py:124
  188.9 5.8 %all-to-all-start.4 = ((f32[32,3,320]{2,1,0:T(4,128)}), f32[32,3,320]{2,1,0:T(4,128)S(1)}, u32[]{:S(2)}, u32[]{:S(2)}) async-start(f32[32,3,320]{2,1,0:T(4,128)} %broadcast_select_fusion.1), calls=%async_computation.4 | async-start | bytes 393216 | tf_op jit(solution)/shard_map/all_to_all | solution.py:145
  194.8 11.5 %while.122 = (s32[]{:T(128)}, f32[7,16,128]{2,1,0:T(8,128)S(1)}, s32[]{:T(128)}, f32[80,128,128]{2,1,0:T(8,128)}, s32[80]{0:T(128)S(1)}, /*index=5*/f32[7,16,128...) while((s32[]{:T(128)}, f32[7,16,128]{2,1,0:T(8,128)S(1)}, ...), condition=%wide.region_35.41_spmd.clone, body=%wide.region_34.40_spmd.clone.sunk | while | flops 13792918 | bytes 1454775 | solution.py:271
  206.9 8.9 %while.123 = (s32[]{:T(128)}, f32[7,16,128]{2,1,0:T(8,128)S(1)}, s32[]{:T(128)}, s32[]{:T(128)}, f32[80,128,128]{2,1,0:T(8,128)}, /*index=5*/s32[80]{0:T(128)S(1...) while((s32[]{:T(128)}, f32[7,16,128]{2,1,0:T(8,128)S(1)}, ...), condition=%wide.region_38.44_spmd.clone, body=%wide.region_37.43_spmd.clone.sunk | while | flops 13792903 | bytes 1454795 | solution.py:271
  (643 shorter events, 128.3 us)
Async XLA Ops:
  16.0 40.8 %all-to-all-start = ((f32[32,16,320]{2,1,0:T(8,128)}), f32[32,16,320]{2,1,0:T(8,128)S(1)}, u32[]{:S(2)}, u32[]{:S(2)}) async-start(f32[32,16,320]{2,1,0:T(8,128)} %concatenate.178), calls=%async_computation | async-start | bytes 1572864 | tf_op jit(solution)/shard_map/all_to_all | solution.py:145
  22.5 32.9 %copy-start.27 = (f32[1,2048]{1,0:T(1,128)}, f32[1,2048]{1,0:T(1,128)S(1)}, u32[]{:S(2)}) copy-start(f32[1,2048]{1,0:T(1,128)S(1)} %get-tuple-element.1273) | copy-start | bytes 24580
  22.5 32.9 %copy-start.29 = (f32[1,2048]{1,0:T(1,128)}, f32[1,2048]{1,0:T(1,128)S(1)}, u32[]{:S(2)}) copy-start(f32[1,2048]{1,0:T(1,128)S(1)} %get-tuple-element.1274) | copy-start | bytes 24580
  22.5 32.9 %copy-start.31 = (f32[1,2048]{1,0:T(1,128)}, f32[1,2048]{1,0:T(1,128)S(1)}, u32[]{:S(2)}) copy-start(f32[1,2048]{1,0:T(1,128)S(1)} %get-tuple-element.1275) | copy-start | bytes 24580
  25.0 30.4 %copy-start.2 = (f32[8,2048]{1,0:T(8,128)}, f32[8,2048]{1,0:T(8,128)S(1)}, u32[]{:S(2)}) copy-start(f32[8,2048]{1,0:T(8,128)S(1)} %stack.298) | copy-start | bytes 196612
  25.1 30.3 %copy-start.4 = (f32[8,2048]{1,0:T(8,128)}, f32[8,2048]{1,0:T(8,128)S(1)}, u32[]{:S(2)}) copy-start(f32[8,2048]{1,0:T(8,128)S(1)} %stack.294) | copy-start | bytes 196612
  25.2 30.2 %copy-start.6 = (f32[8,2048]{1,0:T(8,128)}, f32[8,2048]{1,0:T(8,128)S(1)}, u32[]{:S(2)}) copy-start(f32[8,2048]{1,0:T(8,128)S(1)} %stack.290) | copy-start | bytes 196612
  31.8 23.7 %copy-start.37 = (f32[1,2048]{1,0:T(1,128)S(1)}, f32[1,2048]{1,0:T(1,128)}, u32[]{:S(2)}) copy-start(f32[1,2048]{1,0:T(1,128)} %copy-done.36) | copy-start | bytes 24580
  31.8 24.4 %copy-start.46 = (s32[32]{0:T(128)S(1)}, s32[32]{0:T(128)}, u32[]{:S(2)}) copy-start(s32[32]{0:T(128)} %get-tuple-element.1079) | copy-start | bytes 388
  60.7 20.8 %copy-start.3 = (f32[8,2048]{1,0:T(8,128)S(1)}, f32[8,2048]{1,0:T(8,128)}, u32[]{:S(2)}) copy-start(f32[8,2048]{1,0:T(8,128)} %copy-done.2) | copy-start | bytes 196612
  60.7 20.8 %copy-start.5 = (f32[8,2048]{1,0:T(8,128)S(1)}, f32[8,2048]{1,0:T(8,128)}, u32[]{:S(2)}) copy-start(f32[8,2048]{1,0:T(8,128)} %copy-done.4) | copy-start | bytes 196612
  60.7 20.8 %copy-start.7 = (f32[8,2048]{1,0:T(8,128)S(1)}, f32[8,2048]{1,0:T(8,128)}, u32[]{:S(2)}) copy-start(f32[8,2048]{1,0:T(8,128)} %copy-done.6) | copy-start | bytes 196612
  60.7 20.8 %copy-start.28 = (f32[1,2048]{1,0:T(1,128)S(1)}, f32[1,2048]{1,0:T(1,128)}, u32[]{:S(2)}) copy-start(f32[1,2048]{1,0:T(1,128)} %copy-done.27) | copy-start | bytes 24580
  60.7 20.8 %copy-start.30 = (f32[1,2048]{1,0:T(1,128)S(1)}, f32[1,2048]{1,0:T(1,128)}, u32[]{:S(2)}) copy-start(f32[1,2048]{1,0:T(1,128)} %copy-done.29) | copy-start | bytes 24580
  60.7 20.8 %copy-start.32 = (f32[1,2048]{1,0:T(1,128)S(1)}, f32[1,2048]{1,0:T(1,128)}, u32[]{:S(2)}) copy-start(f32[1,2048]{1,0:T(1,128)} %copy-done.31) | copy-start | bytes 24580
  60.7 21.1 %copy-start.33 = (f32[3,2048]{1,0:T(4,128)S(1)}, f32[3,2048]{1,0:T(4,128)}, u32[]{:S(2)}) copy-start(f32[3,2048]{1,0:T(4,128)} %param.48) | copy-start | bytes 73732
  60.8 24.5 %copy-start.35 = (pred[1088]{0:T(1024)(128)(4,1)S(1)}, pred[1088]{0:T(1024)(128)(4,1)}, u32[]{:S(2)}) copy-start(pred[1088]{0:T(1024)(128)(4,1)} %copy-done.34) | copy-start | bytes 3268
  60.8 24.7 %copy-start.44 = (pred[320]{0:T(512)(128)(4,1)S(1)}, pred[320]{0:T(512)(128)(4,1)}, u32[]{:S(2)}) copy-start(pred[320]{0:T(512)(128)(4,1)} %constant.476.clone.1) | copy-start | bytes 964
  78.8 15.3 %copy-start.13 = (f32[2048]{0:T(1024)S(1)}, f32[2048]{0:T(1024)}, u32[]{:S(2)}) copy-start(f32[2048]{0:T(1024)} %copy-done.12) | copy-start | bytes 24580
  78.8 15.3 %copy-start.18 = (f32[2048]{0:T(1024)S(1)}, f32[2048]{0:T(1024)}, u32[]{:S(2)}) copy-start(f32[2048]{0:T(1024)} %param.51) | copy-start | bytes 24580
  78.8 15.4 %copy-start.41 = (s32[80]{0:T(128)S(1)}, s32[80]{0:T(128)}, u32[]{:S(2)}) copy-start(s32[80]{0:T(128)} %get-tuple-element.2348) | copy-start | bytes 964
  86.1 19.6 %copy-start.11 = (f32[15,320]{1,0:T(8,128)S(1)}, f32[15,320]{1,0:T(8,128)}, u32[]{:S(2)}) copy-start(f32[15,320]{1,0:T(8,128)} %copy-done.10) | copy-start | bytes 57604
  86.1 19.6 %copy-start.15 = (f32[15,160]{1,0:T(8,128)S(1)}, f32[15,160]{1,0:T(8,128)}, u32[]{:S(2)}) copy-start(f32[15,160]{1,0:T(8,128)} %copy-done.14) | copy-start | bytes 28804
  86.1 19.6 %copy-start.17 = (f32[15,160]{1,0:T(8,128)S(1)}, f32[15,160]{1,0:T(8,128)}, u32[]{:S(2)}) copy-start(f32[15,160]{1,0:T(8,128)} %copy-done.16) | copy-start | bytes 28804
  86.1 19.6 %copy-start.20 = (f32[15,32]{1,0:T(8,128)S(1)}, f32[15,32]{1,0:T(8,128)}, u32[]{:S(2)}) copy-start(f32[15,32]{1,0:T(8,128)} %copy-done.19) | copy-start | bytes 5764
  86.1 19.6 %copy-start.22 = (f32[15,32]{1,0:T(8,128)S(1)}, f32[15,32]{1,0:T(8,128)}, u32[]{:S(2)}) copy-start(f32[15,32]{1,0:T(8,128)} %copy-done.21) | copy-start | bytes 5764
  86.1 19.6 %copy-start.24 = (f32[15,32]{1,0:T(8,128)S(1)}, f32[15,32]{1,0:T(8,128)}, u32[]{:S(2)}) copy-start(f32[15,32]{1,0:T(8,128)} %copy-done.23) | copy-start | bytes 5764
  86.2 19.6 %copy-start.26 = (f32[15,32]{1,0:T(8,128)S(1)}, f32[15,32]{1,0:T(8,128)}, u32[]{:S(2)}) copy-start(f32[15,32]{1,0:T(8,128)} %copy-done.25) | copy-start | bytes 5764
  88.3 19.5 %all-to-all-start.1 = ((f32[32,3,320]{2,1,0:T(4,128)}), f32[32,3,320]{2,1,0:T(4,128)S(1)}, u32[]{:S(2)}, u32[]{:S(2)}) async-start(f32[32,3,320]{2,1,0:T(4,128)} %broadcast_select_fusion.4), calls=%async_computation.1 | async-start | bytes 393216 | tf_op jit(solution)/shard_map/all_to_all | solution.py:145
  123.1 17.4 %all-to-all-start.2 = ((f32[32,3,320]{2,1,0:T(4,128)}), f32[32,3,320]{2,1,0:T(4,128)S(1)}, u32[]{:S(2)}, u32[]{:S(2)}) async-start(f32[32,3,320]{2,1,0:T(4,128)} %broadcast_select_fusion.3), calls=%async_computation.2 | async-start | bytes 393216 | tf_op jit(solution)/shard_map/all_to_all | solution.py:145
  155.9 17.4 %all-to-all-start.3 = ((f32[32,3,320]{2,1,0:T(4,128)}), f32[32,3,320]{2,1,0:T(4,128)S(1)}, u32[]{:S(2)}, u32[]{:S(2)}) async-start(f32[32,3,320]{2,1,0:T(4,128)} %broadcast_select_fusion.2), calls=%async_computation.3 | async-start | bytes 393216 | tf_op jit(solution)/shard_map/all_to_all | solution.py:145
  188.9 17.4 %all-to-all-start.4 = ((f32[32,3,320]{2,1,0:T(4,128)}), f32[32,3,320]{2,1,0:T(4,128)S(1)}, u32[]{:S(2)}, u32[]{:S(2)}) async-start(f32[32,3,320]{2,1,0:T(4,128)} %broadcast_select_fusion.1), calls=%async_computation.4 | async-start | bytes 393216 | tf_op jit(solution)/shard_map/all_to_all | solution.py:145
  (23 other events, 166.0 us)

commit v2 on v0

--- a/solution.py
+++ b/solution.py
@@ -125,7 +125,7 @@
     segments = []
     for d in range(8):
         part = sent[:, starts[d] : starts[d] + sizes[d]]
-        segments.append(jnp.pad(part, ((0, 0), (0, width - sizes[d]))))
+        segments.append(jnp.pad(part, ((0, 0), (0, width - sizes[d]))).reshape(-1))
     segments.append(jnp.zeros_like(segments[0]))
     segments = jnp.stack(segments)
     table = [8] * 9
@@ -140,7 +140,7 @@
     outgoing = jnp.take(segments, pick, axis=0)
     nrows = rows.shape[0]
     if extra is not None:
-        tag = jnp.full((nx * ny, 1, width), extra, jnp.float32)
+        tag = jnp.full((nx * ny, width), extra, jnp.float32)
         outgoing = jnp.concatenate([outgoing, tag], axis=1)
     incoming = lax.all_to_all(outgoing, ("gx", "gy"), 0, 0, tiled=True)
     pieces = []
@@ -149,11 +149,12 @@
         inside = (sx >= 0) & (sx < nx) & (sy >= 0) & (sy < ny)
         source = jnp.clip(sx, 0, nx - 1) * ny + jnp.clip(sy, 0, ny - 1)
         block = lax.dynamic_index_in_dim(incoming, source, 0, keepdims=False)
-        pieces.append(jnp.where(inside, block[:nrows, : sizes[d]], 0.0))
+        block = block[: nrows * width].reshape(nrows, width)
+        pieces.append(jnp.where(inside, block[:, : sizes[d]], 0.0))
     ghosts = jnp.concatenate(pieces, axis=1)
     if extra is None:
         return ghosts
-    return (ghosts, jnp.max(incoming[:, nrows, 0]))
+    return (ghosts, jnp.max(incoming[:, nrows * width]))
 
 
 def extend(rows, extra):

time: 191 us -> 195 us (1.021)
  local copies, waits for them, and re-layouts: 46.1 us -> 53.8 us
  other arithmetic: 33 us -> 28 us
    all_to_all x0 -> x6, local copies, waits for them, and re-layouts: none -> 5.35 us  [spread_ghosts(): incoming = lax.all_to_all(outgoing, ('gx', 'gy'), 0, 0, tiled=True)]
    select_n x6 -> x2, other arithmetic: 3.28 us -> 0.13 us  [spread_ghosts(): outgoing = jnp.take(segments, pick, axis=0)]
    reshape x0 -> x30, local copies, waits for them, and re-layouts: none -> 2.3 us  [spread_ghosts(): block = block[:nrows * width].reshape(nrows, width)]
    another operation x68 -> x46, local copies, waits for them, and re-layouts: 4.7 us -> 4.48 us  [spread_ghosts(): segments = jnp.stack(segments)]
  transfers between devices with their start and end apart: 5 -> 5, of which waited for: 4 -> 4; matrix products, arithmetic and copies ran while one was open for 22% -> 18% of each run, Pallas kernels for 0% -> 0%
where the time goes in v2:
time: 195 us; the launch traced here: 191 us
  local copies, waits for them, and re-layouts  53.8 us (28%)
  starting transfers between devices  41.4 us (21%)
  matrix products  39.3 us (20%)
  other arithmetic  28 us (14%)
  waiting for transfers between devices  16.4 us (8%)
  between operations  8.4 us (4%)
  loops' own time  4.07 us (2%)
    all_to_all x5, starting transfers between devices, spread_ghosts(): incoming = lax.all_to_all(outgoing, ('gx', 'gy'), 0, 0, tiled=True)  41.4 us
    dot_general x10, matrix products, fold_batch(): jnp.einsum('rtb,tab->rta', qsel, weight, precision=lax.Precision.HIGH, pr...  36.7 us
    all_to_all x5, waiting for transfers between devices, spread_ghosts(): incoming = lax.all_to_all(outgoing, ('gx', 'gy'), 0, 0, tiled=True)  16.4 us
    gather x5, local copies, waits for them, and re-layouts, spread_ghosts(): sent = jnp.take(rows, ghost_index, axis=1)  12 us
    dynamic_update_slice x2, other arithmetic, step(): stored = lax.dynamic_update_slice_in_dim(stored, weight, offset, 0)  6.19 us
    gather x10, local copies, waits for them, and re-layouts, fold_batch(): qsel = jnp.take(blocks, far_ids, axis=1)  5.9 us
    and x8, other arithmetic, fold_batch(): qsel = jnp.take(blocks, far_ids, axis=1)  5.74 us
    all_to_all x6, local copies, waits for them, and re-layouts, spread_ghosts(): incoming = lax.all_to_all(outgoing, ('gx', 'gy'), 0, 0, tiled=True)  5.35 us
  transfers between devices with their start and end apart: 5, of which 4 were waited for; matrix products, arithmetic and copies ran while one was open for 18% of the time, Pallas kernels for 0%

profile of v2, /device:TPU:0, one launch (start us, length us, event | category | flops | bytes accessed | tf_op | source)
XLA Modules:
  0.0 191.4 jit_solution(12952137674212757450)
XLA Ops:
  15.7 7.3 %all-to-all-start = ((f32[32,1,5120]{2,1,0:T(1,128)}), f32[32,1,5120]{2,1,0:T(1,128)S(1)}, u32[]{:S(2)}, u32[]{:S(2)}) async-start(f32[32,1,5120]{2,1,0:T(1,128)} %copy.522), calls=%async_computation | async-start | bytes 1310720 | tf_op jit(solution)/shard_map/all_to_all | solution.py:145
  29.2 3.4 %broadcast_in_dim.295 = f32[96,128,128]{2,1,0:T(8,128)} broadcast(f32[]{:T(128)} %constant.520.clone.1), dimensions={} | broadcast | bytes 6291460 | tf_op jit(solution)/shard_map/broadcast_in_dim | solution.py:255
  32.6 11.5 %while.114 = (s32[]{:T(128)}, f32[53,16,128]{2,1,0:T(8,128)S(1)}, f32[96,128,128]{2,1,0:T(8,128)}, s32[]{:T(128)}, s32[96]{0:T(128)S(1)}, /*index=5*/f32[3,16,12...) while((s32[]{:T(128)}, f32[53,16,128]{2,1,0:T(8,128)S(1)}, ...), condition=%wide.region_11.13_spmd.clone, body=%wide.region_10.12_spmd.clone.sunk | while | flops 221341248 | bytes 8103843 | solution.py:252
  34.9 4.9 %fusion.397 = f32[53,32,128]{2,0,1:T(8,128)S(1)} fusion(f32[32,128]{1,0:T(8,128)S(1)} %bitcast.608, f32[32,128]{1,0:T(8,128)S(1)} %bitcast.620, f32[32,128]{1,0:T(8,128)S(1)} %bitcast.610, f32[32,128]{1,0:T(8,128)S(1)} %bitcast.622, f32[32,128]{1,0:T(8,128)S(1)} %bitcast.606, f32[32,128]{1,0:T(8,128)S(1)} %bitcast.618, ...), kind=kOutput, calls=%fused_computation.38.clone.1 | convolution fusion | flops 173232128 | bytes 1835040 | tf_op jit(solution)/shard_map/while/body/rtb,tab->rta/dot_general | solution.py:226
  41.0 3.1 %fusion.399 = f32[96,128,128]{2,1,0:T(8,128)} fusion(f32[96,128,128]{2,1,0:T(8,128)} %get-tuple-element.1953, s32[]{:T(128)S(6)} %select_n.1039, f32[32,128]{1,0:T(8,128)S(1)} %bitcast.609, f32[32,128]{1,0:T(8,128)S(1)} %bitcast.621, f32[32,128]{1,0:T(8,128)S(1)} %bitcast.611, f32[32,128]{1,0:T(8,128)S(1)} %bitcast.623, f32[32,128]{1,0:T(8,128)S(1)} %bitcast.607, ...), kind=kLoop, calls=%fused_computation.36.clone.1 | loop fusion | flops 6291456 | bytes 2195460 | tf_op jit(solution)/shard_map/while/body/dynamic_update_slice | solution.py:249
  48.8 12.4 %while.115 = (s32[]{:T(128)}, f32[53,16,128]{2,1,0:T(8,128)S(1)}, f32[96,128,128]{2,1,0:T(8,128)}, s32[]{:T(128)}, s32[]{:T(128)}, /*index=5*/s32[96]{0:T(128)S(...) while((s32[]{:T(128)}, f32[53,16,128]{2,1,0:T(8,128)S(1)}, ...), condition=%wide.region_14.16_spmd.clone, body=%wide.region_13.15_spmd.clone.sunk | while | flops 221341216 | bytes 8103871 | solution.py:252
  51.9 4.9 %fusion.405 = f32[53,32,128]{2,0,1:T(8,128)S(1)} fusion(f32[32,128]{1,0:T(8,128)S(1)} %bitcast.614, f32[32,128]{1,0:T(8,128)S(1)} %bitcast.626, f32[32,128]{1,0:T(8,128)S(1)} %bitcast.616, f32[32,128]{1,0:T(8,128)S(1)} %bitcast.628, f32[32,128]{1,0:T(8,128)S(1)} %bitcast.612, f32[32,128]{1,0:T(8,128)S(1)} %bitcast.624, ...), kind=kOutput, calls=%fused_computation.76.clone.1 | convolution fusion | flops 173232128 | bytes 1835040 | tf_op jit(solution)/shard_map/while/body/rtb,tab->rta/dot_general | solution.py:226
  58.1 3.1 %fusion.407 = f32[96,128,128]{2,1,0:T(8,128)} fusion(f32[96,128,128]{2,1,0:T(8,128)} %get-tuple-element.1994, s32[]{:T(128)S(6)} %select_n.1045, f32[32,128]{1,0:T(8,128)S(1)} %bitcast.615, f32[32,128]{1,0:T(8,128)S(1)} %bitcast.627, f32[32,128]{1,0:T(8,128)S(1)} %bitcast.617, f32[32,128]{1,0:T(8,128)S(1)} %bitcast.629, f32[32,128]{1,0:T(8,128)S(1)} %bitcast.613, ...), kind=kLoop, calls=%fused_computation.74.clone.1 | loop fusion | flops 6291456 | bytes 2195460 | tf_op jit(solution)/shard_map/while/body/dynamic_update_slice | solution.py:249
  68.2 5.0 %while.116 = (s32[]{:T(128)}, f32[7,16,128]{2,1,0:T(8,128)S(1)}, s32[]{:T(128)}, f32[96,128,128]{2,1,0:T(8,128)}, s32[96]{0:T(128)S(1)}, /*index=5*/f32[7,16,128...) while((s32[]{:T(128)}, f32[7,16,128]{2,1,0:T(8,128)S(1)}, ...), condition=%wide.region_17.20_spmd.clone, body=%wide.region_16.19_spmd.clone.sunk | while | flops 27570468 | bytes 2790591 | solution.py:272
  69.6 3.4 %fusion.412 = f32[7,32,128]{2,0,1:T(8,128)S(1)} fusion(f32[96,128,128]{2,1,0:T(8,128)} %get-tuple-element.2049, s32[]{:T(128)S(6)} %select_n.1047, f32[32,7,128]{2,1,0:T(8,128)S(1)} %gather_fusion.6, pred[32]{0:T(512)(128)(4,1)S(1)} %get-tuple-element.1855), kind=kOutput, calls=%fused_computation.113.clone.1 | convolution fusion | flops 22048768 | bytes 2326564 | tf_op jit(solution)/shard_map/while/body/rtb,tab->rta/dot_general | solution.py:226
  76.3 20.4 %all-to-all-start.1 = ((f32[32,1,960]{2,1,0:T(1,128)}), f32[32,1,960]{2,1,0:T(1,128)S(1)}, u32[]{:S(2)}, u32[]{:S(2)}) async-start(f32[32,1,960]{2,1,0:T(1,128)} %copy.542), calls=%async_computation.1 | async-start | bytes 262144 | tf_op jit(solution)/shard_map/all_to_all | solution.py:145
  98.7 6.4 %all-to-all-done.1 = f32[32,1,960]{2,1,0:T(1,128)S(1)} async-done(((f32[32,1,960]{2,1,0:T(1,128)}), f32[32,1,960]{2,1,0:T(1,128)S(1)}, u32[]{:S(2)}, u32[]{:S(2)}) %all-to-all-start.1) | async-done | bytes 122912 | tf_op jit(solution)/shard_map/all_to_all | solution.py:145
  106.3 5.6 %while.117 = (s32[]{:T(128)}, f32[7,16,128]{2,1,0:T(8,128)S(1)}, s32[]{:T(128)}, s32[]{:T(128)}, f32[96,128,128]{2,1,0:T(8,128)}, /*index=5*/s32[96]{0:T(128)S(1...) while((s32[]{:T(128)}, f32[7,16,128]{2,1,0:T(8,128)S(1)}, ...), condition=%wide.region_20.26_spmd.clone, body=%wide.region_19.25_spmd.clone.sunk | while | flops 27570440 | bytes 2790611 | solution.py:272
  108.3 3.4 %fusion.418 = f32[7,32,128]{2,0,1:T(8,128)S(1)} fusion(f32[96,128,128]{2,1,0:T(8,128)} %get-tuple-element.2088, s32[]{:T(128)S(6)} %select_n.1049, f32[32,7,128]{2,1,0:T(8,128)S(1)} %gather_fusion.7, pred[32]{0:T(512)(128)(4,1)S(1)} %get-tuple-element.1867), kind=kOutput, calls=%fused_computation.134.clone.1 | convolution fusion | flops 22048768 | bytes 2326564 | tf_op jit(solution)/shard_map/while/body/rtb,tab->rta/dot_general | solution.py:226
  118.3 2.6 %all-to-all-start.2 = ((f32[32,1,960]{2,1,0:T(1,128)}), f32[32,1,960]{2,1,0:T(1,128)S(1)}, u32[]{:S(2)}, u32[]{:S(2)}) async-start(f32[32,1,960]{2,1,0:T(1,128)} %copy.557), calls=%async_computation.2 | async-start | bytes 262144 | tf_op jit(solution)/shard_map/all_to_all | solution.py:145
  120.9 5.0 %while.118 = (s32[]{:T(128)}, f32[7,16,128]{2,1,0:T(8,128)S(1)}, s32[]{:T(128)}, f32[96,128,128]{2,1,0:T(8,128)}, s32[96]{0:T(128)S(1)}, /*index=5*/f32[7,16,128...) while((s32[]{:T(128)}, f32[7,16,128]{2,1,0:T(8,128)S(1)}, ...), condition=%wide.region_23.29_spmd.clone, body=%wide.region_22.28_spmd.clone.sunk | while | flops 27570468 | bytes 2790591 | solution.py:272
  122.2 3.4 %fusion.424 = f32[7,32,128]{2,0,1:T(8,128)S(1)} fusion(f32[96,128,128]{2,1,0:T(8,128)} %get-tuple-element.2124, s32[]{:T(128)S(6)} %select_n.1051, f32[32,7,128]{2,1,0:T(8,128)S(1)} %gather_fusion.8, pred[32]{0:T(512)(128)(4,1)S(1)} %get-tuple-element.1878), kind=kOutput, calls=%fused_computation.155.clone.1 | convolution fusion | flops 22048768 | bytes 2326564 | tf_op jit(solution)/shard_map/while/body/rtb,tab->rta/dot_general | solution.py:226
  125.9 3.4 %all-to-all-done.2 = f32[32,1,960]{2,1,0:T(1,128)S(1)} async-done(((f32[32,1,960]{2,1,0:T(1,128)}), f32[32,1,960]{2,1,0:T(1,128)S(1)}, u32[]{:S(2)}, u32[]{:S(2)}) %all-to-all-start.2) | async-done | bytes 122912 | tf_op jit(solution)/shard_map/all_to_all | solution.py:145
  130.5 5.8 %while.119 = (s32[]{:T(128)}, f32[7,16,128]{2,1,0:T(8,128)S(1)}, s32[]{:T(128)}, s32[]{:T(128)}, f32[96,128,128]{2,1,0:T(8,128)}, /*index=5*/s32[96]{0:T(128)S(1...) while((s32[]{:T(128)}, f32[7,16,128]{2,1,0:T(8,128)S(1)}, ...), condition=%wide.region_26.32_spmd.clone, body=%wide.region_25.31_spmd.clone.sunk | while | flops 27570440 | bytes 2790611 | solution.py:272
  132.7 3.4 %fusion.430 = f32[7,32,128]{2,0,1:T(8,128)S(1)} fusion(f32[96,128,128]{2,1,0:T(8,128)} %get-tuple-element.2163, s32[]{:T(128)S(6)} %select_n.1053, f32[32,7,128]{2,1,0:T(8,128)S(1)} %gather_fusion.9, pred[32]{0:T(512)(128)(4,1)S(1)} %get-tuple-element.1890), kind=kOutput, calls=%fused_computation.176.clone.1 | convolution fusion | flops 22048768 | bytes 2326564 | tf_op jit(solution)/shard_map/while/body/rtb,tab->rta/dot_general | solution.py:226
  142.7 5.5 %all-to-all-start.3 = ((f32[32,1,960]{2,1,0:T(1,128)}), f32[32,1,960]{2,1,0:T(1,128)S(1)}, u32[]{:S(2)}, u32[]{:S(2)}) async-start(f32[32,1,960]{2,1,0:T(1,128)} %copy.572), calls=%async_computation.3 | async-start | bytes 262144 | tf_op jit(solution)/shard_map/all_to_all | solution.py:145
  148.3 5.0 %while.120 = (s32[]{:T(128)}, f32[7,16,128]{2,1,0:T(8,128)S(1)}, s32[]{:T(128)}, f32[96,128,128]{2,1,0:T(8,128)}, s32[96]{0:T(128)S(1)}, /*index=5*/f32[7,16,128...) while((s32[]{:T(128)}, f32[7,16,128]{2,1,0:T(8,128)S(1)}, ...), condition=%wide.region_29.35_spmd.clone, body=%wide.region_28.34_spmd.clone.sunk | while | flops 27570468 | bytes 2790591 | solution.py:272
  149.6 3.4 %fusion.436 = f32[7,32,128]{2,0,1:T(8,128)S(1)} fusion(f32[96,128,128]{2,1,0:T(8,128)} %get-tuple-element.2199, s32[]{:T(128)S(6)} %select_n.1055, f32[32,7,128]{2,1,0:T(8,128)S(1)} %gather_fusion.10, pred[32]{0:T(512)(128)(4,1)S(1)} %get-tuple-element.1901), kind=kOutput, calls=%fused_computation.197.clone.1 | convolution fusion | flops 22048768 | bytes 2326564 | tf_op jit(solution)/shard_map/while/body/rtb,tab->rta/dot_general | solution.py:226
  153.2 3.4 %all-to-all-done.3 = f32[32,1,960]{2,1,0:T(1,128)S(1)} async-done(((f32[32,1,960]{2,1,0:T(1,128)}), f32[32,1,960]{2,1,0:T(1,128)S(1)}, u32[]{:S(2)}, u32[]{:S(2)}) %all-to-all-start.3) | async-done | bytes 122912 | tf_op jit(solution)/shard_map/all_to_all | solution.py:145
  157.8 5.6 %while.121 = (s32[]{:T(128)}, f32[7,16,128]{2,1,0:T(8,128)S(1)}, s32[]{:T(128)}, s32[]{:T(128)}, f32[96,128,128]{2,1,0:T(8,128)}, /*index=5*/s32[96]{0:T(128)S(1...) while((s32[]{:T(128)}, f32[7,16,128]{2,1,0:T(8,128)S(1)}, ...), condition=%wide.region_32.38_spmd.clone, body=%wide.region_31.37_spmd.clone.sunk | while | flops 27570440 | bytes 2790611 | solution.py:272
  159.8 3.4 %fusion.442 = f32[7,32,128]{2,0,1:T(8,128)S(1)} fusion(f32[96,128,128]{2,1,0:T(8,128)} %get-tuple-element.2238, s32[]{:T(128)S(6)} %select_n.1057, f32[32,7,128]{2,1,0:T(8,128)S(1)} %gather_fusion.11, pred[32]{0:T(512)(128)(4,1)S(1)} %get-tuple-element.1913), kind=kOutput, calls=%fused_computation.218.clone.1 | convolution fusion | flops 22048768 | bytes 2326564 | tf_op jit(solution)/shard_map/while/body/rtb,tab->rta/dot_general | solution.py:226
  169.8 5.6 %all-to-all-start.4 = ((f32[32,1,960]{2,1,0:T(1,128)}), f32[32,1,960]{2,1,0:T(1,128)S(1)}, u32[]{:S(2)}, u32[]{:S(2)}) async-start(f32[32,1,960]{2,1,0:T(1,128)} %copy.587), calls=%async_computation.4 | async-start | bytes 262144 | tf_op jit(solution)/shard_map/all_to_all | solution.py:145
  175.4 5.0 %while.122 = (s32[]{:T(128)}, f32[7,16,128]{2,1,0:T(8,128)S(1)}, s32[]{:T(128)}, f32[96,128,128]{2,1,0:T(8,128)}, s32[96]{0:T(128)S(1)}, /*index=5*/f32[7,16,128...) while((s32[]{:T(128)}, f32[7,16,128]{2,1,0:T(8,128)S(1)}, ...), condition=%wide.region_35.41_spmd.clone, body=%wide.region_34.40_spmd.clone.sunk | while | flops 27570468 | bytes 2790591 | solution.py:272
  176.8 3.4 %fusion.448 = f32[7,32,128]{2,0,1:T(8,128)S(1)} fusion(f32[96,128,128]{2,1,0:T(8,128)} %get-tuple-element.2274, s32[]{:T(128)S(6)} %select_n.1059, f32[32,7,128]{2,1,0:T(8,128)S(1)} %gather_fusion.12, pred[32]{0:T(512)(128)(4,1)S(1)} %get-tuple-element.1924), kind=kOutput, calls=%fused_computation.239.clone.1 | convolution fusion | flops 22048768 | bytes 2326564 | tf_op jit(solution)/shard_map/while/body/rtb,tab->rta/dot_general | solution.py:226
  180.4 3.4 %all-to-all-done.4 = f32[32,1,960]{2,1,0:T(1,128)S(1)} async-done(((f32[32,1,960]{2,1,0:T(1,128)}), f32[32,1,960]{2,1,0:T(1,128)S(1)}, u32[]{:S(2)}, u32[]{:S(2)}) %all-to-all-start.4) | async-done | bytes 122912 | tf_op jit(solution)/shard_map/all_to_all | solution.py:145
  185.0 5.6 %while.123 = (s32[]{:T(128)}, f32[7,16,128]{2,1,0:T(8,128)S(1)}, s32[]{:T(128)}, s32[]{:T(128)}, f32[96,128,128]{2,1,0:T(8,128)}, /*index=5*/s32[96]{0:T(128)S(1...) while((s32[]{:T(128)}, f32[7,16,128]{2,1,0:T(8,128)S(1)}, ...), condition=%wide.region_38.44_spmd.clone, body=%wide.region_37.43_spmd.clone.sunk | while | flops 27570440 | bytes 2790611 | solution.py:272
  187.0 3.4 %fusion.454 = f32[7,32,128]{2,0,1:T(8,128)S(1)} fusion(f32[96,128,128]{2,1,0:T(8,128)} %get-tuple-element.2313, s32[]{:T(128)S(6)} %select_n.1061, f32[32,7,128]{2,1,0:T(8,128)S(1)} %gather_fusion.13, pred[32]{0:T(512)(128)(4,1)S(1)} %get-tuple-element.1936), kind=kOutput, calls=%fused_computation.260.clone.1 | convolution fusion | flops 22048768 | bytes 2326564 | tf_op jit(solution)/shard_map/while/body/rtb,tab->rta/dot_general | solution.py:226
  (502 shorter events, 74.8 us)
Async XLA Ops:
  0.6 9.1 %copy-start = (s32[9]{0:T(128)S(1)}, s32[9]{0:T(128)}, u32[]{:S(2)}) copy-start(s32[9]{0:T(128)} %constant.544.clone) | copy-start | bytes 112
  5.0 5.5 %copy-start.7 = (pred[320]{0:T(512)(128)(4,1)S(1)}, pred[320]{0:T(512)(128)(4,1)}, u32[]{:S(2)}) copy-start(pred[320]{0:T(512)(128)(4,1)} %constant.516.clone.1) | copy-start | bytes 964
  13.3 10.3 %copy-start.8 = (s32[64]{0:T(128)S(1)}, s32[64]{0:T(128)}, u32[]{:S(2)}) copy-start(s32[64]{0:T(128)} %param.55) | copy-start | bytes 772
  13.4 11.6 %copy-start.2 = (f32[3,2048]{1,0:T(4,128)S(1)}, f32[3,2048]{1,0:T(4,128)}, u32[]{:S(2)}) copy-start(f32[3,2048]{1,0:T(4,128)} %param.49) | copy-start | bytes 73732
  13.4 11.9 %copy-start.1 = (f32[3,2048]{1,0:T(4,128)S(1)}, f32[3,2048]{1,0:T(4,128)}, u32[]{:S(2)}) copy-start(f32[3,2048]{1,0:T(4,128)} %param.46) | copy-start | bytes 73732
  14.1 13.9 %copy-start.9 = (s32[64]{0:T(128)S(1)}, s32[64]{0:T(128)}, u32[]{:S(2)}) copy-start(s32[64]{0:T(128)} %param.54) | copy-start | bytes 772
  14.1 14.1 %copy-start.3 = (f32[2048]{0:T(1024)S(1)}, f32[2048]{0:T(1024)}, u32[]{:S(2)}) copy-start(f32[2048]{0:T(1024)} %param.47) | copy-start | bytes 24580
  14.1 14.2 %copy-start.4 = (f32[2048]{0:T(1024)S(1)}, f32[2048]{0:T(1024)}, u32[]{:S(2)}) copy-start(f32[2048]{0:T(1024)} %param.50) | copy-start | bytes 24580
  15.7 30.0 %all-to-all-start = ((f32[32,1,5120]{2,1,0:T(1,128)}), f32[32,1,5120]{2,1,0:T(1,128)S(1)}, u32[]{:S(2)}, u32[]{:S(2)}) async-start(f32[32,1,5120]{2,1,0:T(1,128)} %copy.522), calls=%async_computation | async-start | bytes 1310720 | tf_op jit(solution)/shard_map/all_to_all | solution.py:145
  61.2 3.1 %copy-start.6 = (f32[3,2048]{1,0:T(4,128)S(1)}, f32[3,2048]{1,0:T(4,128)}, u32[]{:S(2)}) copy-start(f32[3,2048]{1,0:T(4,128)} %param.48) | copy-start | bytes 73732
  64.2 3.9 %copy-start.5 = (f32[2048]{0:T(1024)S(1)}, f32[2048]{0:T(1024)}, u32[]{:S(2)}) copy-start(f32[2048]{0:T(1024)} %param.51) | copy-start | bytes 24580
  76.3 28.8 %all-to-all-start.1 = ((f32[32,1,960]{2,1,0:T(1,128)}), f32[32,1,960]{2,1,0:T(1,128)S(1)}, u32[]{:S(2)}, u32[]{:S(2)}) async-start(f32[32,1,960]{2,1,0:T(1,128)} %copy.542), calls=%async_computation.1 | async-start | bytes 262144 | tf_op jit(solution)/shard_map/all_to_all | solution.py:145
  118.3 11.0 %all-to-all-start.2 = ((f32[32,1,960]{2,1,0:T(1,128)}), f32[32,1,960]{2,1,0:T(1,128)S(1)}, u32[]{:S(2)}, u32[]{:S(2)}) async-start(f32[32,1,960]{2,1,0:T(1,128)} %copy.557), calls=%async_computation.2 | async-start | bytes 262144 | tf_op jit(solution)/shard_map/all_to_all | solution.py:145
  142.7 13.9 %all-to-all-start.3 = ((f32[32,1,960]{2,1,0:T(1,128)}), f32[32,1,960]{2,1,0:T(1,128)S(1)}, u32[]{:S(2)}, u32[]{:S(2)}) async-start(f32[32,1,960]{2,1,0:T(1,128)} %copy.572), calls=%async_computation.3 | async-start | bytes 262144 | tf_op jit(solution)/shard_map/all_to_all | solution.py:145
  169.8 14.0 %all-to-all-start.4 = ((f32[32,1,960]{2,1,0:T(1,128)}), f32[32,1,960]{2,1,0:T(1,128)S(1)}, u32[]{:S(2)}, u32[]{:S(2)}) async-start(f32[32,1,960]{2,1,0:T(1,128)} %copy.587), calls=%async_computation.4 | async-start | bytes 262144 | tf_op jit(solution)/shard_map/all_to_all | solution.py:145

commit v3 on v0

--- a/solution.py
+++ b/solution.py
@@ -210,6 +210,7 @@
     pad = jnp.zeros((batch,), jnp.int32)
     list_i = jnp.concatenate([jnp.sum(jnp.where(place, tile_i[None, :], 0), axis=1), pad])
     list_j = jnp.concatenate([jnp.sum(jnp.where(place, tile_j[None, :], 0), axis=1), pad])
+    split = first_n // batch * batch
 
     def batch_lists(offset, stop, clip):
         near_ids = lax.dynamic_slice_in_dim(list_i, offset, batch, 0)
@@ -251,9 +252,9 @@
         return lax.fori_loop(0, (stop - start + batch - 1) // batch, step, carry)
 
     acc_start = jnp.zeros((nrow, nblocks, TILE), jnp.float32)
-    stored_start = jnp.zeros((tiles_total + batch, TILE, TILE), jnp.float32)
-    carry = hydro_pass(0, first_n, pos_local, q_local_blocks, (acc_start, stored_start), True)
-    acc, stored = hydro_pass(first_n, count, pos_blocks, q_blocks, carry, False)
+    stored_start = jnp.zeros((tiles_total, TILE, TILE), jnp.float32)
+    carry = hydro_pass(0, split, pos_local, q_local_blocks, (acc_start, stored_start), True)
+    acc, stored = hydro_pass(split, count, pos_blocks, q_blocks, carry, False)
     acc = acc.reshape(nrow, nlocal)
     rate, count_n = hydro_rate(acc, qlocal, ch)
     density_new = density + dt * rate[0]
@@ -274,7 +275,7 @@
         eta = ohmic + fac * jnp.sum(bfl * bfl, axis=0)
         q_near = jnp.concatenate([bfl, eta[None] * bfl, eta[None]], axis=0)
         acc_diff = diff_pass(
-            0, first_n, q_near.reshape(7, nblocks, TILE), jnp.zeros((7, nblocks, TILE), jnp.float32), True
+            0, split, q_near.reshape(7, nblocks, TILE), jnp.zeros((7, nblocks, TILE), jnp.float32), True
         )
         ghost_b = spread_ghosts(bfl, ghost_index)
         ghost_eta = ghosts[13] + ghosts[14] * jnp.sum(ghost_b * ghost_b, axis=0)
@@ -282,7 +283,7 @@
         eta_ext = extend(eta[None], ghost_eta[None])[0]
         qdiff = jnp.concatenate([b_ext, eta_ext[None] * b_ext, eta_ext[None]], axis=0)
         diff_blocks = qdiff.reshape(7, EXT_BLOCKS, TILE)
-        acc_diff = diff_pass(first_n, count, diff_blocks, acc_diff, False)
+        acc_diff = diff_pass(split, count, diff_blocks, acc_diff, False)
         return diffusion_rate(acc_diff.reshape(7, nlocal), bfl, eta, count_n)
 
     first, rows = rkl_table(SECTIONS)

time: 191 us -> 164 us (0.86)
  waiting for transfers between devices: 14.8 us -> 39.9 us
  matrix products: 39.3 us -> 19.7 us
  starting transfers between devices: 42.7 us -> 24.2 us
  other arithmetic: 33 us -> 26.2 us
  local copies, waits for them, and re-layouts: 46.1 us -> 41.3 us
  loops' own time: 4.18 us -> 0.83 us
    all_to_all x5, waiting for transfers between devices: 14.8 us -> 39.9 us  [spread_ghosts(): incoming = lax.all_to_all(outgoing, ('gx', 'gy'), 0, 0, tiled=True)]
    all_to_all x5, starting transfers between devices: 42.7 us -> 24.2 us  [spread_ghosts(): incoming = lax.all_to_all(outgoing, ('gx', 'gy'), 0, 0, tiled=True)]
    dot_general x10 -> x5, matrix products: 36.7 us -> 18.3 us  [fold_batch(): jnp.einsum('rtb,tab->rta', qsel, weight, precision=lax.Precision.HIGH, pr...]
    dynamic_update_slice x2 -> x1, other arithmetic: 6.13 us -> 3.08 us  [step(): stored = lax.dynamic_update_slice_in_dim(stored, weight, offset, 0)]
    gather x10 -> x5, local copies, waits for them, and re-layouts: 5.9 us -> 2.95 us  [fold_batch(): qsel = jnp.take(blocks, far_ids, axis=1)]
    and x8 -> x4, other arithmetic: 5.77 us -> 2.91 us  [fold_batch(): qsel = jnp.take(blocks, far_ids, axis=1)]
    another operation x8, loops' own time: 3.14 us -> 0.52 us  [diff_pass(): return lax.fori_loop(0, (stop - start + batch - 1) // batch, step, acc)]
  transfers between devices with their start and end apart: 5 -> 5, of which waited for: 4 -> 5; matrix products, arithmetic and copies ran while one was open for 22% -> 6% of each run, Pallas kernels for 0% -> 0%
where the time goes in v3:
time: 164 us; the launch traced here: 162 us
  local copies, waits for them, and re-layouts  41.3 us (25%)
  waiting for transfers between devices  39.9 us (24%)
  other arithmetic  26.2 us (16%)
  starting transfers between devices  24.2 us (15%)
  matrix products  19.7 us (12%)
  between operations  9.92 us (6%)
    all_to_all x5, waiting for transfers between devices, spread_ghosts(): incoming = lax.all_to_all(outgoing, ('gx', 'gy'), 0, 0, tiled=True)  39.9 us
    all_to_all x5, starting transfers between devices, spread_ghosts(): incoming = lax.all_to_all(outgoing, ('gx', 'gy'), 0, 0, tiled=True)  24.2 us
    dot_general x5, matrix products, fold_batch(): jnp.einsum('rtb,tab->rta', qsel, weight, precision=lax.Precision.HIGH, pr...  18.3 us
    gather x5, local copies, waits for them, and re-layouts, spread_ghosts(): sent = jnp.take(rows, ghost_index, axis=1)  12 us
    another operation x68, local copies, waits for them, and re-layouts, spread_ghosts(): segments = jnp.stack(segments)  4.7 us
    select_n x6, other arithmetic, spread_ghosts(): outgoing = jnp.take(segments, pick, axis=0)  3.32 us
    gather x5, local copies, waits for them, and re-layouts, spread_ghosts(): outgoing = jnp.take(segments, pick, axis=0)  3.32 us
  transfers between devices with their start and end apart: 5, of which 5 were waited for; matrix products, arithmetic and copies ran while one was open for 6% of the time, Pallas kernels for 0%

profile of v3, /device:TPU:0, one launch (start us, length us, event | category | flops | bytes accessed | tf_op | source)
XLA Modules:
  0.0 161.9 jit_solution(10933502069735974622)
XLA Ops:
  3.6 1.3 fusion.315
  5.0 1.7 %concatenate.177 = f32[15,2048]{1,0:T(8,128)S(1)} concatenate(f32[3,2048]{1,0:T(4,128)} %param.46, f32[1,2048]{1,0:T(1,128)S(1)} %broadcast_in_dim_broadcast_in_dim.5, f32[1,2048]{1,0:T(1,128)} %bitcast.768, f32[3,2048]{1,0:T(4,128)S(1)} %get-tuple-element.1093, f32[3,2048]{1,0:T(4,128)} %param.49, f32[1,2048]{1,0:T(1,128)} %bitcast.774, f32[1,2048]{1,0:T(1,128)S(1)} %bitcast.783, ...), dimensions={0} | concatenate | bytes 245760 | tf_op jit(solution)/shard_map/concatenate | solution.py:186
  7.0 2.4 %gather_fusion.15 = f32[1088,15]{1,0:T(8,128)S(1)} fusion(f32[15,2048]{0,1:T(8,128)S(1)} %copy.406, s32[2048]{0:T(1024)S(1)} %pad_clamp_fusion.12), kind=kCustom, calls=%fused_computation.23 | custom fusion | bytes 134912 | tf_op jit(solution)/shard_map/jit(_take)/gather | solution.py:124
  13.1 1.6 concatenate.178
  14.7 7.3 %all-to-all-start = ((f32[32,16,320]{2,1,0:T(8,128)}), f32[32,16,320]{2,1,0:T(8,128)S(1)}, u32[]{:S(2)}, u32[]{:S(2)}) async-start(f32[32,16,320]{2,1,0:T(8,128)} %concatenate.178), calls=%async_computation | async-start | bytes 1572864 | tf_op jit(solution)/shard_map/all_to_all | solution.py:145
  30.9 2.5 %broadcast_in_dim.295 = f32[64,128,128]{2,1,0:T(8,128)} broadcast(f32[]{:T(128)} %constant.507.clone.1), dimensions={} | broadcast | bytes 4194308 | tf_op jit(solution)/shard_map/broadcast_in_dim | solution.py:255
  33.6 1.6 concatenate.191
  35.8 5.7 %all-to-all-done = f32[32,16,320]{2,1,0:T(8,128)S(1)} async-done(((f32[32,16,320]{2,1,0:T(8,128)}), f32[32,16,320]{2,1,0:T(8,128)S(1)}, u32[]{:S(2)}, u32[]{:S(2)}) %all-to-all-start) | async-done | bytes 655392 | tf_op jit(solution)/shard_map/all_to_all | solution.py:145
  45.4 11.7 %while.115 = (s32[]{:T(128)}, f32[53,16,128]{2,1,0:T(8,128)S(1)}, f32[64,128,128]{2,1,0:T(8,128)}, s32[]{:T(128)}, s32[]{:T(128)}, /*index=5*/s32[96]{0:T(128)S(...) while((s32[]{:T(128)}, f32[53,16,128]{2,1,0:T(8,128)S(1)}, ...), condition=%wide.region_14.16_spmd.clone, body=%wide.region_13.15_spmd.clone.sunk | while | flops 221341216 | bytes 8103896 | solution.py:252
  47.1 3.1 %fusion.415 = f32[64,128,128]{2,1,0:T(8,128)} fusion(f32[64,128,128]{2,1,0:T(8,128)} %get-tuple-element.2000, s32[]{:T(128)S(6)} %select_n.1071, f32[32,128]{1,0:T(8,128)S(1)} %bitcast.745, f32[32,128]{1,0:T(8,128)S(1)} %bitcast.757, f32[32,128]{1,0:T(8,128)S(1)} %bitcast.747, f32[32,128]{1,0:T(8,128)S(1)} %bitcast.759, f32[32,128]{1,0:T(8,128)S(1)} %bitcast.743, ...), kind=kLoop, calls=%fused_computation.74.clone.1 | loop fusion | flops 6291456 | bytes 2195460 | tf_op jit(solution)/shard_map/while/body/dynamic_update_slice | solution.py:249
  50.8 4.9 %fusion.413 = f32[53,32,128]{2,0,1:T(8,128)S(1)} fusion(f32[32,128]{1,0:T(8,128)S(1)} %bitcast.746, f32[32,128]{1,0:T(8,128)S(1)} %bitcast.758, f32[32,128]{1,0:T(8,128)S(1)} %bitcast.748, f32[32,128]{1,0:T(8,128)S(1)} %bitcast.760, f32[32,128]{1,0:T(8,128)S(1)} %bitcast.744, f32[32,128]{1,0:T(8,128)S(1)} %bitcast.756, ...), kind=kOutput, calls=%fused_computation.76.clone.1 | convolution fusion | flops 173232128 | bytes 1835040 | tf_op jit(solution)/shard_map/while/body/rtb,tab->rta/dot_general | solution.py:226
  59.8 1.4 multiply_reduce_fusion.3
  61.6 2.4 %gather_fusion.17 = f32[1088,3]{1,0:T(8,128)S(1)} fusion(f32[3,2048]{0,1:T(8,128)S(1)} %copy.425, s32[2048]{0:T(1024)S(1)} %pad_clamp_fusion.12), kind=kCustom, calls=%fused_computation.2.clone | custom fusion | bytes 30464 | tf_op jit(solution)/shard_map/jit(_take)/gather | solution.py:124
  67.0 9.1 %all-to-all-start.1 = ((f32[32,3,320]{2,1,0:T(4,128)}), f32[32,3,320]{2,1,0:T(4,128)S(1)}, u32[]{:S(2)}, u32[]{:S(2)}) async-start(f32[32,3,320]{2,1,0:T(4,128)} %broadcast_select_fusion.4), calls=%async_computation.1 | async-start | bytes 393216 | tf_op jit(solution)/shard_map/all_to_all | solution.py:145
  78.9 6.6 %all-to-all-done.1 = f32[32,3,320]{2,1,0:T(4,128)S(1)} async-done(((f32[32,3,320]{2,1,0:T(4,128)}), f32[32,3,320]{2,1,0:T(4,128)S(1)}, u32[]{:S(2)}, u32[]{:S(2)}) %all-to-all-start.1) | async-done | bytes 122912 | tf_op jit(solution)/shard_map/all_to_all | solution.py:145
  86.0 5.0 %while.117 = (s32[]{:T(128)}, f32[7,16,128]{2,1,0:T(8,128)S(1)}, s32[]{:T(128)}, s32[]{:T(128)}, f32[64,128,128]{2,1,0:T(8,128)}, /*index=5*/s32[96]{0:T(128)S(1...) while((s32[]{:T(128)}, f32[7,16,128]{2,1,0:T(8,128)S(1)}, ...), condition=%wide.region_20.26_spmd.clone, body=%wide.region_19.25_spmd.clone.sunk | while | flops 27570440 | bytes 2790636 | solution.py:272
  87.4 3.4 %fusion.426 = f32[7,32,128]{2,0,1:T(8,128)S(1)} fusion(f32[64,128,128]{2,1,0:T(8,128)} %get-tuple-element.2101, s32[]{:T(128)S(6)} %select_n.1076, f32[32,7,128]{2,1,0:T(8,128)S(1)} %gather_fusion.7, pred[32]{0:T(512)(128)(4,1)S(1)} %get-tuple-element.1869), kind=kOutput, calls=%fused_computation.134.clone.1 | convolution fusion | flops 22048768 | bytes 2326564 | tf_op jit(solution)/shard_map/while/body/rtb,tab->rta/dot_general | solution.py:226
  91.5 2.4 %gather_fusion.19 = f32[1088,3]{1,0:T(8,128)S(1)} fusion(f32[3,2048]{0,1:T(8,128)S(1)} %copy.439, s32[2048]{0:T(1024)S(1)} %pad_clamp_fusion.12), kind=kCustom, calls=%fused_computation.13.clone | custom fusion | bytes 30464 | tf_op jit(solution)/shard_map/jit(_take)/gather | solution.py:124
  96.9 2.6 %all-to-all-start.2 = ((f32[32,3,320]{2,1,0:T(4,128)}), f32[32,3,320]{2,1,0:T(4,128)S(1)}, u32[]{:S(2)}, u32[]{:S(2)}) async-start(f32[32,3,320]{2,1,0:T(4,128)} %broadcast_select_fusion.3), calls=%async_computation.2 | async-start | bytes 393216 | tf_op jit(solution)/shard_map/all_to_all | solution.py:145
  99.5 9.2 %all-to-all-done.2 = f32[32,3,320]{2,1,0:T(4,128)S(1)} async-done(((f32[32,3,320]{2,1,0:T(4,128)}), f32[32,3,320]{2,1,0:T(4,128)S(1)}, u32[]{:S(2)}, u32[]{:S(2)}) %all-to-all-start.2) | async-done | bytes 122912 | tf_op jit(solution)/shard_map/all_to_all | solution.py:145
  109.3 5.2 %while.119 = (s32[]{:T(128)}, f32[7,16,128]{2,1,0:T(8,128)S(1)}, s32[]{:T(128)}, s32[]{:T(128)}, f32[64,128,128]{2,1,0:T(8,128)}, /*index=5*/s32[96]{0:T(128)S(1...) while((s32[]{:T(128)}, f32[7,16,128]{2,1,0:T(8,128)S(1)}, ...), condition=%wide.region_26.32_spmd.clone, body=%wide.region_25.31_spmd.clone.sunk | while | flops 27570440 | bytes 2790636 | solution.py:272
  110.7 3.4 %fusion.438 = f32[7,32,128]{2,0,1:T(8,128)S(1)} fusion(f32[64,128,128]{2,1,0:T(8,128)} %get-tuple-element.2182, s32[]{:T(128)S(6)} %select_n.1082, f32[32,7,128]{2,1,0:T(8,128)S(1)} %gather_fusion.9, pred[32]{0:T(512)(128)(4,1)S(1)} %get-tuple-element.1892), kind=kOutput, calls=%fused_computation.176.clone.1 | convolution fusion | flops 22048768 | bytes 2326564 | tf_op jit(solution)/shard_map/while/body/rtb,tab->rta/dot_general | solution.py:226
  115.0 2.4 %gather_fusion.21 = f32[1088,3]{1,0:T(8,128)S(1)} fusion(f32[3,2048]{0,1:T(8,128)S(1)} %copy.453, s32[2048]{0:T(1024)S(1)} %pad_clamp_fusion.12), kind=kCustom, calls=%fused_computation.14.clone | custom fusion | bytes 30464 | tf_op jit(solution)/shard_map/jit(_take)/gather | solution.py:124
  120.4 2.6 %all-to-all-start.3 = ((f32[32,3,320]{2,1,0:T(4,128)}), f32[32,3,320]{2,1,0:T(4,128)S(1)}, u32[]{:S(2)}, u32[]{:S(2)}) async-start(f32[32,3,320]{2,1,0:T(4,128)} %broadcast_select_fusion.2), calls=%async_computation.3 | async-start | bytes 393216 | tf_op jit(solution)/shard_map/all_to_all | solution.py:145
  123.1 9.2 %all-to-all-done.3 = f32[32,3,320]{2,1,0:T(4,128)S(1)} async-done(((f32[32,3,320]{2,1,0:T(4,128)}), f32[32,3,320]{2,1,0:T(4,128)S(1)}, u32[]{:S(2)}, u32[]{:S(2)}) %all-to-all-start.3) | async-done | bytes 122912 | tf_op jit(solution)/shard_map/all_to_all | solution.py:145
  132.9 5.0 %while.121 = (s32[]{:T(128)}, f32[7,16,128]{2,1,0:T(8,128)S(1)}, s32[]{:T(128)}, s32[]{:T(128)}, f32[64,128,128]{2,1,0:T(8,128)}, /*index=5*/s32[96]{0:T(128)S(1...) while((s32[]{:T(128)}, f32[7,16,128]{2,1,0:T(8,128)S(1)}, ...), condition=%wide.region_32.38_spmd.clone, body=%wide.region_31.37_spmd.clone.sunk | while | flops 27570440 | bytes 2790636 | solution.py:272
  134.2 3.4 %fusion.450 = f32[7,32,128]{2,0,1:T(8,128)S(1)} fusion(f32[64,128,128]{2,1,0:T(8,128)} %get-tuple-element.2263, s32[]{:T(128)S(6)} %select_n.1088, f32[32,7,128]{2,1,0:T(8,128)S(1)} %gather_fusion.11, pred[32]{0:T(512)(128)(4,1)S(1)} %get-tuple-element.1915), kind=kOutput, calls=%fused_computation.218.clone.1 | convolution fusion | flops 22048768 | bytes 2326564 | tf_op jit(solution)/shard_map/while/body/rtb,tab->rta/dot_general | solution.py:226
  138.3 2.4 %gather_fusion.23 = f32[1088,3]{1,0:T(8,128)S(1)} fusion(f32[3,2048]{0,1:T(8,128)S(1)} %copy.467, s32[2048]{0:T(1024)S(1)} %pad_clamp_fusion.12), kind=kCustom, calls=%fused_computation.15.clone | custom fusion | bytes 30464 | tf_op jit(solution)/shard_map/jit(_take)/gather | solution.py:124
  143.7 2.6 %all-to-all-start.4 = ((f32[32,3,320]{2,1,0:T(4,128)}), f32[32,3,320]{2,1,0:T(4,128)S(1)}, u32[]{:S(2)}, u32[]{:S(2)}) async-start(f32[32,3,320]{2,1,0:T(4,128)} %broadcast_select_fusion.1), calls=%async_computation.4 | async-start | bytes 393216 | tf_op jit(solution)/shard_map/all_to_all | solution.py:145
  146.4 9.2 %all-to-all-done.4 = f32[32,3,320]{2,1,0:T(4,128)S(1)} async-done(((f32[32,3,320]{2,1,0:T(4,128)}), f32[32,3,320]{2,1,0:T(4,128)S(1)}, u32[]{:S(2)}, u32[]{:S(2)}) %all-to-all-start.4) | async-done | bytes 122912 | tf_op jit(solution)/shard_map/all_to_all | solution.py:145
  156.2 5.0 %while.123 = (s32[]{:T(128)}, f32[7,16,128]{2,1,0:T(8,128)S(1)}, s32[]{:T(128)}, s32[]{:T(128)}, f32[64,128,128]{2,1,0:T(8,128)}, /*index=5*/s32[96]{0:T(128)S(1...) while((s32[]{:T(128)}, f32[7,16,128]{2,1,0:T(8,128)S(1)}, ...), condition=%wide.region_38.44_spmd.clone, body=%wide.region_37.43_spmd.clone.sunk | while | flops 27570440 | bytes 2790636 | solution.py:272
  157.5 3.4 %fusion.462 = f32[7,32,128]{2,0,1:T(8,128)S(1)} fusion(f32[64,128,128]{2,1,0:T(8,128)} %get-tuple-element.2344, s32[]{:T(128)S(6)} %select_n.1094, f32[32,7,128]{2,1,0:T(8,128)S(1)} %gather_fusion.13, pred[32]{0:T(512)(128)(4,1)S(1)} %get-tuple-element.1938), kind=kOutput, calls=%fused_computation.260.clone.1 | convolution fusion | flops 22048768 | bytes 2326564 | tf_op jit(solution)/shard_map/while/body/rtb,tab->rta/dot_general | solution.py:226
  (447 shorter events, 43.7 us)
Async XLA Ops:
  0.6 9.1 %copy-start = (s32[9]{0:T(128)S(1)}, s32[9]{0:T(128)}, u32[]{:S(2)}) copy-start(s32[9]{0:T(128)} %constant.531.clone) | copy-start | bytes 112
  5.0 6.1 %copy-start.24 = (pred[320]{0:T(512)(128)(4,1)S(1)}, pred[320]{0:T(512)(128)(4,1)}, u32[]{:S(2)}) copy-start(pred[320]{0:T(512)(128)(4,1)} %constant.503.clone.1) | copy-start | bytes 964
  11.1 1.8 %copy-start.22 = (pred[32]{0:T(512)(128)(4,1)}, pred[32]{0:T(512)(128)(4,1)S(1)}, u32[]{:S(2)}) copy-start(pred[32]{0:T(512)(128)(4,1)S(1)} %get-tuple-element.1078) | copy-start | bytes 100
  12.9 9.1 %copy-start.2 = (f32[3,2048]{1,0:T(4,128)S(1)}, f32[3,2048]{1,0:T(4,128)}, u32[]{:S(2)}) copy-start(f32[3,2048]{1,0:T(4,128)} %param.49) | copy-start | bytes 73732
  13.0 9.3 %copy-start.1 = (f32[3,2048]{1,0:T(4,128)S(1)}, f32[3,2048]{1,0:T(4,128)}, u32[]{:S(2)}) copy-start(f32[3,2048]{1,0:T(4,128)} %param.46) | copy-start | bytes 73732
  13.1 10.0 %copy-start.28 = (s32[64]{0:T(128)S(1)}, s32[64]{0:T(128)}, u32[]{:S(2)}) copy-start(s32[64]{0:T(128)} %param.55) | copy-start | bytes 772
  13.1 13.3 %copy-start.3 = (f32[2048]{0:T(1024)S(1)}, f32[2048]{0:T(1024)}, u32[]{:S(2)}) copy-start(f32[2048]{0:T(1024)} %param.47) | copy-start | bytes 24580
  13.1 13.4 %copy-start.4 = (f32[2048]{0:T(1024)S(1)}, f32[2048]{0:T(1024)}, u32[]{:S(2)}) copy-start(f32[2048]{0:T(1024)} %param.50) | copy-start | bytes 24580
  14.7 26.8 %all-to-all-start = ((f32[32,16,320]{2,1,0:T(8,128)}), f32[32,16,320]{2,1,0:T(8,128)S(1)}, u32[]{:S(2)}, u32[]{:S(2)}) async-start(f32[32,16,320]{2,1,0:T(8,128)} %concatenate.178), calls=%async_computation | async-start | bytes 1572864 | tf_op jit(solution)/shard_map/all_to_all | solution.py:145
  22.3 11.2 %copy-start.14 = (f32[1,2048]{1,0:T(1,128)}, f32[1,2048]{1,0:T(1,128)S(1)}, u32[]{:S(2)}) copy-start(f32[1,2048]{1,0:T(1,128)S(1)} %get-tuple-element.1273) | copy-start | bytes 24580
  22.3 11.2 %copy-start.16 = (f32[1,2048]{1,0:T(1,128)}, f32[1,2048]{1,0:T(1,128)S(1)}, u32[]{:S(2)}) copy-start(f32[1,2048]{1,0:T(1,128)S(1)} %get-tuple-element.1274) | copy-start | bytes 24580
  22.3 11.2 %copy-start.18 = (f32[1,2048]{1,0:T(1,128)}, f32[1,2048]{1,0:T(1,128)S(1)}, u32[]{:S(2)}) copy-start(f32[1,2048]{1,0:T(1,128)S(1)} %get-tuple-element.1275) | copy-start | bytes 24580
  26.4 4.3 %copy-start.29 = (s32[64]{0:T(128)S(1)}, s32[64]{0:T(128)}, u32[]{:S(2)}) copy-start(s32[64]{0:T(128)} %param.54) | copy-start | bytes 772
  33.4 1.8 %copy-start.27 = (s32[32]{0:T(128)S(1)}, s32[32]{0:T(128)}, u32[]{:S(2)}) copy-start(s32[32]{0:T(128)} %get-tuple-element.1079) | copy-start | bytes 388
  33.4 8.1 %copy-start.20 = (s32[96]{0:T(128)}, s32[96]{0:T(128)S(1)}, u32[]{:S(2)}) copy-start(s32[96]{0:T(128)S(1)} %get-tuple-element.2377) | copy-start | bytes 1156
  41.6 1.5 copy-start.5
  41.6 1.5 copy-start.8
  41.6 1.5 copy-start.10
  41.6 2.4 %copy-start.12 = (f32[15,32]{1,0:T(8,128)}, f32[15,32]{1,0:T(8,128)S(1)}, u32[]{:S(2)}) copy-start(f32[15,32]{1,0:T(8,128)S(1)} %slice_select_fusion.10) | copy-start | bytes 5764
  43.8 1.5 copy-start.21
  45.3 14.2 %copy-start.15 = (f32[1,2048]{1,0:T(1,128)S(1)}, f32[1,2048]{1,0:T(1,128)}, u32[]{:S(2)}) copy-start(f32[1,2048]{1,0:T(1,128)} %copy-done.14) | copy-start | bytes 24580
  45.4 14.2 %copy-start.17 = (f32[1,2048]{1,0:T(1,128)S(1)}, f32[1,2048]{1,0:T(1,128)}, u32[]{:S(2)}) copy-start(f32[1,2048]{1,0:T(1,128)} %copy-done.16) | copy-start | bytes 24580
  45.4 14.2 %copy-start.19 = (f32[1,2048]{1,0:T(1,128)S(1)}, f32[1,2048]{1,0:T(1,128)}, u32[]{:S(2)}) copy-start(f32[1,2048]{1,0:T(1,128)} %copy-done.18) | copy-start | bytes 24580
  57.1 7.1 %copy-start.25 = (pred[320]{0:T(512)(128)(4,1)S(1)}, pred[320]{0:T(512)(128)(4,1)}, u32[]{:S(2)}) copy-start(pred[320]{0:T(512)(128)(4,1)} %constant.503.clone.1) | copy-start | bytes 964
  64.2 1.3 copy-start.26
  64.2 2.0 %copy-start.23 = (pred[32]{0:T(512)(128)(4,1)S(1)}, pred[32]{0:T(512)(128)(4,1)}, u32[]{:S(2)}) copy-start(pred[32]{0:T(512)(128)(4,1)} %copy-done.22) | copy-start | bytes 100
  64.4 11.8 %copy-start.7 = (f32[2048]{0:T(1024)S(1)}, f32[2048]{0:T(1024)}, u32[]{:S(2)}) copy-start(f32[2048]{0:T(1024)} %param.51) | copy-start | bytes 24580
  67.0 18.4 %all-to-all-start.1 = ((f32[32,3,320]{2,1,0:T(4,128)}), f32[32,3,320]{2,1,0:T(4,128)S(1)}, u32[]{:S(2)}, u32[]{:S(2)}) async-start(f32[32,3,320]{2,1,0:T(4,128)} %broadcast_select_fusion.4), calls=%async_computation.1 | async-start | bytes 393216 | tf_op jit(solution)/shard_map/all_to_all | solution.py:145
  76.2 0.7 copy-start.6
  96.9 11.9 %all-to-all-start.2 = ((f32[32,3,320]{2,1,0:T(4,128)}), f32[32,3,320]{2,1,0:T(4,128)S(1)}, u32[]{:S(2)}, u32[]{:S(2)}) async-start(f32[32,3,320]{2,1,0:T(4,128)} %broadcast_select_fusion.3), calls=%async_computation.2 | async-start | bytes 393216 | tf_op jit(solution)/shard_map/all_to_all | solution.py:145
  120.4 11.9 %all-to-all-start.3 = ((f32[32,3,320]{2,1,0:T(4,128)}), f32[32,3,320]{2,1,0:T(4,128)S(1)}, u32[]{:S(2)}, u32[]{:S(2)}) async-start(f32[32,3,320]{2,1,0:T(4,128)} %broadcast_select_fusion.2), calls=%async_computation.3 | async-start | bytes 393216 | tf_op jit(solution)/shard_map/all_to_all | solution.py:145
  143.7 11.9 %all-to-all-start.4 = ((f32[32,3,320]{2,1,0:T(4,128)}), f32[32,3,320]{2,1,0:T(4,128)S(1)}, u32[]{:S(2)}, u32[]{:S(2)}) async-start(f32[32,3,320]{2,1,0:T(4,128)} %broadcast_select_fusion.1), calls=%async_computation.4 | async-start | bytes 393216 | tf_op jit(solution)/shard_map/all_to_all | solution.py:145
  (3 other events, 2.1 us)

commit v4 on v3

--- a/solution.py
+++ b/solution.py
@@ -156,6 +156,16 @@
     return (ghosts, jnp.max(incoming[:, nrows, 0]))
 
 
+def pick_rows(array, index):
+    runs = []
+    for r in index:
+        if runs and runs[-1][1] == r:
+            runs[-1][1] = r + 1
+        else:
+            runs.append([r, r + 1])
+    return jnp.concatenate([array[a:b] for a, b in runs], axis=0)
+
+
 def extend(rows, extra):
     filler = jnp.zeros(
         (rows.shape[0], EXT_BLOCKS * TILE - rows.shape[1] - extra.shape[1]), jnp.float32
@@ -192,8 +202,14 @@
     pos_local = positions.reshape(3, nblocks, TILE)
     qext = jnp.concatenate([qlocal, flux_rows(ext[:, nlocal:])], axis=1)
     nrow = qext.shape[0]
-    q_blocks = qext.reshape(nrow, EXT_BLOCKS, TILE)
-    q_local_blocks = qlocal.reshape(nrow, nblocks, TILE)
+    twin = {}
+    for d in range(3):
+        twin[4 + 8 * d] = 46 + d
+        twin[11 + 8 * d] = 49 + d
+    keep = [r for r in range(nrow) if r not in twin]
+    source = [keep.index(twin.get(r, r)) for r in range(nrow)]
+    q_blocks = pick_rows(qext, keep).reshape(len(keep), EXT_BLOCKS, TILE)
+    q_local_blocks = pick_rows(qlocal, keep).reshape(len(keep), nblocks, TILE)
     count = tile_count[0]
     tiles_total = tile_i.shape[0]
     batch = math.gcd(32, tiles_total)
@@ -251,11 +267,11 @@
 
         return lax.fori_loop(0, (stop - start + batch - 1) // batch, step, carry)
 
-    acc_start = jnp.zeros((nrow, nblocks, TILE), jnp.float32)
+    acc_start = jnp.zeros((len(keep), nblocks, TILE), jnp.float32)
     stored_start = jnp.zeros((tiles_total, TILE, TILE), jnp.float32)
     carry = hydro_pass(0, split, pos_local, q_local_blocks, (acc_start, stored_start), True)
     acc, stored = hydro_pass(split, count, pos_blocks, q_blocks, carry, False)
-    acc = acc.reshape(nrow, nlocal)
+    acc = pick_rows(acc.reshape(len(keep), nlocal), source)
     rate, count_n = hydro_rate(acc, qlocal, ch)
     density_new = density + dt * rate[0]
     momentum_new = momentum + dt * rate[1:4]

time: 164 us -> 164 us (level)
    concatenate x0 -> x2, local copies, waits for them, and re-layouts: none -> 3.34 us  [pick_rows(): return jnp.concatenate([array[a:b] for a, b in runs], axis=0)]
  transfers between devices with their start and end apart: 5 -> 5, of which waited for: 5 -> 5; matrix products, arithmetic and copies ran while one was open for 6% -> 5% of each run, Pallas kernels for 0% -> 0%
where the time goes in v4:
time: 164 us; the launch traced here: 162 us
  local copies, waits for them, and re-layouts  42.8 us (26%)
  waiting for transfers between devices  41 us (25%)
  other arithmetic  24.9 us (15%)
  starting transfers between devices  23.4 us (14%)
  matrix products  19.2 us (12%)
  between operations  10.3 us (6%)
    all_to_all x5, waiting for transfers between devices, spread_ghosts(): incoming = lax.all_to_all(outgoing, ('gx', 'gy'), 0, 0, tiled=True)  41 us
    all_to_all x5, starting transfers between devices, spread_ghosts(): incoming = lax.all_to_all(outgoing, ('gx', 'gy'), 0, 0, tiled=True)  23.4 us
    dot_general x5, matrix products, fold_batch(): jnp.einsum('rtb,tab->rta', qsel, weight, precision=lax.Precision.HIGH, pr...  17.8 us
    gather x5, local copies, waits for them, and re-layouts, spread_ghosts(): sent = jnp.take(rows, ghost_index, axis=1)  12 us
    another operation x68, local copies, waits for them, and re-layouts, spread_ghosts(): segments = jnp.stack(segments)  4.7 us
    select_n x6, other arithmetic, spread_ghosts(): outgoing = jnp.take(segments, pick, axis=0)  3.39 us
    concatenate x2, local copies, waits for them, and re-layouts, pick_rows(): return jnp.concatenate([array[a:b] for a, b in runs], axis=0)  3.34 us
    gather x5, local copies, waits for them, and re-layouts, spread_ghosts(): outgoing = jnp.take(segments, pick, axis=0)  3.32 us
  transfers between devices with their start and end apart: 5, of which 5 were waited for; matrix products, arithmetic and copies ran while one was open for 5% of the time, Pallas kernels for 0%

profile of v4, /device:TPU:0, one launch (start us, length us, event | category | flops | bytes accessed | tf_op | source)
XLA Modules:
  0.0 162.4 jit_solution(8606748994065609136)
XLA Ops:
  3.6 1.3 fusion.313
  5.0 1.7 %concatenate.202 = f32[15,2048]{1,0:T(8,128)S(1)} concatenate(f32[3,2048]{1,0:T(4,128)} %param.46, f32[1,2048]{1,0:T(1,128)S(1)} %broadcast_in_dim_broadcast_in_dim.3, f32[1,2048]{1,0:T(1,128)} %bitcast.778, f32[3,2048]{1,0:T(4,128)S(1)} %get-tuple-element.1093, f32[3,2048]{1,0:T(4,128)} %param.49, f32[1,2048]{1,0:T(1,128)} %bitcast.783, f32[1,2048]{1,0:T(1,128)S(1)} %bitcast.792, ...), dimensions={0} | concatenate | bytes 245760 | tf_op jit(solution)/shard_map/concatenate | solution.py:196
  7.1 2.4 %gather_fusion.15 = f32[1088,15]{1,0:T(8,128)S(1)} fusion(f32[15,2048]{0,1:T(8,128)S(1)} %copy.405, s32[2048]{0:T(1024)S(1)} %pad_clamp_fusion.12), kind=kCustom, calls=%fused_computation.23 | custom fusion | bytes 134912 | tf_op jit(solution)/shard_map/jit(_take)/gather | solution.py:124
  12.6 1.6 %concatenate.203 = f32[32,16,320]{2,1,0:T(8,128)} pad(f32[32,15,320]{2,1,0:T(8,128)S(1)} %broadcast_select_fusion, f32[]{:T(128)} %get-tuple-element.1076), padding=0_0x0_1x0_0 | pad | bytes 1269764 | tf_op jit(solution)/shard_map/concatenate | solution.py:144
  14.2 7.3 %all-to-all-start = ((f32[32,16,320]{2,1,0:T(8,128)}), f32[32,16,320]{2,1,0:T(8,128)S(1)}, u32[]{:S(2)}, u32[]{:S(2)}) async-start(f32[32,16,320]{2,1,0:T(8,128)} %concatenate.203), calls=%async_computation | async-start | bytes 1572864 | tf_op jit(solution)/shard_map/all_to_all | solution.py:145
  29.5 2.5 %broadcast_in_dim.295 = f32[64,128,128]{2,1,0:T(8,128)} broadcast(f32[]{:T(128)} %constant.507.clone.1), dimensions={} | broadcast | bytes 4194308 | tf_op jit(solution)/shard_map/broadcast_in_dim | solution.py:271
  34.0 7.0 %all-to-all-done = f32[32,16,320]{2,1,0:T(8,128)S(1)} async-done(((f32[32,16,320]{2,1,0:T(8,128)}), f32[32,16,320]{2,1,0:T(8,128)S(1)}, u32[]{:S(2)}, u32[]{:S(2)}) %all-to-all-start) | async-done | bytes 655392 | tf_op jit(solution)/shard_map/all_to_all | solution.py:145
  43.4 3.3 %concatenate.225 = f32[47,3200]{1,0:T(8,128)S(1)} concatenate(f32[4,3200]{1,0:T(4,128)} %pad_maximum_fusion.13, f32[6,3200]{1,0:T(8,128)S(1)} %get-tuple-element.1130, f32[6,3200]{1,0:T(8,128)S(1)} %get-tuple-element.1129, f32[6,3200]{1,0:T(8,128)S(1)} %get-tuple-element.1128, f32[25,3200]{1,0:T(8,128)S(1)} %pad_maximum_fusion), dimensions={0} | concatenate | bytes 1203200 | tf_op jit(solution)/shard_map/concatenate | solution.py:166
  47.3 11.2 %while.115 = (s32[]{:T(128)}, f32[47,16,128]{2,1,0:T(8,128)S(1)}, f32[64,128,128]{2,1,0:T(8,128)}, s32[]{:T(128)}, s32[]{:T(128)}, /*index=5*/s32[96]{0:T(128)S(...) while((s32[]{:T(128)}, f32[47,16,128]{2,1,0:T(8,128)S(1)}, ...), condition=%wide.region_14.16_spmd.clone, body=%wide.region_13.15_spmd.clone.sunk | while | flops 197711392 | bytes 7514072 | solution.py:268
  49.0 3.1 %fusion.413 = f32[64,128,128]{2,1,0:T(8,128)} fusion(f32[64,128,128]{2,1,0:T(8,128)} %get-tuple-element.2010, s32[]{:T(128)S(6)} %select_n.1071, f32[32,128]{1,0:T(8,128)S(1)} %bitcast.755, f32[32,128]{1,0:T(8,128)S(1)} %bitcast.767, f32[32,128]{1,0:T(8,128)S(1)} %bitcast.757, f32[32,128]{1,0:T(8,128)S(1)} %bitcast.769, f32[32,128]{1,0:T(8,128)S(1)} %bitcast.753, ...), kind=kLoop, calls=%fused_computation.74.clone.1 | loop fusion | flops 6291456 | bytes 2195460 | tf_op jit(solution)/shard_map/while/body/dynamic_update_slice | solution.py:265
  52.7 4.4 %fusion.411 = f32[47,32,128]{2,0,1:T(8,128)S(1)} fusion(f32[32,128]{1,0:T(8,128)S(1)} %bitcast.756, f32[32,128]{1,0:T(8,128)S(1)} %bitcast.768, f32[32,128]{1,0:T(8,128)S(1)} %bitcast.758, f32[32,128]{1,0:T(8,128)S(1)} %bitcast.770, f32[32,128]{1,0:T(8,128)S(1)} %bitcast.754, f32[32,128]{1,0:T(8,128)S(1)} %bitcast.766, ...), kind=kOutput, calls=%fused_computation.76.clone.1 | convolution fusion | flops 154333184 | bytes 1638432 | tf_op jit(solution)/shard_map/while/body/rtb,tab->rta/dot_general | solution.py:242
  62.7 2.4 %gather_fusion.17 = f32[1088,3]{1,0:T(8,128)S(1)} fusion(f32[3,2048]{0,1:T(8,128)S(1)} %copy.422, s32[2048]{0:T(1024)S(1)} %copy-done.6), kind=kCustom, calls=%fused_computation.2.clone | custom fusion | bytes 30464 | tf_op jit(solution)/shard_map/jit(_take)/gather | solution.py:124
  67.4 0.8 broadcast_select_fusion.4
  68.2 8.3 %all-to-all-start.1 = ((f32[32,3,320]{2,1,0:T(4,128)}), f32[32,3,320]{2,1,0:T(4,128)S(1)}, u32[]{:S(2)}, u32[]{:S(2)}) async-start(f32[32,3,320]{2,1,0:T(4,128)} %broadcast_select_fusion.4), calls=%async_computation.1 | async-start | bytes 393216 | tf_op jit(solution)/shard_map/all_to_all | solution.py:145
  79.4 6.4 %all-to-all-done.1 = f32[32,3,320]{2,1,0:T(4,128)S(1)} async-done(((f32[32,3,320]{2,1,0:T(4,128)}), f32[32,3,320]{2,1,0:T(4,128)S(1)}, u32[]{:S(2)}, u32[]{:S(2)}) %all-to-all-start.1) | async-done | bytes 122912 | tf_op jit(solution)/shard_map/all_to_all | solution.py:145
  86.4 5.0 %while.117 = (s32[]{:T(128)}, f32[7,16,128]{2,1,0:T(8,128)S(1)}, s32[]{:T(128)}, s32[]{:T(128)}, f32[64,128,128]{2,1,0:T(8,128)}, /*index=5*/s32[96]{0:T(128)S(1...) while((s32[]{:T(128)}, f32[7,16,128]{2,1,0:T(8,128)S(1)}, ...), condition=%wide.region_20.26_spmd.clone, body=%wide.region_19.25_spmd.clone.sunk | while | flops 27570440 | bytes 2790636 | solution.py:288
  87.8 3.4 %fusion.424 = f32[7,32,128]{2,0,1:T(8,128)S(1)} fusion(f32[64,128,128]{2,1,0:T(8,128)} %get-tuple-element.2111, s32[]{:T(128)S(6)} %select_n.1076, f32[32,7,128]{2,1,0:T(8,128)S(1)} %gather_fusion.7, pred[32]{0:T(512)(128)(4,1)S(1)} %get-tuple-element.1879), kind=kOutput, calls=%fused_computation.134.clone.1 | convolution fusion | flops 22048768 | bytes 2326564 | tf_op jit(solution)/shard_map/while/body/rtb,tab->rta/dot_general | solution.py:242
  91.9 2.4 %gather_fusion.19 = f32[1088,3]{1,0:T(8,128)S(1)} fusion(f32[3,2048]{0,1:T(8,128)S(1)} %copy.436, s32[2048]{0:T(1024)S(1)} %copy-done.6), kind=kCustom, calls=%fused_computation.13.clone | custom fusion | bytes 30464 | tf_op jit(solution)/shard_map/jit(_take)/gather | solution.py:124
  97.3 2.6 %all-to-all-start.2 = ((f32[32,3,320]{2,1,0:T(4,128)}), f32[32,3,320]{2,1,0:T(4,128)S(1)}, u32[]{:S(2)}, u32[]{:S(2)}) async-start(f32[32,3,320]{2,1,0:T(4,128)} %broadcast_select_fusion.3), calls=%async_computation.2 | async-start | bytes 393216 | tf_op jit(solution)/shard_map/all_to_all | solution.py:145
  100.0 9.2 %all-to-all-done.2 = f32[32,3,320]{2,1,0:T(4,128)S(1)} async-done(((f32[32,3,320]{2,1,0:T(4,128)}), f32[32,3,320]{2,1,0:T(4,128)S(1)}, u32[]{:S(2)}, u32[]{:S(2)}) %all-to-all-start.2) | async-done | bytes 122912 | tf_op jit(solution)/shard_map/all_to_all | solution.py:145
  109.7 5.2 %while.119 = (s32[]{:T(128)}, f32[7,16,128]{2,1,0:T(8,128)S(1)}, s32[]{:T(128)}, s32[]{:T(128)}, f32[64,128,128]{2,1,0:T(8,128)}, /*index=5*/s32[96]{0:T(128)S(1...) while((s32[]{:T(128)}, f32[7,16,128]{2,1,0:T(8,128)S(1)}, ...), condition=%wide.region_26.32_spmd.clone, body=%wide.region_25.31_spmd.clone.sunk | while | flops 27570440 | bytes 2790636 | solution.py:288
  111.1 3.4 %fusion.436 = f32[7,32,128]{2,0,1:T(8,128)S(1)} fusion(f32[64,128,128]{2,1,0:T(8,128)} %get-tuple-element.2192, s32[]{:T(128)S(6)} %select_n.1082, f32[32,7,128]{2,1,0:T(8,128)S(1)} %gather_fusion.9, pred[32]{0:T(512)(128)(4,1)S(1)} %get-tuple-element.1902), kind=kOutput, calls=%fused_computation.176.clone.1 | convolution fusion | flops 22048768 | bytes 2326564 | tf_op jit(solution)/shard_map/while/body/rtb,tab->rta/dot_general | solution.py:242
  115.5 2.4 %gather_fusion.21 = f32[1088,3]{1,0:T(8,128)S(1)} fusion(f32[3,2048]{0,1:T(8,128)S(1)} %copy.450, s32[2048]{0:T(1024)S(1)} %copy-done.6), kind=kCustom, calls=%fused_computation.14.clone | custom fusion | bytes 30464 | tf_op jit(solution)/shard_map/jit(_take)/gather | solution.py:124
  120.8 2.6 %all-to-all-start.3 = ((f32[32,3,320]{2,1,0:T(4,128)}), f32[32,3,320]{2,1,0:T(4,128)S(1)}, u32[]{:S(2)}, u32[]{:S(2)}) async-start(f32[32,3,320]{2,1,0:T(4,128)} %broadcast_select_fusion.2), calls=%async_computation.3 | async-start | bytes 393216 | tf_op jit(solution)/shard_map/all_to_all | solution.py:145
  123.5 9.2 %all-to-all-done.3 = f32[32,3,320]{2,1,0:T(4,128)S(1)} async-done(((f32[32,3,320]{2,1,0:T(4,128)}), f32[32,3,320]{2,1,0:T(4,128)S(1)}, u32[]{:S(2)}, u32[]{:S(2)}) %all-to-all-start.3) | async-done | bytes 122912 | tf_op jit(solution)/shard_map/all_to_all | solution.py:145
  133.3 5.0 %while.121 = (s32[]{:T(128)}, f32[7,16,128]{2,1,0:T(8,128)S(1)}, s32[]{:T(128)}, s32[]{:T(128)}, f32[64,128,128]{2,1,0:T(8,128)}, /*index=5*/s32[96]{0:T(128)S(1...) while((s32[]{:T(128)}, f32[7,16,128]{2,1,0:T(8,128)S(1)}, ...), condition=%wide.region_32.38_spmd.clone, body=%wide.region_31.37_spmd.clone.sunk | while | flops 27570440 | bytes 2790636 | solution.py:288
  134.7 3.4 %fusion.448 = f32[7,32,128]{2,0,1:T(8,128)S(1)} fusion(f32[64,128,128]{2,1,0:T(8,128)} %get-tuple-element.2273, s32[]{:T(128)S(6)} %select_n.1088, f32[32,7,128]{2,1,0:T(8,128)S(1)} %gather_fusion.11, pred[32]{0:T(512)(128)(4,1)S(1)} %get-tuple-element.1925), kind=kOutput, calls=%fused_computation.218.clone.1 | convolution fusion | flops 22048768 | bytes 2326564 | tf_op jit(solution)/shard_map/while/body/rtb,tab->rta/dot_general | solution.py:242
  138.8 2.4 %gather_fusion.23 = f32[1088,3]{1,0:T(8,128)S(1)} fusion(f32[3,2048]{0,1:T(8,128)S(1)} %copy.464, s32[2048]{0:T(1024)S(1)} %copy-done.6), kind=kCustom, calls=%fused_computation.15.clone | custom fusion | bytes 30464 | tf_op jit(solution)/shard_map/jit(_take)/gather | solution.py:124
  144.2 2.6 %all-to-all-start.4 = ((f32[32,3,320]{2,1,0:T(4,128)}), f32[32,3,320]{2,1,0:T(4,128)S(1)}, u32[]{:S(2)}, u32[]{:S(2)}) async-start(f32[32,3,320]{2,1,0:T(4,128)} %broadcast_select_fusion.1), calls=%async_computation.4 | async-start | bytes 393216 | tf_op jit(solution)/shard_map/all_to_all | solution.py:145
  146.8 9.2 %all-to-all-done.4 = f32[32,3,320]{2,1,0:T(4,128)S(1)} async-done(((f32[32,3,320]{2,1,0:T(4,128)}), f32[32,3,320]{2,1,0:T(4,128)S(1)}, u32[]{:S(2)}, u32[]{:S(2)}) %all-to-all-start.4) | async-done | bytes 122912 | tf_op jit(solution)/shard_map/all_to_all | solution.py:145
  156.6 5.0 %while.123 = (s32[]{:T(128)}, f32[7,16,128]{2,1,0:T(8,128)S(1)}, s32[]{:T(128)}, s32[]{:T(128)}, f32[64,128,128]{2,1,0:T(8,128)}, /*index=5*/s32[96]{0:T(128)S(1...) while((s32[]{:T(128)}, f32[7,16,128]{2,1,0:T(8,128)S(1)}, ...), condition=%wide.region_38.44_spmd.clone, body=%wide.region_37.43_spmd.clone.sunk | while | flops 27570440 | bytes 2790636 | solution.py:288
  158.0 3.4 %fusion.460 = f32[7,32,128]{2,0,1:T(8,128)S(1)} fusion(f32[64,128,128]{2,1,0:T(8,128)} %get-tuple-element.2354, s32[]{:T(128)S(6)} %select_n.1094, f32[32,7,128]{2,1,0:T(8,128)S(1)} %gather_fusion.13, pred[32]{0:T(512)(128)(4,1)S(1)} %get-tuple-element.1948), kind=kOutput, calls=%fused_computation.260.clone.1 | convolution fusion | flops 22048768 | bytes 2326564 | tf_op jit(solution)/shard_map/while/body/rtb,tab->rta/dot_general | solution.py:242
  (474 shorter events, 42.7 us)
Async XLA Ops:
  0.6 9.1 %copy-start = (s32[9]{0:T(128)S(1)}, s32[9]{0:T(128)}, u32[]{:S(2)}) copy-start(s32[9]{0:T(128)} %constant.531.clone) | copy-start | bytes 112
  2.1 8.4 %copy-start.27 = (pred[1088]{0:T(1024)(128)(4,1)}, pred[1088]{0:T(1024)(128)(4,1)S(1)}, u32[]{:S(2)}) copy-start(pred[1088]{0:T(1024)(128)(4,1)S(1)} %compare_and_fusion.12) | copy-start | bytes 3268
  5.0 5.5 %copy-start.34 = (pred[320]{0:T(512)(128)(4,1)S(1)}, pred[320]{0:T(512)(128)(4,1)}, u32[]{:S(2)}) copy-start(pred[320]{0:T(512)(128)(4,1)} %constant.503.clone.1) | copy-start | bytes 964
  7.0 3.4 %copy-start.5 = (s32[2048]{0:T(1024)}, s32[2048]{0:T(1024)S(1)}, u32[]{:S(2)}) copy-start(s32[2048]{0:T(1024)S(1)} %pad_clamp_fusion.12) | copy-start | bytes 24580
  12.4 9.2 %copy-start.2 = (f32[3,2048]{1,0:T(4,128)S(1)}, f32[3,2048]{1,0:T(4,128)}, u32[]{:S(2)}) copy-start(f32[3,2048]{1,0:T(4,128)} %param.49) | copy-start | bytes 73732
  12.5 9.3 %copy-start.1 = (f32[3,2048]{1,0:T(4,128)S(1)}, f32[3,2048]{1,0:T(4,128)}, u32[]{:S(2)}) copy-start(f32[3,2048]{1,0:T(4,128)} %param.46) | copy-start | bytes 73732
  12.5 10.0 %copy-start.37 = (s32[64]{0:T(128)S(1)}, s32[64]{0:T(128)}, u32[]{:S(2)}) copy-start(s32[64]{0:T(128)} %param.55) | copy-start | bytes 772
  12.5 13.2 %copy-start.3 = (f32[2048]{0:T(1024)S(1)}, f32[2048]{0:T(1024)}, u32[]{:S(2)}) copy-start(f32[2048]{0:T(1024)} %param.47) | copy-start | bytes 24580
  12.6 13.3 %copy-start.4 = (f32[2048]{0:T(1024)S(1)}, f32[2048]{0:T(1024)}, u32[]{:S(2)}) copy-start(f32[2048]{0:T(1024)} %param.50) | copy-start | bytes 24580
  14.2 26.8 %all-to-all-start = ((f32[32,16,320]{2,1,0:T(8,128)}), f32[32,16,320]{2,1,0:T(8,128)S(1)}, u32[]{:S(2)}, u32[]{:S(2)}) async-start(f32[32,16,320]{2,1,0:T(8,128)} %concatenate.203), calls=%async_computation | async-start | bytes 1572864 | tf_op jit(solution)/shard_map/all_to_all | solution.py:145
  21.8 10.8 %copy-start.20 = (f32[1,2048]{1,0:T(1,128)}, f32[1,2048]{1,0:T(1,128)S(1)}, u32[]{:S(2)}) copy-start(f32[1,2048]{1,0:T(1,128)S(1)} %get-tuple-element.1283) | copy-start | bytes 24580
  21.9 10.8 %copy-start.22 = (f32[1,2048]{1,0:T(1,128)}, f32[1,2048]{1,0:T(1,128)S(1)}, u32[]{:S(2)}) copy-start(f32[1,2048]{1,0:T(1,128)S(1)} %get-tuple-element.1284) | copy-start | bytes 24580
  21.9 10.8 %copy-start.24 = (f32[1,2048]{1,0:T(1,128)}, f32[1,2048]{1,0:T(1,128)S(1)}, u32[]{:S(2)}) copy-start(f32[1,2048]{1,0:T(1,128)S(1)} %get-tuple-element.1285) | copy-start | bytes 24580
  21.9 7.4 %copy-start.38 = (s32[64]{0:T(128)S(1)}, s32[64]{0:T(128)}, u32[]{:S(2)}) copy-start(s32[64]{0:T(128)} %param.54) | copy-start | bytes 772
  41.1 2.2 %copy-start.9 = (f32[15,160]{1,0:T(8,128)}, f32[15,160]{1,0:T(8,128)S(1)}, u32[]{:S(2)}) copy-start(f32[15,160]{1,0:T(8,128)S(1)} %slice_select_fusion.6) | copy-start | bytes 28804
  41.1 2.1 %copy-start.12 = (f32[15,32]{1,0:T(8,128)}, f32[15,32]{1,0:T(8,128)S(1)}, u32[]{:S(2)}) copy-start(f32[15,32]{1,0:T(8,128)S(1)} %slice_select_fusion.7) | copy-start | bytes 5764
  41.1 2.1 %copy-start.14 = (f32[15,32]{1,0:T(8,128)}, f32[15,32]{1,0:T(8,128)S(1)}, u32[]{:S(2)}) copy-start(f32[15,32]{1,0:T(8,128)S(1)} %slice_select_fusion.8) | copy-start | bytes 5764
  43.4 3.9 %copy-start.30 = (s32[96]{0:T(128)S(1)}, s32[96]{0:T(128)}, u32[]{:S(2)}) copy-start(s32[96]{0:T(128)} %copy-done.29) | copy-start | bytes 1156
  47.2 14.2 %copy-start.21 = (f32[1,2048]{1,0:T(1,128)S(1)}, f32[1,2048]{1,0:T(1,128)}, u32[]{:S(2)}) copy-start(f32[1,2048]{1,0:T(1,128)} %copy-done.20) | copy-start | bytes 24580
  47.3 14.2 %copy-start.23 = (f32[1,2048]{1,0:T(1,128)S(1)}, f32[1,2048]{1,0:T(1,128)}, u32[]{:S(2)}) copy-start(f32[1,2048]{1,0:T(1,128)} %copy-done.22) | copy-start | bytes 24580
  47.3 14.2 %copy-start.25 = (f32[1,2048]{1,0:T(1,128)S(1)}, f32[1,2048]{1,0:T(1,128)}, u32[]{:S(2)}) copy-start(f32[1,2048]{1,0:T(1,128)} %copy-done.24) | copy-start | bytes 24580
  58.5 3.2 %copy-start.26 = (f32[3,2048]{1,0:T(4,128)S(1)}, f32[3,2048]{1,0:T(4,128)}, u32[]{:S(2)}) copy-start(f32[3,2048]{1,0:T(4,128)} %param.48) | copy-start | bytes 73732
  58.5 4.2 %copy-start.6 = (s32[2048]{0:T(1024)S(1)}, s32[2048]{0:T(1024)}, u32[]{:S(2)}) copy-start(s32[2048]{0:T(1024)} %copy-done.5) | copy-start | bytes 24580
  58.5 6.6 %copy-start.28 = (pred[1088]{0:T(1024)(128)(4,1)S(1)}, pred[1088]{0:T(1024)(128)(4,1)}, u32[]{:S(2)}) copy-start(pred[1088]{0:T(1024)(128)(4,1)} %copy-done.27) | copy-start | bytes 3268
  58.6 6.7 %copy-start.35 = (pred[320]{0:T(512)(128)(4,1)S(1)}, pred[320]{0:T(512)(128)(4,1)}, u32[]{:S(2)}) copy-start(pred[320]{0:T(512)(128)(4,1)} %constant.503.clone.1) | copy-start | bytes 964
  65.5 11.0 %copy-start.8 = (f32[2048]{0:T(1024)S(1)}, f32[2048]{0:T(1024)}, u32[]{:S(2)}) copy-start(f32[2048]{0:T(1024)} %copy-done.7) | copy-start | bytes 24580
  65.5 11.0 %copy-start.11 = (f32[2048]{0:T(1024)S(1)}, f32[2048]{0:T(1024)}, u32[]{:S(2)}) copy-start(f32[2048]{0:T(1024)} %param.51) | copy-start | bytes 24580
  65.6 11.1 %copy-start.31 = (s32[96]{0:T(128)S(1)}, s32[96]{0:T(128)}, u32[]{:S(2)}) copy-start(s32[96]{0:T(128)} %copy-done.29) | copy-start | bytes 1156
  68.2 17.6 %all-to-all-start.1 = ((f32[32,3,320]{2,1,0:T(4,128)}), f32[32,3,320]{2,1,0:T(4,128)S(1)}, u32[]{:S(2)}, u32[]{:S(2)}) async-start(f32[32,3,320]{2,1,0:T(4,128)} %broadcast_select_fusion.4), calls=%async_computation.1 | async-start | bytes 393216 | tf_op jit(solution)/shard_map/all_to_all | solution.py:145
  97.3 11.9 %all-to-all-start.2 = ((f32[32,3,320]{2,1,0:T(4,128)}), f32[32,3,320]{2,1,0:T(4,128)S(1)}, u32[]{:S(2)}, u32[]{:S(2)}) async-start(f32[32,3,320]{2,1,0:T(4,128)} %broadcast_select_fusion.3), calls=%async_computation.2 | async-start | bytes 393216 | tf_op jit(solution)/shard_map/all_to_all | solution.py:145
  120.8 11.9 %all-to-all-start.3 = ((f32[32,3,320]{2,1,0:T(4,128)}), f32[32,3,320]{2,1,0:T(4,128)S(1)}, u32[]{:S(2)}, u32[]{:S(2)}) async-start(f32[32,3,320]{2,1,0:T(4,128)} %broadcast_select_fusion.2), calls=%async_computation.3 | async-start | bytes 393216 | tf_op jit(solution)/shard_map/all_to_all | solution.py:145
  144.2 11.9 %all-to-all-start.4 = ((f32[32,3,320]{2,1,0:T(4,128)}), f32[32,3,320]{2,1,0:T(4,128)S(1)}, u32[]{:S(2)}, u32[]{:S(2)}) async-start(f32[32,3,320]{2,1,0:T(4,128)} %broadcast_select_fusion.1), calls=%async_computation.4 | async-start | bytes 393216 | tf_op jit(solution)/shard_map/all_to_all | solution.py:145
  (12 other events, 15.2 us)

commit v5 on v4

--- a/solution.py
+++ b/solution.py
@@ -228,13 +228,19 @@
     list_j = jnp.concatenate([jnp.sum(jnp.where(place, tile_j[None, :], 0), axis=1), pad])
     split = first_n // batch * batch
 
+    spots = jnp.arange(tiles_total + batch, dtype=jnp.int32)
+    owner = list_i[None, :] == block_ids[:, None]
+    onehots = {
+        stop: (owner & (spots < bound)[None, :]).astype(jnp.float32)
+        for stop, bound in (("split", split), ("count", count))
+    }
+
     def batch_lists(offset, stop, clip):
         near_ids = lax.dynamic_slice_in_dim(list_i, offset, batch, 0)
         far_ids = lax.dynamic_slice_in_dim(list_j, offset, batch, 0)
         if clip:
             far_ids = jnp.minimum(far_ids, nblocks - 1)
-        usable = offset + jnp.arange(batch, dtype=jnp.int32) < stop
-        onehot = ((near_ids[None, :] == block_ids[:, None]) & usable[None, :]).astype(jnp.float32)
+        onehot = lax.dynamic_slice_in_dim(onehots[stop], offset, batch, 1)
         return (near_ids, far_ids, onehot)
 
     def fold_batch(acc, blocks, weight, far_ids, onehot):
@@ -254,7 +260,11 @@
             preferred_element_type=jnp.float32,
         )
 
-    def hydro_pass(start, stop, pos_far, blocks, carry, clip):
+    bounds = {0: 0, "split": split, "count": count}
+
+    def hydro_pass(first, stop, pos_far, blocks, carry, clip):
+        start = bounds[first]
+
         def step(turn, carry):
             acc, stored = carry
             offset = start + turn * batch
@@ -265,12 +275,12 @@
             stored = lax.dynamic_update_slice_in_dim(stored, weight, offset, 0)
             return (fold_batch(acc, blocks, weight, far_ids, onehot), stored)
 
-        return lax.fori_loop(0, (stop - start + batch - 1) // batch, step, carry)
+        return lax.fori_loop(0, (bounds[stop] - start + batch - 1) // batch, step, carry)
 
     acc_start = jnp.zeros((len(keep), nblocks, TILE), jnp.float32)
     stored_start = jnp.zeros((tiles_total, TILE, TILE), jnp.float32)
-    carry = hydro_pass(0, split, pos_local, q_local_blocks, (acc_start, stored_start), True)
-    acc, stored = hydro_pass(split, count, pos_blocks, q_blocks, carry, False)
+    carry = hydro_pass(0, "split", pos_local, q_local_blocks, (acc_start, stored_start), True)
+    acc, stored = hydro_pass("split", "count", pos_blocks, q_blocks, carry, False)
     acc = pick_rows(acc.reshape(len(keep), nlocal), source)
     rate, count_n = hydro_rate(acc, qlocal, ch)
     density_new = density + dt * rate[0]
@@ -278,20 +288,22 @@
     yzero = field + dt * rate[4:7]
     psi_new = (psi + dt * rate[7]) * jnp.exp(-damping * dt * ch)
 
-    def diff_pass(start, stop, blocks, acc, clip):
+    def diff_pass(first, stop, blocks, acc, clip):
+        start = bounds[first]
+
         def step(turn, acc_diff):
             offset = start + turn * batch
             near_ids, far_ids, onehot = batch_lists(offset, stop, clip)
             weight = lax.dynamic_slice_in_dim(stored, offset, batch, 0)
             return fold_batch(acc_diff, blocks, weight, far_ids, onehot)
 
-        return lax.fori_loop(0, (stop - start + batch - 1) // batch, step, acc)
+        return lax.fori_loop(0, (bounds[stop] - start + batch - 1) // batch, step, acc)
 
     def operator(bfl):
         eta = ohmic + fac * jnp.sum(bfl * bfl, axis=0)
         q_near = jnp.concatenate([bfl, eta[None] * bfl, eta[None]], axis=0)
         acc_diff = diff_pass(
-            0, split, q_near.reshape(7, nblocks, TILE), jnp.zeros((7, nblocks, TILE), jnp.float32), True
+            0, "split", q_near.reshape(7, nblocks, TILE), jnp.zeros((7, nblocks, TILE), jnp.float32), True
         )
         ghost_b = spread_ghosts(bfl, ghost_index)
         ghost_eta = ghosts[13] + ghosts[14] * jnp.sum(ghost_b * ghost_b, axis=0)
@@ -299,7 +311,7 @@
         eta_ext = extend(eta[None], ghost_eta[None])[0]
         qdiff = jnp.concatenate([b_ext, eta_ext[None] * b_ext, eta_ext[None]], axis=0)
         diff_blocks = qdiff.reshape(7, EXT_BLOCKS, TILE)
-        acc_diff = diff_pass(split, count, diff_blocks, acc_diff, False)
+        acc_diff = diff_pass("split", "count", diff_blocks, acc_diff, False)
         return diffusion_rate(acc_diff.reshape(7, nlocal), bfl, eta, count_n)
 
     first, rows = rkl_table(SECTIONS)

time: 164 us -> 159 us (0.970)
  other arithmetic: 24.9 us -> 20.3 us
  waiting for transfers between devices: 41 us -> 42.7 us
    and x4, other arithmetic: 2.91 us -> 0.33 us  [fold_batch(): qsel = jnp.take(blocks, far_ids, axis=1)]
    unnamed x155 -> x94, local copies, waits for them, and re-layouts: 2.47 us -> 0.68 us
where the time goes in v5:
time: 159 us; the launch traced here: 158 us
  waiting for transfers between devices  42.7 us (27%)
  local copies, waits for them, and re-layouts  41.8 us (26%)
  starting transfers between devices  22.6 us (14%)
  other arithmetic  20.3 us (13%)
  matrix products  19.7 us (12%)
  between operations  10.2 us (6%)
    all_to_all x5, waiting for transfers between devices, spread_ghosts(): incoming = lax.all_to_all(outgoing, ('gx', 'gy'), 0, 0, tiled=True)  42.7 us
    all_to_all x5, starting transfers between devices, spread_ghosts(): incoming = lax.all_to_all(outgoing, ('gx', 'gy'), 0, 0, tiled=True)  22.6 us
    dot_general x5, matrix products, fold_batch(): jnp.einsum('rtb,tab->rta', qsel, weight, precision=lax.Precision.HIGH, pr...  17.8 us
    gather x5, local copies, waits for them, and re-layouts, spread_ghosts(): sent = jnp.take(rows, ghost_index, axis=1)  12 us
    another operation x68, local copies, waits for them, and re-layouts, spread_ghosts(): segments = jnp.stack(segments)  4.7 us
    gather x5, local copies, waits for them, and re-layouts, spread_ghosts(): outgoing = jnp.take(segments, pick, axis=0)  3.32 us
    select_n x6, other arithmetic, spread_ghosts(): outgoing = jnp.take(segments, pick, axis=0)  3.28 us
  transfers between devices with their start and end apart: 5, of which 5 were waited for; matrix products, arithmetic and copies ran while one was open for 5% of the time, Pallas kernels for 0%

profile of v5, /device:TPU:0, one launch (start us, length us, event | category | flops | bytes accessed | tf_op | source)
XLA Modules:
  0.0 158.0 jit_solution(10416792067090099495)
XLA Ops:
  3.6 1.3 fusion.277
  5.0 1.7 %concatenate.202 = f32[15,2048]{1,0:T(8,128)S(1)} concatenate(f32[3,2048]{1,0:T(4,128)} %param.46, f32[1,2048]{1,0:T(1,128)S(1)} %broadcast_in_dim_broadcast_in_dim.3, f32[1,2048]{1,0:T(1,128)} %bitcast.779, f32[3,2048]{1,0:T(4,128)S(1)} %get-tuple-element.781, f32[3,2048]{1,0:T(4,128)} %param.49, f32[1,2048]{1,0:T(1,128)} %bitcast.784, f32[1,2048]{1,0:T(1,128)S(1)} %bitcast.793, ...), dimensions={0} | concatenate | bytes 245760 | tf_op jit(solution)/shard_map/concatenate | solution.py:196
  7.0 2.4 %gather_fusion.15 = f32[1088,15]{1,0:T(8,128)S(1)} fusion(f32[15,2048]{0,1:T(8,128)S(1)} %copy.405, s32[2048]{0:T(1024)S(1)} %pad_clamp_fusion.12), kind=kCustom, calls=%fused_computation.23 | custom fusion | bytes 134912 | tf_op jit(solution)/shard_map/jit(_take)/gather | solution.py:124
  12.5 1.6 %concatenate.203 = f32[32,16,320]{2,1,0:T(8,128)} pad(f32[32,15,320]{2,1,0:T(8,128)S(1)} %broadcast_select_fusion, f32[]{:T(128)} %get-tuple-element.764), padding=0_0x0_1x0_0 | pad | bytes 1269764 | tf_op jit(solution)/shard_map/concatenate | solution.py:144
  14.1 7.3 %all-to-all-start = ((f32[32,16,320]{2,1,0:T(8,128)}), f32[32,16,320]{2,1,0:T(8,128)S(1)}, u32[]{:S(2)}, u32[]{:S(2)}) async-start(f32[32,16,320]{2,1,0:T(8,128)} %concatenate.203), calls=%async_computation | async-start | bytes 1572864 | tf_op jit(solution)/shard_map/all_to_all | solution.py:145
  29.6 2.5 %broadcast_in_dim.269 = f32[64,128,128]{2,1,0:T(8,128)} broadcast(f32[]{:T(128)} %constant.507.clone.1), dimensions={} | broadcast | bytes 4194308 | tf_op jit(solution)/shard_map/broadcast_in_dim | solution.py:281
  33.0 7.9 %all-to-all-done = f32[32,16,320]{2,1,0:T(8,128)S(1)} async-done(((f32[32,16,320]{2,1,0:T(8,128)}), f32[32,16,320]{2,1,0:T(8,128)S(1)}, u32[]{:S(2)}, u32[]{:S(2)}) %all-to-all-start) | async-done | bytes 655392 | tf_op jit(solution)/shard_map/all_to_all | solution.py:145
  43.3 2.5 %concatenate.225 = f32[47,3200]{1,0:T(8,128)S(1)} concatenate(f32[4,3200]{1,0:T(4,128)S(1)} %pad_maximum_fusion.13, f32[6,3200]{1,0:T(8,128)S(1)} %get-tuple-element.810, f32[6,3200]{1,0:T(8,128)S(1)} %get-tuple-element.809, f32[6,3200]{1,0:T(8,128)S(1)} %get-tuple-element.808, f32[25,3200]{1,0:T(8,128)S(1)} %pad_maximum_fusion), dimensions={0} | concatenate | bytes 1203200 | tf_op jit(solution)/shard_map/concatenate | solution.py:166
  46.3 0.9 slice_bitcast_fusion.16
  47.2 10.7 %while.105 = (s32[]{:T(128)}, f32[47,16,128]{2,1,0:T(8,128)S(1)}, f32[64,128,128]{2,1,0:T(8,128)}, s32[]{:T(128)}, s32[]{:T(128)}, /*index=5*/s32[96]{0:T(128)S(...) while((s32[]{:T(128)}, f32[47,16,128]{2,1,0:T(8,128)S(1)}, ...), condition=%wide.region_14.16_spmd, body=%wide.region_13.15_spmd.sunk | while | flops 197710208 | bytes 7519764 | solution.py:278
  48.8 3.1 %fusion.377 = f32[64,128,128]{2,1,0:T(8,128)} fusion(f32[64,128,128]{2,1,0:T(8,128)} %get-tuple-element.1630, s32[]{:T(128)S(6)} %select_n.1040, f32[32,128]{1,0:T(8,128)S(1)} %bitcast.756, f32[32,128]{1,0:T(8,128)S(1)} %bitcast.768, f32[32,128]{1,0:T(8,128)S(1)} %bitcast.758, f32[32,128]{1,0:T(8,128)S(1)} %bitcast.770, f32[32,128]{1,0:T(8,128)S(1)} %bitcast.754, ...), kind=kLoop, calls=%fused_computation.61.clone.1 | loop fusion | flops 6291456 | bytes 2195460 | tf_op jit(solution)/shard_map/while/body/dynamic_update_slice | solution.py:275
  52.5 4.4 %fusion.375 = f32[47,32,128]{2,0,1:T(8,128)S(1)} fusion(f32[32,128]{1,0:T(8,128)S(1)} %bitcast.757, f32[32,128]{1,0:T(8,128)S(1)} %bitcast.769, f32[32,128]{1,0:T(8,128)S(1)} %bitcast.759, f32[32,128]{1,0:T(8,128)S(1)} %bitcast.771, f32[32,128]{1,0:T(8,128)S(1)} %bitcast.755, f32[32,128]{1,0:T(8,128)S(1)} %bitcast.767, ...), kind=kOutput, calls=%fused_computation.63.clone.1 | convolution fusion | flops 154333184 | bytes 1638432 | tf_op jit(solution)/shard_map/while/body/rtb,tab->rta/dot_general | solution.py:248
  62.0 2.4 %gather_fusion.17 = f32[1088,3]{1,0:T(8,128)S(1)} fusion(f32[3,2048]{0,1:T(8,128)S(1)} %copy.422, s32[2048]{0:T(1024)S(1)} %pad_clamp_fusion.12), kind=kCustom, calls=%fused_computation.2.clone | custom fusion | bytes 30464 | tf_op jit(solution)/shard_map/jit(_take)/gather | solution.py:124
  67.3 7.5 %all-to-all-start.1 = ((f32[32,3,320]{2,1,0:T(4,128)}), f32[32,3,320]{2,1,0:T(4,128)S(1)}, u32[]{:S(2)}, u32[]{:S(2)}) async-start(f32[32,3,320]{2,1,0:T(4,128)} %broadcast_select_fusion.4), calls=%async_computation.1 | async-start | bytes 393216 | tf_op jit(solution)/shard_map/all_to_all | solution.py:145
  77.0 7.2 %all-to-all-done.1 = f32[32,3,320]{2,1,0:T(4,128)S(1)} async-done(((f32[32,3,320]{2,1,0:T(4,128)}), f32[32,3,320]{2,1,0:T(4,128)S(1)}, u32[]{:S(2)}, u32[]{:S(2)}) %all-to-all-start.1) | async-done | bytes 122912 | tf_op jit(solution)/shard_map/all_to_all | solution.py:145
  84.8 4.4 %while.107 = (s32[]{:T(128)}, f32[7,16,128]{2,1,0:T(8,128)S(1)}, s32[]{:T(128)}, s32[]{:T(128)}, f32[64,128,128]{2,1,0:T(8,128)}, /*index=5*/s32[96]{0:T(128)S(1...) while((s32[]{:T(128)}, f32[7,16,128]{2,1,0:T(8,128)S(1)}, ...), condition=%wide.region_20.26_spmd, body=%wide.region_19.25_spmd.sunk | while | flops 27569352 | bytes 2796316 | solution.py:300
  85.5 3.4 %fusion.388 = f32[7,32,128]{2,0,1:T(8,128)S(1)} fusion(f32[64,128,128]{2,1,0:T(8,128)} %get-tuple-element.1726, s32[]{:T(128)S(6)} %select_n.1045, f32[32,7,128]{2,1,0:T(8,128)S(1)} %gather_fusion.7, pred[32]{0:T(512)(128)(4,1)S(1)} %get-tuple-element.1512), kind=kOutput, calls=%fused_computation.115.clone.1 | convolution fusion | flops 22048768 | bytes 2326564 | tf_op jit(solution)/shard_map/while/body/rtb,tab->rta/dot_general | solution.py:248
  89.6 2.4 %gather_fusion.19 = f32[1088,3]{1,0:T(8,128)S(1)} fusion(f32[3,2048]{0,1:T(8,128)S(1)} %copy.436, s32[2048]{0:T(1024)S(1)} %pad_clamp_fusion.12), kind=kCustom, calls=%fused_computation.13.clone | custom fusion | bytes 30464 | tf_op jit(solution)/shard_map/jit(_take)/gather | solution.py:124
  94.9 2.6 %all-to-all-start.2 = ((f32[32,3,320]{2,1,0:T(4,128)}), f32[32,3,320]{2,1,0:T(4,128)S(1)}, u32[]{:S(2)}, u32[]{:S(2)}) async-start(f32[32,3,320]{2,1,0:T(4,128)} %broadcast_select_fusion.3), calls=%async_computation.2 | async-start | bytes 393216 | tf_op jit(solution)/shard_map/all_to_all | solution.py:145
  97.6 9.2 %all-to-all-done.2 = f32[32,3,320]{2,1,0:T(4,128)S(1)} async-done(((f32[32,3,320]{2,1,0:T(4,128)}), f32[32,3,320]{2,1,0:T(4,128)S(1)}, u32[]{:S(2)}, u32[]{:S(2)}) %all-to-all-start.2) | async-done | bytes 122912 | tf_op jit(solution)/shard_map/all_to_all | solution.py:145
  107.4 4.6 %while.109 = (s32[]{:T(128)}, f32[7,16,128]{2,1,0:T(8,128)S(1)}, s32[]{:T(128)}, s32[]{:T(128)}, f32[64,128,128]{2,1,0:T(8,128)}, /*index=5*/s32[96]{0:T(128)S(1...) while((s32[]{:T(128)}, f32[7,16,128]{2,1,0:T(8,128)S(1)}, ...), condition=%wide.region_26.32_spmd, body=%wide.region_25.31_spmd.sunk | while | flops 27569352 | bytes 2796316 | solution.py:300
  108.1 3.4 %fusion.400 = f32[7,32,128]{2,0,1:T(8,128)S(1)} fusion(f32[64,128,128]{2,1,0:T(8,128)} %get-tuple-element.1801, s32[]{:T(128)S(6)} %select_n.1051, f32[32,7,128]{2,1,0:T(8,128)S(1)} %gather_fusion.9, pred[32]{0:T(512)(128)(4,1)S(1)} %get-tuple-element.1531), kind=kOutput, calls=%fused_computation.151.clone.1 | convolution fusion | flops 22048768 | bytes 2326564 | tf_op jit(solution)/shard_map/while/body/rtb,tab->rta/dot_general | solution.py:248
  112.5 2.4 %gather_fusion.21 = f32[1088,3]{1,0:T(8,128)S(1)} fusion(f32[3,2048]{0,1:T(8,128)S(1)} %copy.450, s32[2048]{0:T(1024)S(1)} %pad_clamp_fusion.12), kind=kCustom, calls=%fused_computation.14.clone | custom fusion | bytes 30464 | tf_op jit(solution)/shard_map/jit(_take)/gather | solution.py:124
  117.8 2.6 %all-to-all-start.3 = ((f32[32,3,320]{2,1,0:T(4,128)}), f32[32,3,320]{2,1,0:T(4,128)S(1)}, u32[]{:S(2)}, u32[]{:S(2)}) async-start(f32[32,3,320]{2,1,0:T(4,128)} %broadcast_select_fusion.2), calls=%async_computation.3 | async-start | bytes 393216 | tf_op jit(solution)/shard_map/all_to_all | solution.py:145
  120.5 9.2 %all-to-all-done.3 = f32[32,3,320]{2,1,0:T(4,128)S(1)} async-done(((f32[32,3,320]{2,1,0:T(4,128)}), f32[32,3,320]{2,1,0:T(4,128)S(1)}, u32[]{:S(2)}, u32[]{:S(2)}) %all-to-all-start.3) | async-done | bytes 122912 | tf_op jit(solution)/shard_map/all_to_all | solution.py:145
  130.3 4.4 %while.111 = (s32[]{:T(128)}, f32[7,16,128]{2,1,0:T(8,128)S(1)}, s32[]{:T(128)}, s32[]{:T(128)}, f32[64,128,128]{2,1,0:T(8,128)}, /*index=5*/s32[96]{0:T(128)S(1...) while((s32[]{:T(128)}, f32[7,16,128]{2,1,0:T(8,128)S(1)}, ...), condition=%wide.region_32.38_spmd, body=%wide.region_31.37_spmd.sunk | while | flops 27569352 | bytes 2796316 | solution.py:300
  131.0 3.4 %fusion.412 = f32[7,32,128]{2,0,1:T(8,128)S(1)} fusion(f32[64,128,128]{2,1,0:T(8,128)} %get-tuple-element.1876, s32[]{:T(128)S(6)} %select_n.1057, f32[32,7,128]{2,1,0:T(8,128)S(1)} %gather_fusion.11, pred[32]{0:T(512)(128)(4,1)S(1)} %get-tuple-element.1550), kind=kOutput, calls=%fused_computation.187.clone.1 | convolution fusion | flops 22048768 | bytes 2326564 | tf_op jit(solution)/shard_map/while/body/rtb,tab->rta/dot_general | solution.py:248
  135.1 2.4 %gather_fusion.23 = f32[1088,3]{1,0:T(8,128)S(1)} fusion(f32[3,2048]{0,1:T(8,128)S(1)} %copy.464, s32[2048]{0:T(1024)S(1)} %pad_clamp_fusion.12), kind=kCustom, calls=%fused_computation.15.clone | custom fusion | bytes 30464 | tf_op jit(solution)/shard_map/jit(_take)/gather | solution.py:124
  140.5 2.6 %all-to-all-start.4 = ((f32[32,3,320]{2,1,0:T(4,128)}), f32[32,3,320]{2,1,0:T(4,128)S(1)}, u32[]{:S(2)}, u32[]{:S(2)}) async-start(f32[32,3,320]{2,1,0:T(4,128)} %broadcast_select_fusion.1), calls=%async_computation.4 | async-start | bytes 393216 | tf_op jit(solution)/shard_map/all_to_all | solution.py:145
  143.2 9.2 %all-to-all-done.4 = f32[32,3,320]{2,1,0:T(4,128)S(1)} async-done(((f32[32,3,320]{2,1,0:T(4,128)}), f32[32,3,320]{2,1,0:T(4,128)S(1)}, u32[]{:S(2)}, u32[]{:S(2)}) %all-to-all-start.4) | async-done | bytes 122912 | tf_op jit(solution)/shard_map/all_to_all | solution.py:145
  153.0 4.4 %while.113 = (s32[]{:T(128)}, f32[7,16,128]{2,1,0:T(8,128)S(1)}, s32[]{:T(128)}, s32[]{:T(128)}, f32[64,128,128]{2,1,0:T(8,128)}, /*index=5*/s32[96]{0:T(128)S(1...) while((s32[]{:T(128)}, f32[7,16,128]{2,1,0:T(8,128)S(1)}, ...), condition=%wide.region_38.44_spmd, body=%wide.region_37.43_spmd.sunk | while | flops 27569352 | bytes 2796316 | solution.py:300
  153.7 3.4 %fusion.424 = f32[7,32,128]{2,0,1:T(8,128)S(1)} fusion(f32[64,128,128]{2,1,0:T(8,128)} %get-tuple-element.1951, s32[]{:T(128)S(6)} %select_n.1063, f32[32,7,128]{2,1,0:T(8,128)S(1)} %gather_fusion.13, pred[32]{0:T(512)(128)(4,1)S(1)} %get-tuple-element.1569), kind=kOutput, calls=%fused_computation.223.clone.1 | convolution fusion | flops 22048768 | bytes 2326564 | tf_op jit(solution)/shard_map/while/body/rtb,tab->rta/dot_general | solution.py:248
  (412 shorter events, 38.5 us)
Async XLA Ops:
  0.6 9.1 %copy-start = (s32[9]{0:T(128)S(1)}, s32[9]{0:T(128)}, u32[]{:S(2)}) copy-start(s32[9]{0:T(128)} %constant.531.clone) | copy-start | bytes 112
  5.0 5.5 %copy-start.7 = (pred[320]{0:T(512)(128)(4,1)S(1)}, pred[320]{0:T(512)(128)(4,1)}, u32[]{:S(2)}) copy-start(pred[320]{0:T(512)(128)(4,1)} %constant.503.clone.1) | copy-start | bytes 964
  12.3 9.1 %copy-start.2 = (f32[3,2048]{1,0:T(4,128)S(1)}, f32[3,2048]{1,0:T(4,128)}, u32[]{:S(2)}) copy-start(f32[3,2048]{1,0:T(4,128)} %param.49) | copy-start | bytes 73732
  12.5 9.3 %copy-start.1 = (f32[3,2048]{1,0:T(4,128)S(1)}, f32[3,2048]{1,0:T(4,128)}, u32[]{:S(2)}) copy-start(f32[3,2048]{1,0:T(4,128)} %param.46) | copy-start | bytes 73732
  12.5 10.0 %copy-start.8 = (s32[64]{0:T(128)S(1)}, s32[64]{0:T(128)}, u32[]{:S(2)}) copy-start(s32[64]{0:T(128)} %param.55) | copy-start | bytes 772
  12.5 13.3 %copy-start.3 = (f32[2048]{0:T(1024)S(1)}, f32[2048]{0:T(1024)}, u32[]{:S(2)}) copy-start(f32[2048]{0:T(1024)} %param.47) | copy-start | bytes 24580
  12.5 13.4 %copy-start.4 = (f32[2048]{0:T(1024)S(1)}, f32[2048]{0:T(1024)}, u32[]{:S(2)}) copy-start(f32[2048]{0:T(1024)} %param.50) | copy-start | bytes 24580
  14.1 26.8 %all-to-all-start = ((f32[32,16,320]{2,1,0:T(8,128)}), f32[32,16,320]{2,1,0:T(8,128)S(1)}, u32[]{:S(2)}, u32[]{:S(2)}) async-start(f32[32,16,320]{2,1,0:T(8,128)} %concatenate.203), calls=%async_computation | async-start | bytes 1572864 | tf_op jit(solution)/shard_map/all_to_all | solution.py:145
  21.8 7.7 %copy-start.9 = (s32[64]{0:T(128)S(1)}, s32[64]{0:T(128)}, u32[]{:S(2)}) copy-start(s32[64]{0:T(128)} %param.54) | copy-start | bytes 772
  57.9 3.1 %copy-start.6 = (f32[3,2048]{1,0:T(4,128)S(1)}, f32[3,2048]{1,0:T(4,128)}, u32[]{:S(2)}) copy-start(f32[3,2048]{1,0:T(4,128)} %param.48) | copy-start | bytes 73732
  64.7 10.1 %copy-start.5 = (f32[2048]{0:T(1024)S(1)}, f32[2048]{0:T(1024)}, u32[]{:S(2)}) copy-start(f32[2048]{0:T(1024)} %param.51) | copy-start | bytes 24580
  67.3 16.8 %all-to-all-start.1 = ((f32[32,3,320]{2,1,0:T(4,128)}), f32[32,3,320]{2,1,0:T(4,128)S(1)}, u32[]{:S(2)}, u32[]{:S(2)}) async-start(f32[32,3,320]{2,1,0:T(4,128)} %broadcast_select_fusion.4), calls=%async_computation.1 | async-start | bytes 393216 | tf_op jit(solution)/shard_map/all_to_all | solution.py:145
  94.9 11.9 %all-to-all-start.2 = ((f32[32,3,320]{2,1,0:T(4,128)}), f32[32,3,320]{2,1,0:T(4,128)S(1)}, u32[]{:S(2)}, u32[]{:S(2)}) async-start(f32[32,3,320]{2,1,0:T(4,128)} %broadcast_select_fusion.3), calls=%async_computation.2 | async-start | bytes 393216 | tf_op jit(solution)/shard_map/all_to_all | solution.py:145
  117.8 11.9 %all-to-all-start.3 = ((f32[32,3,320]{2,1,0:T(4,128)}), f32[32,3,320]{2,1,0:T(4,128)S(1)}, u32[]{:S(2)}, u32[]{:S(2)}) async-start(f32[32,3,320]{2,1,0:T(4,128)} %broadcast_select_fusion.2), calls=%async_computation.3 | async-start | bytes 393216 | tf_op jit(solution)/shard_map/all_to_all | solution.py:145
  140.5 11.9 %all-to-all-start.4 = ((f32[32,3,320]{2,1,0:T(4,128)}), f32[32,3,320]{2,1,0:T(4,128)S(1)}, u32[]{:S(2)}, u32[]{:S(2)}) async-start(f32[32,3,320]{2,1,0:T(4,128)} %broadcast_select_fusion.1), calls=%async_computation.4 | async-start | bytes 393216 | tf_op jit(solution)/shard_map/all_to_all | solution.py:145

commit v6 on v5

--- a/solution.py
+++ b/solution.py
@@ -121,7 +121,7 @@
     width = max(sizes)
     nx, ny = (lax.axis_size("gx"), lax.axis_size("gy"))
     ix, iy = (lax.axis_index("gx"), lax.axis_index("gy"))
-    sent = jnp.take(rows, ghost_index, axis=1)
+    sent = jnp.take(rows.T, ghost_index, axis=0).T
     segments = []
     for d in range(8):
         part = sent[:, starts[d] : starts[d] + sizes[d]]

time: 159 us -> 158 us (level)
  no operation moved by 1% of the time
where the time goes in v6:
time: 158 us; the launch traced here: 157 us
  waiting for transfers between devices  42.7 us (27%)
  local copies, waits for them, and re-layouts  41.8 us (26%)
  starting transfers between devices  21.7 us (14%)
  other arithmetic  20.3 us (13%)
  matrix products  19.7 us (12%)
  between operations  10.3 us (7%)
    all_to_all x5, waiting for transfers between devices, spread_ghosts(): incoming = lax.all_to_all(outgoing, ('gx', 'gy'), 0, 0, tiled=True)  42.7 us
    all_to_all x5, starting transfers between devices, spread_ghosts(): incoming = lax.all_to_all(outgoing, ('gx', 'gy'), 0, 0, tiled=True)  21.7 us
    dot_general x5, matrix products, fold_batch(): jnp.einsum('rtb,tab->rta', qsel, weight, precision=lax.Precision.HIGH, pr...  17.8 us
    gather x5, local copies, waits for them, and re-layouts, spread_ghosts(): sent = jnp.take(rows.T, ghost_index, axis=0).T  12 us
    another operation x68, local copies, waits for them, and re-layouts, spread_ghosts(): segments = jnp.stack(segments)  4.7 us
    gather x5, local copies, waits for them, and re-layouts, spread_ghosts(): outgoing = jnp.take(segments, pick, axis=0)  3.32 us
    select_n x6, other arithmetic, spread_ghosts(): outgoing = jnp.take(segments, pick, axis=0)  3.28 us
  transfers between devices with their start and end apart: 5, of which 5 were waited for; matrix products, arithmetic and copies ran while one was open for 5% of the time, Pallas kernels for 0%

profile of v6, /device:TPU:0, one launch (start us, length us, event | category | flops | bytes accessed | tf_op | source)
XLA Modules:
  0.0 157.1 jit_solution(16690236695131580728)
XLA Ops:
  3.6 1.3 fusion.277
  5.0 1.7 %concatenate.202 = f32[15,2048]{1,0:T(8,128)S(1)} concatenate(f32[3,2048]{1,0:T(4,128)} %param.46, f32[1,2048]{1,0:T(1,128)S(1)} %broadcast_in_dim_broadcast_in_dim.3, f32[1,2048]{1,0:T(1,128)} %bitcast.789, f32[3,2048]{1,0:T(4,128)S(1)} %get-tuple-element.781, f32[3,2048]{1,0:T(4,128)} %param.49, f32[1,2048]{1,0:T(1,128)} %bitcast.794, f32[1,2048]{1,0:T(1,128)S(1)} %bitcast.803, ...), dimensions={0} | concatenate | bytes 245760 | tf_op jit(solution)/shard_map/concatenate | solution.py:196
  7.0 2.4 %gather_fusion.15 = f32[1088,15]{1,0:T(8,128)S(1)} fusion(f32[2048,15]{1,0:T(8,128)S(1)} %bitcast.748, s32[2048]{0:T(1024)S(1)} %pad_clamp_fusion.12), kind=kCustom, calls=%fused_computation.23 | custom fusion | bytes 134912 | tf_op jit(solution)/shard_map/jit(_take)/gather | solution.py:124
  12.5 1.6 %concatenate.203 = f32[32,16,320]{2,1,0:T(8,128)} pad(f32[32,15,320]{2,1,0:T(8,128)S(1)} %broadcast_select_fusion, f32[]{:T(128)} %get-tuple-element.764), padding=0_0x0_1x0_0 | pad | bytes 1269764 | tf_op jit(solution)/shard_map/concatenate | solution.py:144
  14.1 7.3 %all-to-all-start = ((f32[32,16,320]{2,1,0:T(8,128)}), f32[32,16,320]{2,1,0:T(8,128)S(1)}, u32[]{:S(2)}, u32[]{:S(2)}) async-start(f32[32,16,320]{2,1,0:T(8,128)} %concatenate.203), calls=%async_computation | async-start | bytes 1572864 | tf_op jit(solution)/shard_map/all_to_all | solution.py:145
  29.6 2.5 %broadcast_in_dim.269 = f32[64,128,128]{2,1,0:T(8,128)} broadcast(f32[]{:T(128)} %constant.507.clone.1), dimensions={} | broadcast | bytes 4194308 | tf_op jit(solution)/shard_map/broadcast_in_dim | solution.py:281
  33.0 7.9 %all-to-all-done = f32[32,16,320]{2,1,0:T(8,128)S(1)} async-done(((f32[32,16,320]{2,1,0:T(8,128)}), f32[32,16,320]{2,1,0:T(8,128)S(1)}, u32[]{:S(2)}, u32[]{:S(2)}) %all-to-all-start) | async-done | bytes 655392 | tf_op jit(solution)/shard_map/all_to_all | solution.py:145
  43.3 2.5 %concatenate.225 = f32[47,3200]{1,0:T(8,128)S(1)} concatenate(f32[4,3200]{1,0:T(4,128)S(1)} %pad_maximum_fusion.13, f32[6,3200]{1,0:T(8,128)S(1)} %get-tuple-element.810, f32[6,3200]{1,0:T(8,128)S(1)} %get-tuple-element.809, f32[6,3200]{1,0:T(8,128)S(1)} %get-tuple-element.808, f32[25,3200]{1,0:T(8,128)S(1)} %pad_maximum_fusion), dimensions={0} | concatenate | bytes 1203200 | tf_op jit(solution)/shard_map/concatenate | solution.py:166
  46.3 0.9 slice_bitcast_fusion.16
  47.2 10.7 %while.105 = (s32[]{:T(128)}, f32[47,16,128]{2,1,0:T(8,128)S(1)}, f32[64,128,128]{2,1,0:T(8,128)}, s32[]{:T(128)}, s32[]{:T(128)}, /*index=5*/s32[96]{0:T(128)S(...) while((s32[]{:T(128)}, f32[47,16,128]{2,1,0:T(8,128)S(1)}, ...), condition=%wide.region_14.16_spmd, body=%wide.region_13.15_spmd.sunk | while | flops 197710208 | bytes 7519764 | solution.py:278
  48.8 3.1 %fusion.377 = f32[64,128,128]{2,1,0:T(8,128)} fusion(f32[64,128,128]{2,1,0:T(8,128)} %get-tuple-element.1630, s32[]{:T(128)S(6)} %select_n.1040, f32[32,128]{1,0:T(8,128)S(1)} %bitcast.763, f32[32,128]{1,0:T(8,128)S(1)} %bitcast.775, f32[32,128]{1,0:T(8,128)S(1)} %bitcast.765, f32[32,128]{1,0:T(8,128)S(1)} %bitcast.777, f32[32,128]{1,0:T(8,128)S(1)} %bitcast.761, ...), kind=kLoop, calls=%fused_computation.61.clone.1 | loop fusion | flops 6291456 | bytes 2195460 | tf_op jit(solution)/shard_map/while/body/dynamic_update_slice | solution.py:275
  52.5 4.4 %fusion.375 = f32[47,32,128]{2,0,1:T(8,128)S(1)} fusion(f32[32,128]{1,0:T(8,128)S(1)} %bitcast.764, f32[32,128]{1,0:T(8,128)S(1)} %bitcast.776, f32[32,128]{1,0:T(8,128)S(1)} %bitcast.766, f32[32,128]{1,0:T(8,128)S(1)} %bitcast.778, f32[32,128]{1,0:T(8,128)S(1)} %bitcast.762, f32[32,128]{1,0:T(8,128)S(1)} %bitcast.774, ...), kind=kOutput, calls=%fused_computation.63.clone.1 | convolution fusion | flops 154333184 | bytes 1638432 | tf_op jit(solution)/shard_map/while/body/rtb,tab->rta/dot_general | solution.py:248
  62.0 2.4 %gather_fusion.17 = f32[1088,3]{1,0:T(8,128)S(1)} fusion(f32[2048,3]{1,0:T(8,128)S(1)} %copy.422, s32[2048]{0:T(1024)S(1)} %pad_clamp_fusion.12), kind=kCustom, calls=%fused_computation.2.clone | custom fusion | bytes 30464 | tf_op jit(solution)/shard_map/jit(_take)/gather | solution.py:124
  67.3 6.6 %all-to-all-start.1 = ((f32[32,3,320]{2,1,0:T(4,128)}), f32[32,3,320]{2,1,0:T(4,128)S(1)}, u32[]{:S(2)}, u32[]{:S(2)}) async-start(f32[32,3,320]{2,1,0:T(4,128)} %broadcast_select_fusion.4), calls=%async_computation.1 | async-start | bytes 393216 | tf_op jit(solution)/shard_map/all_to_all | solution.py:145
  76.1 7.2 %all-to-all-done.1 = f32[32,3,320]{2,1,0:T(4,128)S(1)} async-done(((f32[32,3,320]{2,1,0:T(4,128)}), f32[32,3,320]{2,1,0:T(4,128)S(1)}, u32[]{:S(2)}, u32[]{:S(2)}) %all-to-all-start.1) | async-done | bytes 122912 | tf_op jit(solution)/shard_map/all_to_all | solution.py:145
  83.8 4.4 %while.107 = (s32[]{:T(128)}, f32[7,16,128]{2,1,0:T(8,128)S(1)}, s32[]{:T(128)}, s32[]{:T(128)}, f32[64,128,128]{2,1,0:T(8,128)}, /*index=5*/s32[96]{0:T(128)S(1...) while((s32[]{:T(128)}, f32[7,16,128]{2,1,0:T(8,128)S(1)}, ...), condition=%wide.region_20.26_spmd, body=%wide.region_19.25_spmd.sunk | while | flops 27569352 | bytes 2796316 | solution.py:300
  84.6 3.4 %fusion.388 = f32[7,32,128]{2,0,1:T(8,128)S(1)} fusion(f32[64,128,128]{2,1,0:T(8,128)} %get-tuple-element.1726, s32[]{:T(128)S(6)} %select_n.1045, f32[32,7,128]{2,1,0:T(8,128)S(1)} %gather_fusion.7, pred[32]{0:T(512)(128)(4,1)S(1)} %get-tuple-element.1512), kind=kOutput, calls=%fused_computation.115.clone.1 | convolution fusion | flops 22048768 | bytes 2326564 | tf_op jit(solution)/shard_map/while/body/rtb,tab->rta/dot_general | solution.py:248
  88.7 2.4 %gather_fusion.19 = f32[1088,3]{1,0:T(8,128)S(1)} fusion(f32[2048,3]{1,0:T(8,128)S(1)} %copy.436, s32[2048]{0:T(1024)S(1)} %pad_clamp_fusion.12), kind=kCustom, calls=%fused_computation.13.clone | custom fusion | bytes 30464 | tf_op jit(solution)/shard_map/jit(_take)/gather | solution.py:124
  94.0 2.6 %all-to-all-start.2 = ((f32[32,3,320]{2,1,0:T(4,128)}), f32[32,3,320]{2,1,0:T(4,128)S(1)}, u32[]{:S(2)}, u32[]{:S(2)}) async-start(f32[32,3,320]{2,1,0:T(4,128)} %broadcast_select_fusion.3), calls=%async_computation.2 | async-start | bytes 393216 | tf_op jit(solution)/shard_map/all_to_all | solution.py:145
  96.7 9.2 %all-to-all-done.2 = f32[32,3,320]{2,1,0:T(4,128)S(1)} async-done(((f32[32,3,320]{2,1,0:T(4,128)}), f32[32,3,320]{2,1,0:T(4,128)S(1)}, u32[]{:S(2)}, u32[]{:S(2)}) %all-to-all-start.2) | async-done | bytes 122912 | tf_op jit(solution)/shard_map/all_to_all | solution.py:145
  106.5 4.6 %while.109 = (s32[]{:T(128)}, f32[7,16,128]{2,1,0:T(8,128)S(1)}, s32[]{:T(128)}, s32[]{:T(128)}, f32[64,128,128]{2,1,0:T(8,128)}, /*index=5*/s32[96]{0:T(128)S(1...) while((s32[]{:T(128)}, f32[7,16,128]{2,1,0:T(8,128)S(1)}, ...), condition=%wide.region_26.32_spmd, body=%wide.region_25.31_spmd.sunk | while | flops 27569352 | bytes 2796316 | solution.py:300
  107.2 3.4 %fusion.400 = f32[7,32,128]{2,0,1:T(8,128)S(1)} fusion(f32[64,128,128]{2,1,0:T(8,128)} %get-tuple-element.1801, s32[]{:T(128)S(6)} %select_n.1051, f32[32,7,128]{2,1,0:T(8,128)S(1)} %gather_fusion.9, pred[32]{0:T(512)(128)(4,1)S(1)} %get-tuple-element.1531), kind=kOutput, calls=%fused_computation.151.clone.1 | convolution fusion | flops 22048768 | bytes 2326564 | tf_op jit(solution)/shard_map/while/body/rtb,tab->rta/dot_general | solution.py:248
  111.6 2.4 %gather_fusion.21 = f32[1088,3]{1,0:T(8,128)S(1)} fusion(f32[2048,3]{1,0:T(8,128)S(1)} %copy.450, s32[2048]{0:T(1024)S(1)} %pad_clamp_fusion.12), kind=kCustom, calls=%fused_computation.14.clone | custom fusion | bytes 30464 | tf_op jit(solution)/shard_map/jit(_take)/gather | solution.py:124
  116.9 2.6 %all-to-all-start.3 = ((f32[32,3,320]{2,1,0:T(4,128)}), f32[32,3,320]{2,1,0:T(4,128)S(1)}, u32[]{:S(2)}, u32[]{:S(2)}) async-start(f32[32,3,320]{2,1,0:T(4,128)} %broadcast_select_fusion.2), calls=%async_computation.3 | async-start | bytes 393216 | tf_op jit(solution)/shard_map/all_to_all | solution.py:145
  119.6 9.2 %all-to-all-done.3 = f32[32,3,320]{2,1,0:T(4,128)S(1)} async-done(((f32[32,3,320]{2,1,0:T(4,128)}), f32[32,3,320]{2,1,0:T(4,128)S(1)}, u32[]{:S(2)}, u32[]{:S(2)}) %all-to-all-start.3) | async-done | bytes 122912 | tf_op jit(solution)/shard_map/all_to_all | solution.py:145
  129.4 4.4 %while.111 = (s32[]{:T(128)}, f32[7,16,128]{2,1,0:T(8,128)S(1)}, s32[]{:T(128)}, s32[]{:T(128)}, f32[64,128,128]{2,1,0:T(8,128)}, /*index=5*/s32[96]{0:T(128)S(1...) while((s32[]{:T(128)}, f32[7,16,128]{2,1,0:T(8,128)S(1)}, ...), condition=%wide.region_32.38_spmd, body=%wide.region_31.37_spmd.sunk | while | flops 27569352 | bytes 2796316 | solution.py:300
  130.1 3.4 %fusion.412 = f32[7,32,128]{2,0,1:T(8,128)S(1)} fusion(f32[64,128,128]{2,1,0:T(8,128)} %get-tuple-element.1876, s32[]{:T(128)S(6)} %select_n.1057, f32[32,7,128]{2,1,0:T(8,128)S(1)} %gather_fusion.11, pred[32]{0:T(512)(128)(4,1)S(1)} %get-tuple-element.1550), kind=kOutput, calls=%fused_computation.187.clone.1 | convolution fusion | flops 22048768 | bytes 2326564 | tf_op jit(solution)/shard_map/while/body/rtb,tab->rta/dot_general | solution.py:248
  134.2 2.4 %gather_fusion.23 = f32[1088,3]{1,0:T(8,128)S(1)} fusion(f32[2048,3]{1,0:T(8,128)S(1)} %copy.464, s32[2048]{0:T(1024)S(1)} %pad_clamp_fusion.12), kind=kCustom, calls=%fused_computation.15.clone | custom fusion | bytes 30464 | tf_op jit(solution)/shard_map/jit(_take)/gather | solution.py:124
  139.6 2.6 %all-to-all-start.4 = ((f32[32,3,320]{2,1,0:T(4,128)}), f32[32,3,320]{2,1,0:T(4,128)S(1)}, u32[]{:S(2)}, u32[]{:S(2)}) async-start(f32[32,3,320]{2,1,0:T(4,128)} %broadcast_select_fusion.1), calls=%async_computation.4 | async-start | bytes 393216 | tf_op jit(solution)/shard_map/all_to_all | solution.py:145
  142.2 9.2 %all-to-all-done.4 = f32[32,3,320]{2,1,0:T(4,128)S(1)} async-done(((f32[32,3,320]{2,1,0:T(4,128)}), f32[32,3,320]{2,1,0:T(4,128)S(1)}, u32[]{:S(2)}, u32[]{:S(2)}) %all-to-all-start.4) | async-done | bytes 122912 | tf_op jit(solution)/shard_map/all_to_all | solution.py:145
  152.0 4.4 %while.113 = (s32[]{:T(128)}, f32[7,16,128]{2,1,0:T(8,128)S(1)}, s32[]{:T(128)}, s32[]{:T(128)}, f32[64,128,128]{2,1,0:T(8,128)}, /*index=5*/s32[96]{0:T(128)S(1...) while((s32[]{:T(128)}, f32[7,16,128]{2,1,0:T(8,128)S(1)}, ...), condition=%wide.region_38.44_spmd, body=%wide.region_37.43_spmd.sunk | while | flops 27569352 | bytes 2796316 | solution.py:300
  152.8 3.4 %fusion.424 = f32[7,32,128]{2,0,1:T(8,128)S(1)} fusion(f32[64,128,128]{2,1,0:T(8,128)} %get-tuple-element.1951, s32[]{:T(128)S(6)} %select_n.1063, f32[32,7,128]{2,1,0:T(8,128)S(1)} %gather_fusion.13, pred[32]{0:T(512)(128)(4,1)S(1)} %get-tuple-element.1569), kind=kOutput, calls=%fused_computation.223.clone.1 | convolution fusion | flops 22048768 | bytes 2326564 | tf_op jit(solution)/shard_map/while/body/rtb,tab->rta/dot_general | solution.py:248
  (412 shorter events, 38.4 us)
Async XLA Ops:
  7.0 2.7 %copy-start = (s32[9]{0:T(128)S(1)}, s32[9]{0:T(128)}, u32[]{:S(2)}) copy-start(s32[9]{0:T(128)} %constant.531.clone) | copy-start | bytes 112
  7.0 3.5 %copy-start.7 = (pred[320]{0:T(512)(128)(4,1)S(1)}, pred[320]{0:T(512)(128)(4,1)}, u32[]{:S(2)}) copy-start(pred[320]{0:T(512)(128)(4,1)} %constant.503.clone.1) | copy-start | bytes 964
  12.3 9.1 %copy-start.2 = (f32[3,2048]{1,0:T(4,128)S(1)}, f32[3,2048]{1,0:T(4,128)}, u32[]{:S(2)}) copy-start(f32[3,2048]{1,0:T(4,128)} %param.49) | copy-start | bytes 73732
  12.5 9.3 %copy-start.1 = (f32[3,2048]{1,0:T(4,128)S(1)}, f32[3,2048]{1,0:T(4,128)}, u32[]{:S(2)}) copy-start(f32[3,2048]{1,0:T(4,128)} %param.46) | copy-start | bytes 73732
  12.5 10.0 %copy-start.8 = (s32[64]{0:T(128)S(1)}, s32[64]{0:T(128)}, u32[]{:S(2)}) copy-start(s32[64]{0:T(128)} %param.55) | copy-start | bytes 772
  12.5 13.3 %copy-start.3 = (f32[2048]{0:T(1024)S(1)}, f32[2048]{0:T(1024)}, u32[]{:S(2)}) copy-start(f32[2048]{0:T(1024)} %param.47) | copy-start | bytes 24580
  12.5 13.4 %copy-start.4 = (f32[2048]{0:T(1024)S(1)}, f32[2048]{0:T(1024)}, u32[]{:S(2)}) copy-start(f32[2048]{0:T(1024)} %param.50) | copy-start | bytes 24580
  14.1 26.8 %all-to-all-start = ((f32[32,16,320]{2,1,0:T(8,128)}), f32[32,16,320]{2,1,0:T(8,128)S(1)}, u32[]{:S(2)}, u32[]{:S(2)}) async-start(f32[32,16,320]{2,1,0:T(8,128)} %concatenate.203), calls=%async_computation | async-start | bytes 1572864 | tf_op jit(solution)/shard_map/all_to_all | solution.py:145
  21.8 7.7 %copy-start.9 = (s32[64]{0:T(128)S(1)}, s32[64]{0:T(128)}, u32[]{:S(2)}) copy-start(s32[64]{0:T(128)} %param.54) | copy-start | bytes 772
  57.9 3.1 %copy-start.6 = (f32[3,2048]{1,0:T(4,128)S(1)}, f32[3,2048]{1,0:T(4,128)}, u32[]{:S(2)}) copy-start(f32[3,2048]{1,0:T(4,128)} %param.48) | copy-start | bytes 73732
  64.7 9.2 %copy-start.5 = (f32[2048]{0:T(1024)S(1)}, f32[2048]{0:T(1024)}, u32[]{:S(2)}) copy-start(f32[2048]{0:T(1024)} %param.51) | copy-start | bytes 24580
  67.3 15.9 %all-to-all-start.1 = ((f32[32,3,320]{2,1,0:T(4,128)}), f32[32,3,320]{2,1,0:T(4,128)S(1)}, u32[]{:S(2)}, u32[]{:S(2)}) async-start(f32[32,3,320]{2,1,0:T(4,128)} %broadcast_select_fusion.4), calls=%async_computation.1 | async-start | bytes 393216 | tf_op jit(solution)/shard_map/all_to_all | solution.py:145
  94.0 11.9 %all-to-all-start.2 = ((f32[32,3,320]{2,1,0:T(4,128)}), f32[32,3,320]{2,1,0:T(4,128)S(1)}, u32[]{:S(2)}, u32[]{:S(2)}) async-start(f32[32,3,320]{2,1,0:T(4,128)} %broadcast_select_fusion.3), calls=%async_computation.2 | async-start | bytes 393216 | tf_op jit(solution)/shard_map/all_to_all | solution.py:145
  116.9 11.9 %all-to-all-start.3 = ((f32[32,3,320]{2,1,0:T(4,128)}), f32[32,3,320]{2,1,0:T(4,128)S(1)}, u32[]{:S(2)}, u32[]{:S(2)}) async-start(f32[32,3,320]{2,1,0:T(4,128)} %broadcast_select_fusion.2), calls=%async_computation.3 | async-start | bytes 393216 | tf_op jit(solution)/shard_map/all_to_all | solution.py:145
  139.6 11.9 %all-to-all-start.4 = ((f32[32,3,320]{2,1,0:T(4,128)}), f32[32,3,320]{2,1,0:T(4,128)S(1)}, u32[]{:S(2)}, u32[]{:S(2)}) async-start(f32[32,3,320]{2,1,0:T(4,128)} %broadcast_select_fusion.1), calls=%async_computation.4 | async-start | bytes 393216 | tf_op jit(solution)/shard_map/all_to_all | solution.py:145

commit v7 on v6

--- a/solution.py
+++ b/solution.py
@@ -256,7 +256,7 @@
             "pt,rta->rpa",
             onehot,
             part,
-            precision=lax.Precision.HIGHEST,
+            precision=lax.Precision.HIGH,
             preferred_element_type=jnp.float32,
         )
 

time: 158 us -> 159 us (level)
  no operation moved by 1% of the time
where the time goes in v7:
time: 159 us; the launch traced here: 158 us
  waiting for transfers between devices  42.7 us (27%)
  local copies, waits for them, and re-layouts  41.8 us (26%)
  starting transfers between devices  22.4 us (14%)
  other arithmetic  20.3 us (13%)
  matrix products  19.3 us (12%)
  between operations  10.3 us (6%)
    all_to_all x5, waiting for transfers between devices, spread_ghosts(): incoming = lax.all_to_all(outgoing, ('gx', 'gy'), 0, 0, tiled=True)  42.7 us
    all_to_all x5, starting transfers between devices, spread_ghosts(): incoming = lax.all_to_all(outgoing, ('gx', 'gy'), 0, 0, tiled=True)  22.4 us
    dot_general x5, matrix products, fold_batch(): jnp.einsum('rtb,tab->rta', qsel, weight, precision=lax.Precision.HIGH, pr...  17.8 us
    gather x5, local copies, waits for them, and re-layouts, spread_ghosts(): sent = jnp.take(rows.T, ghost_index, axis=0).T  12 us
    another operation x68, local copies, waits for them, and re-layouts, spread_ghosts(): segments = jnp.stack(segments)  4.7 us
    gather x5, local copies, waits for them, and re-layouts, spread_ghosts(): outgoing = jnp.take(segments, pick, axis=0)  3.32 us
    select_n x6, other arithmetic, spread_ghosts(): outgoing = jnp.take(segments, pick, axis=0)  3.28 us
  transfers between devices with their start and end apart: 5, of which 5 were waited for; matrix products, arithmetic and copies ran while one was open for 5% of the time, Pallas kernels for 0%

profile of v7, /device:TPU:0, one launch (start us, length us, event | category | flops | bytes accessed | tf_op | source)
XLA Modules:
  0.0 157.5 jit_solution(7083112116248656814)
XLA Ops:
  3.6 1.3 fusion.277
  5.0 1.7 %concatenate.202 = f32[15,2048]{1,0:T(8,128)S(1)} concatenate(f32[3,2048]{1,0:T(4,128)} %param.46, f32[1,2048]{1,0:T(1,128)S(1)} %broadcast_in_dim_broadcast_in_dim.3, f32[1,2048]{1,0:T(1,128)} %bitcast.789, f32[3,2048]{1,0:T(4,128)S(1)} %get-tuple-element.781, f32[3,2048]{1,0:T(4,128)} %param.49, f32[1,2048]{1,0:T(1,128)} %bitcast.794, f32[1,2048]{1,0:T(1,128)S(1)} %bitcast.803, ...), dimensions={0} | concatenate | bytes 245760 | tf_op jit(solution)/shard_map/concatenate | solution.py:196
  7.0 2.4 %gather_fusion.15 = f32[1088,15]{1,0:T(8,128)S(1)} fusion(f32[2048,15]{1,0:T(8,128)S(1)} %bitcast.748, s32[2048]{0:T(1024)S(1)} %pad_clamp_fusion.12), kind=kCustom, calls=%fused_computation.23 | custom fusion | bytes 134912 | tf_op jit(solution)/shard_map/jit(_take)/gather | solution.py:124
  12.5 1.6 %concatenate.203 = f32[32,16,320]{2,1,0:T(8,128)} pad(f32[32,15,320]{2,1,0:T(8,128)S(1)} %broadcast_select_fusion, f32[]{:T(128)} %get-tuple-element.764), padding=0_0x0_1x0_0 | pad | bytes 1269764 | tf_op jit(solution)/shard_map/concatenate | solution.py:144
  14.1 7.3 %all-to-all-start = ((f32[32,16,320]{2,1,0:T(8,128)}), f32[32,16,320]{2,1,0:T(8,128)S(1)}, u32[]{:S(2)}, u32[]{:S(2)}) async-start(f32[32,16,320]{2,1,0:T(8,128)} %concatenate.203), calls=%async_computation | async-start | bytes 1572864 | tf_op jit(solution)/shard_map/all_to_all | solution.py:145
  29.6 2.5 %broadcast_in_dim.269 = f32[64,128,128]{2,1,0:T(8,128)} broadcast(f32[]{:T(128)} %constant.507.clone.1), dimensions={} | broadcast | bytes 4194308 | tf_op jit(solution)/shard_map/broadcast_in_dim | solution.py:281
  33.0 7.9 %all-to-all-done = f32[32,16,320]{2,1,0:T(8,128)S(1)} async-done(((f32[32,16,320]{2,1,0:T(8,128)}), f32[32,16,320]{2,1,0:T(8,128)S(1)}, u32[]{:S(2)}, u32[]{:S(2)}) %all-to-all-start) | async-done | bytes 655392 | tf_op jit(solution)/shard_map/all_to_all | solution.py:145
  43.3 2.5 %concatenate.225 = f32[47,3200]{1,0:T(8,128)S(1)} concatenate(f32[4,3200]{1,0:T(4,128)S(1)} %pad_maximum_fusion.13, f32[6,3200]{1,0:T(8,128)S(1)} %get-tuple-element.810, f32[6,3200]{1,0:T(8,128)S(1)} %get-tuple-element.809, f32[6,3200]{1,0:T(8,128)S(1)} %get-tuple-element.808, f32[25,3200]{1,0:T(8,128)S(1)} %pad_maximum_fusion), dimensions={0} | concatenate | bytes 1203200 | tf_op jit(solution)/shard_map/concatenate | solution.py:166
  46.3 0.9 slice_bitcast_fusion.16
  47.2 10.5 %while.105 = (s32[]{:T(128)}, f32[47,16,128]{2,1,0:T(8,128)S(1)}, f32[64,128,128]{2,1,0:T(8,128)}, s32[]{:T(128)}, s32[]{:T(128)}, /*index=5*/s32[96]{0:T(128)S(...) while((s32[]{:T(128)}, f32[47,16,128]{2,1,0:T(8,128)S(1)}, ...), condition=%wide.region_14.16_spmd, body=%wide.region_13.15_spmd.sunk | while | flops 179229056 | bytes 7519764 | solution.py:278
  48.8 3.1 %fusion.377 = f32[64,128,128]{2,1,0:T(8,128)} fusion(f32[64,128,128]{2,1,0:T(8,128)} %get-tuple-element.1630, s32[]{:T(128)S(6)} %select_n.1040, f32[32,128]{1,0:T(8,128)S(1)} %bitcast.763, f32[32,128]{1,0:T(8,128)S(1)} %bitcast.775, f32[32,128]{1,0:T(8,128)S(1)} %bitcast.765, f32[32,128]{1,0:T(8,128)S(1)} %bitcast.777, f32[32,128]{1,0:T(8,128)S(1)} %bitcast.761, ...), kind=kLoop, calls=%fused_computation.61.clone.1 | loop fusion | flops 6291456 | bytes 2195460 | tf_op jit(solution)/shard_map/while/body/dynamic_update_slice | solution.py:275
  52.5 4.4 %fusion.375 = f32[47,32,128]{2,0,1:T(8,128)S(1)} fusion(f32[32,128]{1,0:T(8,128)S(1)} %bitcast.764, f32[32,128]{1,0:T(8,128)S(1)} %bitcast.776, f32[32,128]{1,0:T(8,128)S(1)} %bitcast.766, f32[32,128]{1,0:T(8,128)S(1)} %bitcast.778, f32[32,128]{1,0:T(8,128)S(1)} %bitcast.762, f32[32,128]{1,0:T(8,128)S(1)} %bitcast.774, ...), kind=kOutput, calls=%fused_computation.63.clone.1 | convolution fusion | flops 154333184 | bytes 1638432 | tf_op jit(solution)/shard_map/while/body/rtb,tab->rta/dot_general | solution.py:248
  61.8 2.4 %gather_fusion.17 = f32[1088,3]{1,0:T(8,128)S(1)} fusion(f32[2048,3]{1,0:T(8,128)S(1)} %copy.422, s32[2048]{0:T(1024)S(1)} %pad_clamp_fusion.12), kind=kCustom, calls=%fused_computation.2.clone | custom fusion | bytes 30464 | tf_op jit(solution)/shard_map/jit(_take)/gather | solution.py:124
  67.1 7.3 %all-to-all-start.1 = ((f32[32,3,320]{2,1,0:T(4,128)}), f32[32,3,320]{2,1,0:T(4,128)S(1)}, u32[]{:S(2)}, u32[]{:S(2)}) async-start(f32[32,3,320]{2,1,0:T(4,128)} %broadcast_select_fusion.4), calls=%async_computation.1 | async-start | bytes 393216 | tf_op jit(solution)/shard_map/all_to_all | solution.py:145
  76.6 7.2 %all-to-all-done.1 = f32[32,3,320]{2,1,0:T(4,128)S(1)} async-done(((f32[32,3,320]{2,1,0:T(4,128)}), f32[32,3,320]{2,1,0:T(4,128)S(1)}, u32[]{:S(2)}, u32[]{:S(2)}) %all-to-all-start.1) | async-done | bytes 122912 | tf_op jit(solution)/shard_map/all_to_all | solution.py:145
  84.4 4.3 %while.107 = (s32[]{:T(128)}, f32[7,16,128]{2,1,0:T(8,128)S(1)}, s32[]{:T(128)}, s32[]{:T(128)}, f32[64,128,128]{2,1,0:T(8,128)}, /*index=5*/s32[96]{0:T(128)S(1...) while((s32[]{:T(128)}, f32[7,16,128]{2,1,0:T(8,128)S(1)}, ...), condition=%wide.region_20.26_spmd, body=%wide.region_19.25_spmd.sunk | while | flops 24816840 | bytes 2796316 | solution.py:300
  85.1 3.4 %fusion.388 = f32[7,32,128]{2,0,1:T(8,128)S(1)} fusion(f32[64,128,128]{2,1,0:T(8,128)} %get-tuple-element.1726, s32[]{:T(128)S(6)} %select_n.1045, f32[32,7,128]{2,1,0:T(8,128)S(1)} %gather_fusion.7, pred[32]{0:T(512)(128)(4,1)S(1)} %get-tuple-element.1512), kind=kOutput, calls=%fused_computation.115.clone.1 | convolution fusion | flops 22048768 | bytes 2326564 | tf_op jit(solution)/shard_map/while/body/rtb,tab->rta/dot_general | solution.py:248
  89.2 2.4 %gather_fusion.19 = f32[1088,3]{1,0:T(8,128)S(1)} fusion(f32[2048,3]{1,0:T(8,128)S(1)} %copy.436, s32[2048]{0:T(1024)S(1)} %pad_clamp_fusion.12), kind=kCustom, calls=%fused_computation.13.clone | custom fusion | bytes 30464 | tf_op jit(solution)/shard_map/jit(_take)/gather | solution.py:124
  94.5 2.6 %all-to-all-start.2 = ((f32[32,3,320]{2,1,0:T(4,128)}), f32[32,3,320]{2,1,0:T(4,128)S(1)}, u32[]{:S(2)}, u32[]{:S(2)}) async-start(f32[32,3,320]{2,1,0:T(4,128)} %broadcast_select_fusion.3), calls=%async_computation.2 | async-start | bytes 393216 | tf_op jit(solution)/shard_map/all_to_all | solution.py:145
  97.2 9.2 %all-to-all-done.2 = f32[32,3,320]{2,1,0:T(4,128)S(1)} async-done(((f32[32,3,320]{2,1,0:T(4,128)}), f32[32,3,320]{2,1,0:T(4,128)S(1)}, u32[]{:S(2)}, u32[]{:S(2)}) %all-to-all-start.2) | async-done | bytes 122912 | tf_op jit(solution)/shard_map/all_to_all | solution.py:145
  107.0 4.5 %while.109 = (s32[]{:T(128)}, f32[7,16,128]{2,1,0:T(8,128)S(1)}, s32[]{:T(128)}, s32[]{:T(128)}, f32[64,128,128]{2,1,0:T(8,128)}, /*index=5*/s32[96]{0:T(128)S(1...) while((s32[]{:T(128)}, f32[7,16,128]{2,1,0:T(8,128)S(1)}, ...), condition=%wide.region_26.32_spmd, body=%wide.region_25.31_spmd.sunk | while | flops 24816840 | bytes 2796316 | solution.py:300
  107.7 3.4 %fusion.400 = f32[7,32,128]{2,0,1:T(8,128)S(1)} fusion(f32[64,128,128]{2,1,0:T(8,128)} %get-tuple-element.1801, s32[]{:T(128)S(6)} %select_n.1051, f32[32,7,128]{2,1,0:T(8,128)S(1)} %gather_fusion.9, pred[32]{0:T(512)(128)(4,1)S(1)} %get-tuple-element.1531), kind=kOutput, calls=%fused_computation.151.clone.1 | convolution fusion | flops 22048768 | bytes 2326564 | tf_op jit(solution)/shard_map/while/body/rtb,tab->rta/dot_general | solution.py:248
  112.0 2.4 %gather_fusion.21 = f32[1088,3]{1,0:T(8,128)S(1)} fusion(f32[2048,3]{1,0:T(8,128)S(1)} %copy.450, s32[2048]{0:T(1024)S(1)} %pad_clamp_fusion.12), kind=kCustom, calls=%fused_computation.14.clone | custom fusion | bytes 30464 | tf_op jit(solution)/shard_map/jit(_take)/gather | solution.py:124
  117.4 2.6 %all-to-all-start.3 = ((f32[32,3,320]{2,1,0:T(4,128)}), f32[32,3,320]{2,1,0:T(4,128)S(1)}, u32[]{:S(2)}, u32[]{:S(2)}) async-start(f32[32,3,320]{2,1,0:T(4,128)} %broadcast_select_fusion.2), calls=%async_computation.3 | async-start | bytes 393216 | tf_op jit(solution)/shard_map/all_to_all | solution.py:145
  120.1 9.2 %all-to-all-done.3 = f32[32,3,320]{2,1,0:T(4,128)S(1)} async-done(((f32[32,3,320]{2,1,0:T(4,128)}), f32[32,3,320]{2,1,0:T(4,128)S(1)}, u32[]{:S(2)}, u32[]{:S(2)}) %all-to-all-start.3) | async-done | bytes 122912 | tf_op jit(solution)/shard_map/all_to_all | solution.py:145
  129.8 4.3 %while.111 = (s32[]{:T(128)}, f32[7,16,128]{2,1,0:T(8,128)S(1)}, s32[]{:T(128)}, s32[]{:T(128)}, f32[64,128,128]{2,1,0:T(8,128)}, /*index=5*/s32[96]{0:T(128)S(1...) while((s32[]{:T(128)}, f32[7,16,128]{2,1,0:T(8,128)S(1)}, ...), condition=%wide.region_32.38_spmd, body=%wide.region_31.37_spmd.sunk | while | flops 24816840 | bytes 2796316 | solution.py:300
  130.6 3.4 %fusion.412 = f32[7,32,128]{2,0,1:T(8,128)S(1)} fusion(f32[64,128,128]{2,1,0:T(8,128)} %get-tuple-element.1876, s32[]{:T(128)S(6)} %select_n.1057, f32[32,7,128]{2,1,0:T(8,128)S(1)} %gather_fusion.11, pred[32]{0:T(512)(128)(4,1)S(1)} %get-tuple-element.1550), kind=kOutput, calls=%fused_computation.187.clone.1 | convolution fusion | flops 22048768 | bytes 2326564 | tf_op jit(solution)/shard_map/while/body/rtb,tab->rta/dot_general | solution.py:248
  134.7 2.4 %gather_fusion.23 = f32[1088,3]{1,0:T(8,128)S(1)} fusion(f32[2048,3]{1,0:T(8,128)S(1)} %copy.464, s32[2048]{0:T(1024)S(1)} %pad_clamp_fusion.12), kind=kCustom, calls=%fused_computation.15.clone | custom fusion | bytes 30464 | tf_op jit(solution)/shard_map/jit(_take)/gather | solution.py:124
  140.0 2.6 %all-to-all-start.4 = ((f32[32,3,320]{2,1,0:T(4,128)}), f32[32,3,320]{2,1,0:T(4,128)S(1)}, u32[]{:S(2)}, u32[]{:S(2)}) async-start(f32[32,3,320]{2,1,0:T(4,128)} %broadcast_select_fusion.1), calls=%async_computation.4 | async-start | bytes 393216 | tf_op jit(solution)/shard_map/all_to_all | solution.py:145
  142.7 9.2 %all-to-all-done.4 = f32[32,3,320]{2,1,0:T(4,128)S(1)} async-done(((f32[32,3,320]{2,1,0:T(4,128)}), f32[32,3,320]{2,1,0:T(4,128)S(1)}, u32[]{:S(2)}, u32[]{:S(2)}) %all-to-all-start.4) | async-done | bytes 122912 | tf_op jit(solution)/shard_map/all_to_all | solution.py:145
  152.5 4.3 %while.113 = (s32[]{:T(128)}, f32[7,16,128]{2,1,0:T(8,128)S(1)}, s32[]{:T(128)}, s32[]{:T(128)}, f32[64,128,128]{2,1,0:T(8,128)}, /*index=5*/s32[96]{0:T(128)S(1...) while((s32[]{:T(128)}, f32[7,16,128]{2,1,0:T(8,128)S(1)}, ...), condition=%wide.region_38.44_spmd, body=%wide.region_37.43_spmd.sunk | while | flops 24816840 | bytes 2796316 | solution.py:300
  153.2 3.4 %fusion.424 = f32[7,32,128]{2,0,1:T(8,128)S(1)} fusion(f32[64,128,128]{2,1,0:T(8,128)} %get-tuple-element.1951, s32[]{:T(128)S(6)} %select_n.1063, f32[32,7,128]{2,1,0:T(8,128)S(1)} %gather_fusion.13, pred[32]{0:T(512)(128)(4,1)S(1)} %get-tuple-element.1569), kind=kOutput, calls=%fused_computation.223.clone.1 | convolution fusion | flops 22048768 | bytes 2326564 | tf_op jit(solution)/shard_map/while/body/rtb,tab->rta/dot_general | solution.py:248
  (412 shorter events, 38.1 us)
Async XLA Ops:
  7.0 2.7 %copy-start = (s32[9]{0:T(128)S(1)}, s32[9]{0:T(128)}, u32[]{:S(2)}) copy-start(s32[9]{0:T(128)} %constant.531.clone) | copy-start | bytes 112
  7.0 3.5 %copy-start.7 = (pred[320]{0:T(512)(128)(4,1)S(1)}, pred[320]{0:T(512)(128)(4,1)}, u32[]{:S(2)}) copy-start(pred[320]{0:T(512)(128)(4,1)} %constant.503.clone.1) | copy-start | bytes 964
  12.3 9.1 %copy-start.2 = (f32[3,2048]{1,0:T(4,128)S(1)}, f32[3,2048]{1,0:T(4,128)}, u32[]{:S(2)}) copy-start(f32[3,2048]{1,0:T(4,128)} %param.49) | copy-start | bytes 73732
  12.5 9.3 %copy-start.1 = (f32[3,2048]{1,0:T(4,128)S(1)}, f32[3,2048]{1,0:T(4,128)}, u32[]{:S(2)}) copy-start(f32[3,2048]{1,0:T(4,128)} %param.46) | copy-start | bytes 73732
  12.5 10.0 %copy-start.8 = (s32[64]{0:T(128)S(1)}, s32[64]{0:T(128)}, u32[]{:S(2)}) copy-start(s32[64]{0:T(128)} %param.55) | copy-start | bytes 772
  12.5 13.3 %copy-start.3 = (f32[2048]{0:T(1024)S(1)}, f32[2048]{0:T(1024)}, u32[]{:S(2)}) copy-start(f32[2048]{0:T(1024)} %param.47) | copy-start | bytes 24580
  12.5 13.4 %copy-start.4 = (f32[2048]{0:T(1024)S(1)}, f32[2048]{0:T(1024)}, u32[]{:S(2)}) copy-start(f32[2048]{0:T(1024)} %param.50) | copy-start | bytes 24580
  14.1 26.8 %all-to-all-start = ((f32[32,16,320]{2,1,0:T(8,128)}), f32[32,16,320]{2,1,0:T(8,128)S(1)}, u32[]{:S(2)}, u32[]{:S(2)}) async-start(f32[32,16,320]{2,1,0:T(8,128)} %concatenate.203), calls=%async_computation | async-start | bytes 1572864 | tf_op jit(solution)/shard_map/all_to_all | solution.py:145
  21.8 7.7 %copy-start.9 = (s32[64]{0:T(128)S(1)}, s32[64]{0:T(128)}, u32[]{:S(2)}) copy-start(s32[64]{0:T(128)} %param.54) | copy-start | bytes 772
  57.7 3.1 %copy-start.6 = (f32[3,2048]{1,0:T(4,128)S(1)}, f32[3,2048]{1,0:T(4,128)}, u32[]{:S(2)}) copy-start(f32[3,2048]{1,0:T(4,128)} %param.48) | copy-start | bytes 73732
  64.5 9.9 %copy-start.5 = (f32[2048]{0:T(1024)S(1)}, f32[2048]{0:T(1024)}, u32[]{:S(2)}) copy-start(f32[2048]{0:T(1024)} %param.51) | copy-start | bytes 24580
  67.1 16.6 %all-to-all-start.1 = ((f32[32,3,320]{2,1,0:T(4,128)}), f32[32,3,320]{2,1,0:T(4,128)S(1)}, u32[]{:S(2)}, u32[]{:S(2)}) async-start(f32[32,3,320]{2,1,0:T(4,128)} %broadcast_select_fusion.4), calls=%async_computation.1 | async-start | bytes 393216 | tf_op jit(solution)/shard_map/all_to_all | solution.py:145
  94.5 11.9 %all-to-all-start.2 = ((f32[32,3,320]{2,1,0:T(4,128)}), f32[32,3,320]{2,1,0:T(4,128)S(1)}, u32[]{:S(2)}, u32[]{:S(2)}) async-start(f32[32,3,320]{2,1,0:T(4,128)} %broadcast_select_fusion.3), calls=%async_computation.2 | async-start | bytes 393216 | tf_op jit(solution)/shard_map/all_to_all | solution.py:145
  117.4 11.9 %all-to-all-start.3 = ((f32[32,3,320]{2,1,0:T(4,128)}), f32[32,3,320]{2,1,0:T(4,128)S(1)}, u32[]{:S(2)}, u32[]{:S(2)}) async-start(f32[32,3,320]{2,1,0:T(4,128)} %broadcast_select_fusion.2), calls=%async_computation.3 | async-start | bytes 393216 | tf_op jit(solution)/shard_map/all_to_all | solution.py:145
  140.0 11.9 %all-to-all-start.4 = ((f32[32,3,320]{2,1,0:T(4,128)}), f32[32,3,320]{2,1,0:T(4,128)S(1)}, u32[]{:S(2)}, u32[]{:S(2)}) async-start(f32[32,3,320]{2,1,0:T(4,128)} %broadcast_select_fusion.1), calls=%async_computation.4 | async-start | bytes 393216 | tf_op jit(solution)/shard_map/all_to_all | solution.py:145

commit v8 on v6

--- a/solution.py
+++ b/solution.py
@@ -195,7 +195,14 @@
     core_rows = [positions, live[None], density[None], velocity, field, psi[None], speed[None]]
     payload = jnp.concatenate(core_rows + [ohmic[None], fac[None]], axis=0)
     qlocal = flux_rows(payload)
-    ghosts, ch = spread_ghosts(payload, ghost_index, jnp.max(speed))
+    sendable = jnp.concatenate([payload[0:3], payload[4:12], payload[13:15]], axis=0)
+    got, ch = spread_ghosts(sendable, ghost_index, jnp.max(speed))
+    real = got[3] > 0.0
+    safe_rho = jnp.where(real, got[3], 1.0)
+    ghost_speed = jnp.where(real, jnp.sqrt(1.0 + jnp.sum(got[7:10] * got[7:10], axis=0) / safe_rho), 0.0)
+    ghosts = jnp.concatenate(
+        [got[0:3], real.astype(jnp.float32)[None], got[3:11], ghost_speed[None], got[11:13]], axis=0
+    )
     dt = courant / ch
     ext = extend(payload, ghosts)
     pos_blocks = ext[0:3].reshape(3, EXT_BLOCKS, TILE)

time: 158 us -> 164 us (1.038)
  starting transfers between devices: 21.7 us -> 26.8 us
  waiting for transfers between devices: 42.7 us -> 38.7 us
  other arithmetic: 20.3 us -> 22.8 us
  local copies, waits for them, and re-layouts: 41.8 us -> 43.7 us
    all_to_all x5, starting transfers between devices: 21.7 us -> 26.8 us  [spread_ghosts(): incoming = lax.all_to_all(outgoing, ('gx', 'gy'), 0, 0, tiled=True)]
    all_to_all x5, waiting for transfers between devices: 42.7 us -> 38.7 us  [spread_ghosts(): incoming = lax.all_to_all(outgoing, ('gx', 'gy'), 0, 0, tiled=True)]
    concatenate x0 -> x3, local copies, waits for them, and re-layouts: none -> 2.98 us  [the longest x2 2.81 us: shards(): jnp.concatenate([payload[0:3], payload[4:12], payload[13:15]], axis=0)]
  transfers between devices with their start and end apart: 5 -> 5, of which waited for: 5 -> 5; matrix products, arithmetic and copies ran while one was open for 5% -> 7% of each run, Pallas kernels for 0% -> 0%
where the time goes in v8:
time: 164 us; the launch traced here: 163 us
  local copies, waits for them, and re-layouts  43.7 us (27%)
  waiting for transfers between devices  38.7 us (24%)
  starting transfers between devices  26.8 us (16%)
  other arithmetic  22.8 us (14%)
  matrix products  19.7 us (12%)
  between operations  10.7 us (7%)
    all_to_all x5, waiting for transfers between devices, spread_ghosts(): incoming = lax.all_to_all(outgoing, ('gx', 'gy'), 0, 0, tiled=True)  38.7 us
    all_to_all x5, starting transfers between devices, spread_ghosts(): incoming = lax.all_to_all(outgoing, ('gx', 'gy'), 0, 0, tiled=True)  26.8 us
    dot_general x5, matrix products, fold_batch(): jnp.einsum('rtb,tab->rta', qsel, weight, precision=lax.Precision.HIGH, pr...  17.8 us
    gather x5, local copies, waits for them, and re-layouts, spread_ghosts(): sent = jnp.take(rows.T, ghost_index, axis=0).T  12 us
    another operation x68, local copies, waits for them, and re-layouts, spread_ghosts(): segments = jnp.stack(segments)  4.7 us
    gather x5, local copies, waits for them, and re-layouts, spread_ghosts(): outgoing = jnp.take(segments, pick, axis=0)  3.32 us
  transfers between devices with their start and end apart: 5, of which 5 were waited for; matrix products, arithmetic and copies ran while one was open for 7% of the time, Pallas kernels for 0%

profile of v8, /device:TPU:0, one launch (start us, length us, event | category | flops | bytes accessed | tf_op | source)
XLA Modules:
  0.0 163.1 jit_solution(5907450131452623234)
XLA Ops:
  3.6 1.3 fusion.280
  5.0 2.5 %concatenate.210 = f32[13,2048]{1,0:T(8,128)S(1)} concatenate(f32[3,2048]{1,0:T(4,128)} %param.46, f32[1,2048]{1,0:T(1,128)} %bitcast.790, f32[3,2048]{1,0:T(4,128)S(1)} %get-tuple-element.781, f32[3,2048]{1,0:T(4,128)} %param.49, f32[1,2048]{1,0:T(1,128)} %bitcast.796, f32[1,2048]{1,0:T(1,128)} %bitcast.815, f32[1,2048]{1,0:T(1,128)S(1)} %bitcast.809), dimensions={0} | concatenate | bytes 212992 | tf_op jit(solution)/shard_map/concatenate | solution.py:198
  7.8 2.4 %gather_fusion.15 = f32[1088,13]{1,0:T(8,128)S(1)} fusion(f32[2048,13]{1,0:T(8,128)S(1)} %bitcast.748, s32[2048]{0:T(1024)S(1)} %pad_clamp_fusion.12), kind=kCustom, calls=%fused_computation.23 | custom fusion | bytes 117504 | tf_op jit(solution)/shard_map/jit(_take)/gather | solution.py:124
  13.9 1.6 concatenate.211
  15.5 7.3 %all-to-all-start = ((f32[32,14,320]{2,1,0:T(8,128)}), f32[32,14,320]{2,1,0:T(8,128)S(1)}, u32[]{:S(2)}, u32[]{:S(2)}) async-start(f32[32,14,320]{2,1,0:T(8,128)} %concatenate.211), calls=%async_computation | async-start | bytes 1572864 | tf_op jit(solution)/shard_map/all_to_all | solution.py:145
  32.5 2.5 %broadcast_in_dim.275 = f32[64,128,128]{2,1,0:T(8,128)} broadcast(f32[]{:T(128)} %constant.510.clone.1), dimensions={} | broadcast | bytes 4194308 | tf_op jit(solution)/shard_map/broadcast_in_dim | solution.py:288
  35.7 1.4 concatenate.226
  38.5 3.8 %all-to-all-done = f32[32,14,320]{2,1,0:T(8,128)S(1)} async-done(((f32[32,14,320]{2,1,0:T(8,128)}), f32[32,14,320]{2,1,0:T(8,128)S(1)}, u32[]{:S(2)}, u32[]{:S(2)}) %all-to-all-start) | async-done | bytes 573472 | tf_op jit(solution)/shard_map/all_to_all | solution.py:145
  44.0 2.5 %concatenate.236 = f32[47,3200]{1,0:T(8,128)S(1)} concatenate(f32[4,3200]{1,0:T(4,128)S(1)} %pad_maximum_fusion.13, f32[6,3200]{1,0:T(8,128)S(1)} %get-tuple-element.810, f32[6,3200]{1,0:T(8,128)S(1)} %get-tuple-element.809, f32[6,3200]{1,0:T(8,128)S(1)} %get-tuple-element.808, f32[25,3200]{1,0:T(8,128)S(1)} %pad_maximum_fusion), dimensions={0} | concatenate | bytes 1203200 | tf_op jit(solution)/shard_map/concatenate | solution.py:166
  47.3 11.3 %while.105 = (s32[]{:T(128)}, f32[47,16,128]{2,1,0:T(8,128)S(1)}, f32[64,128,128]{2,1,0:T(8,128)}, s32[]{:T(128)}, s32[]{:T(128)}, /*index=5*/s32[96]{0:T(128)},...) while((s32[]{:T(128)}, f32[47,16,128]{2,1,0:T(8,128)S(1)}, ...), condition=%wide.region_15.17_spmd, body=%wide.region_14.16_spmd.sunk | while | flops 197710208 | bytes 7519764 | solution.py:285
  49.6 3.1 %fusion.379 = f32[64,128,128]{2,1,0:T(8,128)} fusion(f32[64,128,128]{2,1,0:T(8,128)} %get-tuple-element.1638, s32[]{:T(128)S(6)} %select_n.1057, f32[32,128]{1,0:T(8,128)S(1)} %bitcast.764, f32[32,128]{1,0:T(8,128)S(1)} %bitcast.776, f32[32,128]{1,0:T(8,128)S(1)} %bitcast.766, f32[32,128]{1,0:T(8,128)S(1)} %bitcast.778, f32[32,128]{1,0:T(8,128)S(1)} %bitcast.762, ...), kind=kLoop, calls=%fused_computation.61.clone.1 | loop fusion | flops 6291456 | bytes 2195460 | tf_op jit(solution)/shard_map/while/body/dynamic_update_slice | solution.py:282
  53.2 4.3 %fusion.377 = f32[47,32,128]{2,0,1:T(8,128)S(1)} fusion(f32[32,128]{1,0:T(8,128)S(1)} %bitcast.765, f32[32,128]{1,0:T(8,128)S(1)} %bitcast.777, f32[32,128]{1,0:T(8,128)S(1)} %bitcast.767, f32[32,128]{1,0:T(8,128)S(1)} %bitcast.779, f32[32,128]{1,0:T(8,128)S(1)} %bitcast.763, f32[32,128]{1,0:T(8,128)S(1)} %bitcast.775, ...), kind=kOutput, calls=%fused_computation.63.clone.1 | convolution fusion | flops 154333184 | bytes 1638432 | tf_op jit(solution)/shard_map/while/body/rtb,tab->rta/dot_general | solution.py:255
  62.8 2.4 %gather_fusion.17 = f32[1088,3]{1,0:T(8,128)S(1)} fusion(f32[2048,3]{1,0:T(8,128)S(1)} %copy.431, s32[2048]{0:T(1024)S(1)} %copy-done.15), kind=kCustom, calls=%fused_computation.2.clone | custom fusion | bytes 30464 | tf_op jit(solution)/shard_map/jit(_take)/gather | solution.py:124
  68.2 11.7 %all-to-all-start.1 = ((f32[32,3,320]{2,1,0:T(4,128)}), f32[32,3,320]{2,1,0:T(4,128)S(1)}, u32[]{:S(2)}, u32[]{:S(2)}) async-start(f32[32,3,320]{2,1,0:T(4,128)} %broadcast_select_fusion.4), calls=%async_computation.1 | async-start | bytes 393216 | tf_op jit(solution)/shard_map/all_to_all | solution.py:145
  82.0 7.3 %all-to-all-done.1 = f32[32,3,320]{2,1,0:T(4,128)S(1)} async-done(((f32[32,3,320]{2,1,0:T(4,128)}), f32[32,3,320]{2,1,0:T(4,128)S(1)}, u32[]{:S(2)}, u32[]{:S(2)}) %all-to-all-start.1) | async-done | bytes 122912 | tf_op jit(solution)/shard_map/all_to_all | solution.py:145
  89.9 4.4 %while.107 = (s32[]{:T(128)}, f32[7,16,128]{2,1,0:T(8,128)S(1)}, s32[]{:T(128)}, s32[]{:T(128)}, f32[64,128,128]{2,1,0:T(8,128)}, /*index=5*/s32[96]{0:T(128)S(1...) while((s32[]{:T(128)}, f32[7,16,128]{2,1,0:T(8,128)S(1)}, ...), condition=%wide.region_21.27_spmd, body=%wide.region_20.26_spmd.sunk | while | flops 27569352 | bytes 2796316 | solution.py:307
  90.6 3.4 %fusion.390 = f32[7,32,128]{2,0,1:T(8,128)S(1)} fusion(f32[64,128,128]{2,1,0:T(8,128)} %get-tuple-element.1734, s32[]{:T(128)S(6)} %select_n.1062, f32[32,7,128]{2,1,0:T(8,128)S(1)} %gather_fusion.7, pred[32]{0:T(512)(128)(4,1)S(1)} %get-tuple-element.1520), kind=kOutput, calls=%fused_computation.115.clone.1 | convolution fusion | flops 22048768 | bytes 2326564 | tf_op jit(solution)/shard_map/while/body/rtb,tab->rta/dot_general | solution.py:255
  94.7 2.4 %gather_fusion.19 = f32[1088,3]{1,0:T(8,128)S(1)} fusion(f32[2048,3]{1,0:T(8,128)S(1)} %copy.445, s32[2048]{0:T(1024)S(1)} %copy-done.15), kind=kCustom, calls=%fused_computation.13.clone | custom fusion | bytes 30464 | tf_op jit(solution)/shard_map/jit(_take)/gather | solution.py:124
  100.0 2.6 %all-to-all-start.2 = ((f32[32,3,320]{2,1,0:T(4,128)}), f32[32,3,320]{2,1,0:T(4,128)S(1)}, u32[]{:S(2)}, u32[]{:S(2)}) async-start(f32[32,3,320]{2,1,0:T(4,128)} %broadcast_select_fusion.3), calls=%async_computation.2 | async-start | bytes 393216 | tf_op jit(solution)/shard_map/all_to_all | solution.py:145
  102.7 9.2 %all-to-all-done.2 = f32[32,3,320]{2,1,0:T(4,128)S(1)} async-done(((f32[32,3,320]{2,1,0:T(4,128)}), f32[32,3,320]{2,1,0:T(4,128)S(1)}, u32[]{:S(2)}, u32[]{:S(2)}) %all-to-all-start.2) | async-done | bytes 122912 | tf_op jit(solution)/shard_map/all_to_all | solution.py:145
  112.5 4.6 %while.109 = (s32[]{:T(128)}, f32[7,16,128]{2,1,0:T(8,128)S(1)}, s32[]{:T(128)}, s32[]{:T(128)}, f32[64,128,128]{2,1,0:T(8,128)}, /*index=5*/s32[96]{0:T(128)S(1...) while((s32[]{:T(128)}, f32[7,16,128]{2,1,0:T(8,128)S(1)}, ...), condition=%wide.region_27.33_spmd, body=%wide.region_26.32_spmd.sunk | while | flops 27569352 | bytes 2796316 | solution.py:307
  113.2 3.4 %fusion.402 = f32[7,32,128]{2,0,1:T(8,128)S(1)} fusion(f32[64,128,128]{2,1,0:T(8,128)} %get-tuple-element.1809, s32[]{:T(128)S(6)} %select_n.1068, f32[32,7,128]{2,1,0:T(8,128)S(1)} %gather_fusion.9, pred[32]{0:T(512)(128)(4,1)S(1)} %get-tuple-element.1539), kind=kOutput, calls=%fused_computation.151.clone.1 | convolution fusion | flops 22048768 | bytes 2326564 | tf_op jit(solution)/shard_map/while/body/rtb,tab->rta/dot_general | solution.py:255
  117.6 2.4 %gather_fusion.21 = f32[1088,3]{1,0:T(8,128)S(1)} fusion(f32[2048,3]{1,0:T(8,128)S(1)} %copy.459, s32[2048]{0:T(1024)S(1)} %copy-done.15), kind=kCustom, calls=%fused_computation.14.clone | custom fusion | bytes 30464 | tf_op jit(solution)/shard_map/jit(_take)/gather | solution.py:124
  122.9 2.6 %all-to-all-start.3 = ((f32[32,3,320]{2,1,0:T(4,128)}), f32[32,3,320]{2,1,0:T(4,128)S(1)}, u32[]{:S(2)}, u32[]{:S(2)}) async-start(f32[32,3,320]{2,1,0:T(4,128)} %broadcast_select_fusion.2), calls=%async_computation.3 | async-start | bytes 393216 | tf_op jit(solution)/shard_map/all_to_all | solution.py:145
  125.6 9.2 %all-to-all-done.3 = f32[32,3,320]{2,1,0:T(4,128)S(1)} async-done(((f32[32,3,320]{2,1,0:T(4,128)}), f32[32,3,320]{2,1,0:T(4,128)S(1)}, u32[]{:S(2)}, u32[]{:S(2)}) %all-to-all-start.3) | async-done | bytes 122912 | tf_op jit(solution)/shard_map/all_to_all | solution.py:145
  135.4 4.4 %while.111 = (s32[]{:T(128)}, f32[7,16,128]{2,1,0:T(8,128)S(1)}, s32[]{:T(128)}, s32[]{:T(128)}, f32[64,128,128]{2,1,0:T(8,128)}, /*index=5*/s32[96]{0:T(128)S(1...) while((s32[]{:T(128)}, f32[7,16,128]{2,1,0:T(8,128)S(1)}, ...), condition=%wide.region_33.39_spmd, body=%wide.region_32.38_spmd.sunk | while | flops 27569352 | bytes 2796316 | solution.py:307
  136.1 3.4 %fusion.414 = f32[7,32,128]{2,0,1:T(8,128)S(1)} fusion(f32[64,128,128]{2,1,0:T(8,128)} %get-tuple-element.1884, s32[]{:T(128)S(6)} %select_n.1074, f32[32,7,128]{2,1,0:T(8,128)S(1)} %gather_fusion.11, pred[32]{0:T(512)(128)(4,1)S(1)} %get-tuple-element.1558), kind=kOutput, calls=%fused_computation.187.clone.1 | convolution fusion | flops 22048768 | bytes 2326564 | tf_op jit(solution)/shard_map/while/body/rtb,tab->rta/dot_general | solution.py:255
  140.2 2.4 %gather_fusion.23 = f32[1088,3]{1,0:T(8,128)S(1)} fusion(f32[2048,3]{1,0:T(8,128)S(1)} %copy.473, s32[2048]{0:T(1024)S(1)} %copy-done.15), kind=kCustom, calls=%fused_computation.15.clone | custom fusion | bytes 30464 | tf_op jit(solution)/shard_map/jit(_take)/gather | solution.py:124
  145.6 2.6 %all-to-all-start.4 = ((f32[32,3,320]{2,1,0:T(4,128)}), f32[32,3,320]{2,1,0:T(4,128)S(1)}, u32[]{:S(2)}, u32[]{:S(2)}) async-start(f32[32,3,320]{2,1,0:T(4,128)} %broadcast_select_fusion.1), calls=%async_computation.4 | async-start | bytes 393216 | tf_op jit(solution)/shard_map/all_to_all | solution.py:145
  148.3 9.2 %all-to-all-done.4 = f32[32,3,320]{2,1,0:T(4,128)S(1)} async-done(((f32[32,3,320]{2,1,0:T(4,128)}), f32[32,3,320]{2,1,0:T(4,128)S(1)}, u32[]{:S(2)}, u32[]{:S(2)}) %all-to-all-start.4) | async-done | bytes 122912 | tf_op jit(solution)/shard_map/all_to_all | solution.py:145
  158.0 4.4 %while.113 = (s32[]{:T(128)}, f32[7,16,128]{2,1,0:T(8,128)S(1)}, s32[]{:T(128)}, s32[]{:T(128)}, f32[64,128,128]{2,1,0:T(8,128)}, /*index=5*/s32[96]{0:T(128)S(1...) while((s32[]{:T(128)}, f32[7,16,128]{2,1,0:T(8,128)S(1)}, ...), condition=%wide.region_39.45_spmd, body=%wide.region_38.44_spmd.sunk | while | flops 27569352 | bytes 2796316 | solution.py:307
  158.8 3.4 %fusion.426 = f32[7,32,128]{2,0,1:T(8,128)S(1)} fusion(f32[64,128,128]{2,1,0:T(8,128)} %get-tuple-element.1959, s32[]{:T(128)S(6)} %select_n.1080, f32[32,7,128]{2,1,0:T(8,128)S(1)} %gather_fusion.13, pred[32]{0:T(512)(128)(4,1)S(1)} %get-tuple-element.1577), kind=kOutput, calls=%fused_computation.223.clone.1 | convolution fusion | flops 22048768 | bytes 2326564 | tf_op jit(solution)/shard_map/while/body/rtb,tab->rta/dot_general | solution.py:255
  (465 shorter events, 41.6 us)
Async XLA Ops:
  5.0 30.2 %copy-start.12 = (f32[2048]{0:T(1024)}, f32[2048]{0:T(1024)S(1)}, u32[]{:S(2)}) copy-start(f32[2048]{0:T(1024)S(1)} %get-tuple-element.985) | copy-start | bytes 24580
  7.8 2.7 %copy-start = (s32[9]{0:T(128)S(1)}, s32[9]{0:T(128)}, u32[]{:S(2)}) copy-start(s32[9]{0:T(128)} %constant.534.clone) | copy-start | bytes 112
  7.8 4.0 %copy-start.29 = (pred[320]{0:T(512)(128)(4,1)S(1)}, pred[320]{0:T(512)(128)(4,1)}, u32[]{:S(2)}) copy-start(pred[320]{0:T(512)(128)(4,1)} %constant.506.clone.1) | copy-start | bytes 964
  13.7 9.1 %copy-start.2 = (f32[3,2048]{1,0:T(4,128)S(1)}, f32[3,2048]{1,0:T(4,128)}, u32[]{:S(2)}) copy-start(f32[3,2048]{1,0:T(4,128)} %param.49) | copy-start | bytes 73732
  13.8 9.3 %copy-start.1 = (f32[3,2048]{1,0:T(4,128)S(1)}, f32[3,2048]{1,0:T(4,128)}, u32[]{:S(2)}) copy-start(f32[3,2048]{1,0:T(4,128)} %param.46) | copy-start | bytes 73732
  13.8 10.0 %copy-start.33 = (s32[64]{0:T(128)S(1)}, s32[64]{0:T(128)}, u32[]{:S(2)}) copy-start(s32[64]{0:T(128)} %param.55) | copy-start | bytes 772
  13.8 13.6 %copy-start.7 = (f32[2048]{0:T(1024)S(1)}, f32[2048]{0:T(1024)}, u32[]{:S(2)}) copy-start(f32[2048]{0:T(1024)} %param.47) | copy-start | bytes 24580
  13.8 13.7 %copy-start.8 = (f32[2048]{0:T(1024)S(1)}, f32[2048]{0:T(1024)}, u32[]{:S(2)}) copy-start(f32[2048]{0:T(1024)} %param.50) | copy-start | bytes 24580
  15.5 26.8 %all-to-all-start = ((f32[32,14,320]{2,1,0:T(8,128)}), f32[32,14,320]{2,1,0:T(8,128)S(1)}, u32[]{:S(2)}, u32[]{:S(2)}) async-start(f32[32,14,320]{2,1,0:T(8,128)} %concatenate.211), calls=%async_computation | async-start | bytes 1572864 | tf_op jit(solution)/shard_map/all_to_all | solution.py:145
  23.1 8.0 %copy-start.20 = (f32[1,2048]{1,0:T(1,128)}, f32[1,2048]{1,0:T(1,128)S(1)}, u32[]{:S(2)}) copy-start(f32[1,2048]{1,0:T(1,128)S(1)} %get-tuple-element.971) | copy-start | bytes 24580
  23.1 8.0 %copy-start.23 = (f32[1,2048]{1,0:T(1,128)}, f32[1,2048]{1,0:T(1,128)S(1)}, u32[]{:S(2)}) copy-start(f32[1,2048]{1,0:T(1,128)S(1)} %get-tuple-element.972) | copy-start | bytes 24580
  23.1 14.0 %copy-start.18 = (f32[1,2048]{1,0:T(1,128)}, f32[1,2048]{1,0:T(1,128)S(1)}, u32[]{:S(2)}) copy-start(f32[1,2048]{1,0:T(1,128)S(1)} %get-tuple-element.970) | copy-start | bytes 24580
  23.1 8.0 %copy-start.34 = (s32[64]{0:T(128)S(1)}, s32[64]{0:T(128)}, u32[]{:S(2)}) copy-start(s32[64]{0:T(128)} %param.54) | copy-start | bytes 772
  27.8 9.3 %copy-start.3 = (f32[8,2048]{1,0:T(8,128)}, f32[8,2048]{1,0:T(8,128)S(1)}, u32[]{:S(2)}) copy-start(f32[8,2048]{1,0:T(8,128)S(1)} %stack.294) | copy-start | bytes 196612
  27.9 9.2 %copy-start.5 = (f32[8,2048]{1,0:T(8,128)}, f32[8,2048]{1,0:T(8,128)S(1)}, u32[]{:S(2)}) copy-start(f32[8,2048]{1,0:T(8,128)S(1)} %stack.290) | copy-start | bytes 196612
  35.0 2.9 %copy-start.32 = (s32[32]{0:T(128)S(1)}, s32[32]{0:T(128)}, u32[]{:S(2)}) copy-start(s32[32]{0:T(128)} %get-tuple-element.767) | copy-start | bytes 388
  44.0 3.1 %copy-start.11 = (f32[15,2048]{1,0:T(8,128)S(1)}, f32[15,2048]{1,0:T(8,128)}, u32[]{:S(2)}) copy-start(f32[15,2048]{1,0:T(8,128)} %concatenate.226) | copy-start | bytes 368644
  47.2 14.2 %copy-start.4 = (f32[8,2048]{1,0:T(8,128)S(1)}, f32[8,2048]{1,0:T(8,128)}, u32[]{:S(2)}) copy-start(f32[8,2048]{1,0:T(8,128)} %copy-done.3) | copy-start | bytes 196612
  47.2 14.2 %copy-start.6 = (f32[8,2048]{1,0:T(8,128)S(1)}, f32[8,2048]{1,0:T(8,128)}, u32[]{:S(2)}) copy-start(f32[8,2048]{1,0:T(8,128)} %copy-done.5) | copy-start | bytes 196612
  47.2 14.2 %copy-start.19 = (f32[1,2048]{1,0:T(1,128)S(1)}, f32[1,2048]{1,0:T(1,128)}, u32[]{:S(2)}) copy-start(f32[1,2048]{1,0:T(1,128)} %copy-done.18) | copy-start | bytes 24580
  47.2 14.2 %copy-start.22 = (f32[1,2048]{1,0:T(1,128)S(1)}, f32[1,2048]{1,0:T(1,128)}, u32[]{:S(2)}) copy-start(f32[1,2048]{1,0:T(1,128)} %copy-done.20) | copy-start | bytes 24580
  47.2 14.2 %copy-start.25 = (f32[1,2048]{1,0:T(1,128)S(1)}, f32[1,2048]{1,0:T(1,128)}, u32[]{:S(2)}) copy-start(f32[1,2048]{1,0:T(1,128)} %copy-done.23) | copy-start | bytes 24580
  58.6 3.1 %copy-start.26 = (f32[3,2048]{1,0:T(4,128)S(1)}, f32[3,2048]{1,0:T(4,128)}, u32[]{:S(2)}) copy-start(f32[3,2048]{1,0:T(4,128)} %param.48) | copy-start | bytes 73732
  58.6 4.1 %copy-start.15 = (s32[2048]{0:T(1024)S(1)}, s32[2048]{0:T(1024)}, u32[]{:S(2)}) copy-start(s32[2048]{0:T(1024)} %copy-done.14) | copy-start | bytes 24580
  62.8 2.6 %copy-start.30 = (pred[320]{0:T(512)(128)(4,1)S(1)}, pred[320]{0:T(512)(128)(4,1)}, u32[]{:S(2)}) copy-start(pred[320]{0:T(512)(128)(4,1)} %constant.506.clone.1) | copy-start | bytes 964
  65.5 14.4 %copy-start.13 = (f32[2048]{0:T(1024)S(1)}, f32[2048]{0:T(1024)}, u32[]{:S(2)}) copy-start(f32[2048]{0:T(1024)} %copy-done.12) | copy-start | bytes 24580
  65.6 14.4 %copy-start.17 = (f32[2048]{0:T(1024)S(1)}, f32[2048]{0:T(1024)}, u32[]{:S(2)}) copy-start(f32[2048]{0:T(1024)} %param.51) | copy-start | bytes 24580
  68.2 21.1 %all-to-all-start.1 = ((f32[32,3,320]{2,1,0:T(4,128)}), f32[32,3,320]{2,1,0:T(4,128)S(1)}, u32[]{:S(2)}, u32[]{:S(2)}) async-start(f32[32,3,320]{2,1,0:T(4,128)} %broadcast_select_fusion.4), calls=%async_computation.1 | async-start | bytes 393216 | tf_op jit(solution)/shard_map/all_to_all | solution.py:145
  80.0 9.6 %copy-start.10 = (f32[13,1088]{1,0:T(8,128)S(1)}, f32[13,1088]{1,0:T(8,128)}, u32[]{:S(2)}) copy-start(f32[13,1088]{1,0:T(8,128)} %copy-done.9) | copy-start | bytes 169732
  100.0 11.9 %all-to-all-start.2 = ((f32[32,3,320]{2,1,0:T(4,128)}), f32[32,3,320]{2,1,0:T(4,128)S(1)}, u32[]{:S(2)}, u32[]{:S(2)}) async-start(f32[32,3,320]{2,1,0:T(4,128)} %broadcast_select_fusion.3), calls=%async_computation.2 | async-start | bytes 393216 | tf_op jit(solution)/shard_map/all_to_all | solution.py:145
  122.9 11.9 %all-to-all-start.3 = ((f32[32,3,320]{2,1,0:T(4,128)}), f32[32,3,320]{2,1,0:T(4,128)S(1)}, u32[]{:S(2)}, u32[]{:S(2)}) async-start(f32[32,3,320]{2,1,0:T(4,128)} %broadcast_select_fusion.2), calls=%async_computation.3 | async-start | bytes 393216 | tf_op jit(solution)/shard_map/all_to_all | solution.py:145
  145.6 11.9 %all-to-all-start.4 = ((f32[32,3,320]{2,1,0:T(4,128)}), f32[32,3,320]{2,1,0:T(4,128)S(1)}, u32[]{:S(2)}, u32[]{:S(2)}) async-start(f32[32,3,320]{2,1,0:T(4,128)} %broadcast_select_fusion.1), calls=%async_computation.4 | async-start | bytes 393216 | tf_op jit(solution)/shard_map/all_to_all | solution.py:145
  (8 other events, 14.1 us)
